TPU v7x, 256 devices: a whole 4x4x8 slice. The times are simulated.
256 devices in a mesh: row: 32 (over x, y, core), col: 8 (over z).
Axes of the slice: x: 4, y: 4, z: 8, core: 2. Of those that a mesh axis runs over, the one named last changes fastest.
Arguments:
- features: bfloat16 [8192, 1024], P('row', 'col'), may hold values from -6 to 6
- grad_out: bfloat16 [8192, 1024], P('row', 'col'), may hold values from -6 to 6
- weight: bfloat16 [1024, 1024], replicated, may hold values from -0.1875 to 0.1875
- root_weight: bfloat16 [1024, 1024], replicated, may hold values from -0.1875 to 0.1875
- values: bfloat16 [32, 8, 8, 128, 128], P('row', 'col'), may hold values from -0.125 to 0.125
- positions: int32 [32, 8, 8], P('row', 'col'), may hold values from 0 to 15, as said below
- counts: int32 [32, 8], P('row', 'col'), may hold values from 1 to 8, as said below
Outputs:
- activations: bfloat16 [8192, 1024], P('row', 'col')
- feature_grad: float32 [8192, 1024], P('row', 'col')
- weight_grad: float32 [1024, 1024], P('col')
- root_grad: float32 [1024, 1024], P('col')
Inputs may be any that keep to these rules, and one draw needn't show every extreme that they name: Within the first counts slots of a tile the positions are distinct; position p is block row p // 8 and block column p % 8 of the tile. `counts`: some tile uses all 8 slots in every draw; about a quarter of the block rows have much fuller tiles (4 or 8 used slots) than the rest (1 or 2).
All inputs are finite; a program needn't handle non-finite values.
Results may differ from a plain program's by a relative error of at most 0.012.
Values may be sent and summed in bfloat16 or wider, within the bound.
No kernel may reach another device: no remote copies, remote signals or barrier semaphores. Data moves between devices by JAX's collectives and lax.ppermute only.
A program may use at most 64 MiB of HBM per device.

v0:
```python
import math

import jax
import jax.numpy as jnp
from jax import lax
from jax.sharding import PartitionSpec as P


def silu_grad(preact):
    sig = jax.nn.sigmoid(preact)
    return sig * (1.0 + preact * (1.0 - sig))


def forward_slots(slot_vals, slot_pos, live_mask, x_tile, row_blocks, col_blocks):
    picker = (
        slot_pos[:, None] % col_blocks == jnp.arange(col_blocks, dtype=jnp.int32)[None, :]
    ).astype(jnp.bfloat16)
    chosen = jnp.einsum("sq,qjf->sjf", picker, x_tile, preferred_element_type=jnp.float32).astype(
        jnp.bfloat16
    )
    products = jnp.einsum("sij,sjf->sif", slot_vals, chosen, preferred_element_type=jnp.float32)
    placer = (
        (slot_pos[:, None] // col_blocks == jnp.arange(row_blocks, dtype=jnp.int32)[None, :])
        & live_mask[:, None]
    ).astype(jnp.float32)
    return jnp.einsum("sr,sif->rif", placer, products)


def backward_slots(slot_vals, slot_pos, live_mask, g_tile, row_blocks, col_blocks):
    picker = (
        slot_pos[:, None] // col_blocks == jnp.arange(row_blocks, dtype=jnp.int32)[None, :]
    ).astype(jnp.bfloat16)
    chosen = jnp.einsum("sr,rjf->sjf", picker, g_tile, preferred_element_type=jnp.float32).astype(
        jnp.bfloat16
    )
    products = jnp.einsum("sji,sjf->sif", slot_vals, chosen, preferred_element_type=jnp.float32)
    placer = (
        (slot_pos[:, None] % col_blocks == jnp.arange(col_blocks, dtype=jnp.int32)[None, :])
        & live_mask[:, None]
    ).astype(jnp.float32)
    return jnp.einsum("sq,sif->qif", placer, products)


def run_tile(slot_fn, slot_vals, slot_pos, used, operand):
    slot_total = slot_vals.shape[0]
    slot_index = jnp.arange(slot_total, dtype=jnp.int32)
    return slot_fn(slot_vals, slot_pos, slot_index < used, operand)


def per_device(features, grad_out, weight, root_weight, values, positions, counts):
    node_rows, feat_dev = features.shape
    block_edge = values.shape[-1]
    row_blocks = node_rows // block_edge
    col_count = lax.axis_size("col")
    col_index = lax.axis_index("col")
    everything = lax.all_gather(features, "row", axis=0, tiled=True)
    nodes = everything.shape[0]
    col_blocks = nodes // col_count // block_edge
    feat_blocks = everything.reshape(col_count, col_blocks, block_edge, feat_dev)

    def forward_fn(slot_vals, slot_pos, live_mask, x_tile):
        return forward_slots(slot_vals, slot_pos, live_mask, x_tile, row_blocks, col_blocks)

    def backward_fn(slot_vals, slot_pos, live_mask, g_tile):
        return backward_slots(slot_vals, slot_pos, live_mask, g_tile, row_blocks, col_blocks)

    forward_zero = jnp.zeros((row_blocks, block_edge, feat_dev), jnp.float32)
    all_vals, all_pos, all_counts = (
        lax.all_gather(values, "col", axis=1, tiled=True),
        lax.all_gather(positions, "col", axis=1, tiled=True),
        lax.all_gather(counts, "col", axis=1, tiled=True),
    )
    running = forward_zero
    for which in range(all_vals.shape[1]):
        x_tile = lax.dynamic_index_in_dim(feat_blocks, 0 + which, 0, keepdims=False)
        running = running + run_tile(
            forward_fn, all_vals[0, which], all_pos[0, which], all_counts[0, which], x_tile
        )
    summed_rows = running
    aggregated = summed_rows.reshape(node_rows, feat_dev).astype(jnp.bfloat16)
    w_rows = lax.dynamic_slice_in_dim(weight, col_index * feat_dev, feat_dev, 0)
    r_rows = lax.dynamic_slice_in_dim(root_weight, col_index * feat_dev, feat_dev, 0)
    partial_value = jnp.dot(aggregated, w_rows, preferred_element_type=jnp.float32) + jnp.dot(
        features, r_rows, preferred_element_type=jnp.float32
    )
    preact = lax.psum_scatter(partial_value, "col", scatter_dimension=1, tiled=True)
    activations = jax.nn.silu(preact).astype(jnp.bfloat16)
    preact_grad = (grad_out.astype(jnp.float32) * silu_grad(preact)).astype(jnp.bfloat16)
    whole_grad = lax.all_gather(preact_grad, "col", axis=1, tiled=True)
    contract_rows = (((0,), (0,)), ((), ()))
    weight_part = lax.dot_general(
        aggregated, whole_grad, contract_rows, preferred_element_type=jnp.float32
    )
    root_part = lax.dot_general(
        features, whole_grad, contract_rows, preferred_element_type=jnp.float32
    )
    weight_sum, root_sum = lax.psum((weight_part, root_part), "row")
    grad_scale = 1.0 / math.sqrt(nodes)
    contract_cols = (((1,), (1,)), ((), ()))
    aggregated_grad = lax.dot_general(
        whole_grad, w_rows, contract_cols, preferred_element_type=jnp.float32
    ).astype(jnp.bfloat16)
    own_grad = lax.dot_general(
        whole_grad, r_rows, contract_cols, preferred_element_type=jnp.float32
    )
    g_tile = aggregated_grad.reshape(row_blocks, block_edge, feat_dev)
    backward_zero = jnp.zeros((col_count, col_blocks, block_edge, feat_dev), jnp.float32)
    running = backward_zero
    for which in range(all_vals.shape[1]):
        added = run_tile(
            backward_fn, all_vals[0, which], all_pos[0, which], all_counts[0, which], g_tile
        )
        slot_here = 0 + which
        current = lax.dynamic_index_in_dim(running, slot_here, 0, keepdims=False)
        running = lax.dynamic_update_index_in_dim(running, current + added, slot_here, 0)
    column_terms = running
    column_terms = column_terms.reshape(nodes, feat_dev)
    summed_cols = lax.psum_scatter(
        column_terms.astype(jnp.bfloat16), "row", scatter_dimension=0, tiled=True
    ).astype(jnp.float32)
    feature_grad = summed_cols + own_grad
    return (activations, feature_grad, weight_sum * grad_scale, root_sum * grad_scale)


def solution(mesh):
    in_specs = (
        P("row", "col"),
        P("row", "col"),
        P(),
        P(),
        P("row", "col", None, None, None),
        P("row", "col", None),
        P("row", "col"),
    )
    out_specs = (P("row", "col"), P("row", "col"), P("col", None), P("col", None))
    return jax.shard_map(
        per_device, mesh=mesh, in_specs=in_specs, out_specs=out_specs, check_vma=False
    )
```

profile of v0, /device:TPU:1, one launch (start us, length us, event | category | flops | bytes accessed | tf_op | source)
XLA Modules:
  0.0 463.1 jit_solution(10715064648895597442)
XLA Ops:
  11.3 14.1 %all-reduce.1 = s32[8]{0:T(128)S(1)} all-reduce(s32[8]{0:T(128)S(1)} %bitcast_dynamic-update-slice_fusion), channel_id=1, replica_groups=mesh['row'=32,'col'=8] {'col'}, use_global_device_ids=true, to_apply=%add.1 | all-reduce | flops 8 | bytes 64
  25.4 11.3 %all_gather.15 = s32[1,8,8]{2,0,1:T(1,128)S(1)} all-gather(s32[1,1,8]{2,0,1:T(1,128)} %bitcast.358), channel_id=1, replica_groups=mesh['row'=32,'col'=8] {'col'}, dimensions={1}, use_global_device_ids=true | all-gather | bytes 288 | tf_op jit(solution)/shard_map/all_gather | solution.py:70
  42.6 20.7 %all-gather.3.cloned.1.call-done = bf16[8192,128]{1,0:T(8,128)(2,1)} async-done(((bf16[256,128]{1,0:T(8,128)(2,1)}), bf16[8192,128]{1,0:T(8,128)(2,1)}) %all-gather.3.cloned.1.call-update) | async-done | bytes 2097168 | tf_op jit(solution)/shard_map/all_gather | solution.py:56
  63.3 2.4 fusion.169
  66.8 34.1 %all-gather.5.cloned.1.call-done = bf16[1,8,8,128,128]{4,3,2,0,1:T(8,128)(2,1)} async-done(((bf16[1,1,8,128,128]{4,3,2,0,1:T(8,128)(2,1)}), bf16[1,8,8,128,128]{4,3,2,0,1:T(8,128)(2,1)}) %all-gather.5.cloned.1.call-update) | async-done | bytes 2097168 | tf_op jit(solution)/shard_map/all_gather | solution.py:69
  100.8 2.1 convolution_bitcast_fusion.19
  106.0 2.0 convolution_bitcast_fusion.18
  111.0 2.0 convolution_bitcast_fusion.17
  130.4 2.2 fusion
  132.7 36.8 %reduce-scatter.3.cloned.1.call-done = f32[256,128]{1,0:T(8,128)} async-done(((f32[256,1024]{1,0:T(8,128)}), f32[256,128]{1,0:T(8,128)}) %reduce-scatter.3.cloned.1.call-update) | async-done | bytes 131088 | tf_op jit(solution)/shard_map/reduce_scatter | solution.py:86
  171.1 18.6 %all_gather.19 = bf16[256,1024]{1,0:T(8,128)(2,1)S(1)} all-gather(bf16[256,128]{1,0:T(8,128)(2,1)S(1)} %get-tuple-element.30), channel_id=1, replica_groups=mesh['row'=32,'col'=8] {'col'}, dimensions={1}, use_global_device_ids=true | all-gather | bytes 589824 | tf_op jit(solution)/shard_map/all_gather | solution.py:89
  202.0 2.0 convolution_bitcast_fusion.10
  207.0 2.0 copy-done.1
  209.0 1.9 convolution_bitcast_fusion.9
  212.8 2.0 fusion.13
  215.9 1.9 convolution_bitcast_fusion.8
  219.6 2.0 fusion.11
  222.7 1.9 convolution_bitcast_fusion.7
  224.7 1.8 copy.137
  226.5 2.0 fusion.9
  229.6 2.0 convolution_bitcast_fusion.6
  231.6 1.8 copy.140
  233.4 2.0 fusion.7
  236.5 1.9 convolution_bitcast_fusion.5
  240.3 2.0 fusion.5
  245.8 2.5 convert_element_type.129
  248.4 1.9 copy.147
  250.3 115.9 %all-reduce.5.cloned.1.call-done = (f32[128,1024]{1,0:T(8,128)}, f32[128,1024]{1,0:T(8,128)}) async-done(((f32[128,1024]{1,0:T(8,128)}, f32[128,1024]{1,0:T(8,128)}), (f32[128,1024]{1,0:T(8,128)}, f32[128,1024]{1,0:T(8,128)})) %all-reduce.5.cloned.1.call-update) | async-done | bytes 1048592 | tf_op jit(solution)/shard_map/psum | solution.py:97
  366.2 1.9 broadcast_multiply_fusion.1
  368.1 1.9 broadcast_multiply_fusion
  370.0 84.6 %reduce-scatter.5.cloned.1.call-done = bf16[256,128]{1,0:T(8,128)(2,1)} async-done(((bf16[8192,128]{1,0:T(8,128)(2,1)}), bf16[256,128]{1,0:T(8,128)(2,1)}) %reduce-scatter.5.cloned.1.call-update) | async-done | bytes 65552 | tf_op jit(solution)/shard_map/reduce_scatter | solution.py:118
  454.6 1.9 convolution_add_fusion.6
  (121 shorter events, 63.8 us)
Async XLA Ops:
  7.2 122.9 %copy-start = (bf16[1024,1024]{1,0:T(8,128)(2,1)S(1)}, bf16[1024,1024]{1,0:T(8,128)(2,1)}, u32[]{:S(2)}) copy-start(bf16[1024,1024]{1,0:T(8,128)(2,1)} %param.9) | copy-start | bytes 6291460
  7.2 56.2 %all-gather.3.cloned.1.call-start = ((), (), s32[]{:S(2)}) async-start(), calls=%async_computation.2 | async-start | bytes 2162688 | tf_op jit(solution)/shard_map/all_gather | solution.py:56
  7.9 92.9 %all-gather.5.cloned.1.call-start = ((), (), s32[]{:S(2)}) async-start(), calls=%async_computation.3 | async-start | bytes 2359296 | tf_op jit(solution)/shard_map/all_gather | solution.py:69
  8.7 160.8 %reduce-scatter.3.cloned.1.call-start = ((), (), s32[]{:S(2)}) async-start(), calls=%async_computation.4 | async-start | bytes 1179648 | tf_op jit(solution)/shard_map/reduce_scatter | solution.py:86
  121.3 5.9 %copy-start.7 = (bf16[8,128,128]{2,0,1:T(8,128)(2,1)S(1)}, bf16[8,128,128]{2,0,1:T(8,128)(2,1)}, u32[]{:S(2)}) copy-start(bf16[8,128,128]{2,0,1:T(8,128)(2,1)} %copy.85) | copy-start | bytes 786436
  122.2 5.2 %copy-start.8 = (bf16[8,128,128]{2,0,1:T(8,128)(2,1)S(1)}, bf16[8,128,128]{2,0,1:T(8,128)(2,1)}, u32[]{:S(2)}) copy-start(bf16[8,128,128]{2,0,1:T(8,128)(2,1)} %copy.90) | copy-start | bytes 786436
  122.5 5.2 %copy-start.9 = (bf16[8,128,128]{2,0,1:T(8,128)(2,1)S(1)}, bf16[8,128,128]{2,0,1:T(8,128)(2,1)}, u32[]{:S(2)}) copy-start(bf16[8,128,128]{2,0,1:T(8,128)(2,1)} %copy.95) | copy-start | bytes 786436
  124.8 3.2 copy-start.10
  127.3 2.1 copy-start.11
  127.3 2.3 copy-start.12
  127.3 2.5 copy-start.15
  127.9 2.4 copy-start.14
  130.0 39.5 %copy-start.16 = (bf16[256,128]{1,0:T(8,128)(2,1)S(1)}, bf16[256,128]{1,0:T(8,128)(2,1)}, u32[]{:S(2)}) copy-start(bf16[256,128]{1,0:T(8,128)(2,1)} %param.8) | copy-start | bytes 196612
  132.6 233.6 %all-reduce.5.cloned.1.call-start = ((), (), s32[]{:S(2)}) async-start(), calls=%async_computation.6 | async-start | bytes 2097152 | tf_op jit(solution)/shard_map/psum | solution.py:97
  205.8 0.9 copy-start.13
  205.8 3.2 copy-start.6
  207.0 2.0 copy-start.1
  212.7 3.1 copy-start.5
  219.6 3.1 copy-start.4
  226.5 3.1 copy-start.3
  233.4 3.1 copy-start.2
  242.3 212.4 %reduce-scatter.5.cloned.1.call-start = ((), (), s32[]{:S(2)}) async-start(), calls=%async_computation.5 | async-start | bytes 2162688 | tf_op jit(solution)/shard_map/reduce_scatter | solution.py:118
Sparse Core Ops, SparseCore 0:
  10.5 52.7 all-gather.2
  65.1 35.6 all-gather.4
  132.7 36.7 reduce-scatter.2
  242.4 123.8 all-reduce.4
  369.9 84.6 reduce-scatter.4
where the time goes:
time: 465 us; the launch traced here: 463 us
  waiting for transfers between devices  294 us (63%)
  matrix products  60 us (13%)
  blocking collectives  44 us (9%)
  local copies, waits for them, and re-layouts  37.4 us (8%)
  between operations  14.9 us (3%)
  other arithmetic  13.1 us (3%)
    psum x1, waiting for transfers between devices, per_device(): weight_sum, root_sum = lax.psum((weight_part, root_part), 'row')  116 us
    reduce_scatter x1, waiting for transfers between devices, per_device(): lax.psum_scatter(column_terms.astype(jnp.bfloat16), 'row', scatter_dimens...  84.6 us
    reduce_scatter x1, waiting for transfers between devices, per_device(): lax.psum_scatter(partial_value, 'col', scatter_dimension=1, tiled=True)  36.8 us
    all_gather x1, waiting for transfers between devices, per_device(): lax.all_gather(values, 'col', axis=1, tiled=True)  34.1 us
    all_gather x1, waiting for transfers between devices, per_device(): everything = lax.all_gather(features, 'row', axis=0, tiled=True)  20.7 us
    all_gather x1, blocking collectives, per_device(): whole_grad = lax.all_gather(preact_grad, 'col', axis=1, tiled=True)  18.6 us
    dot_general x8, matrix products, backward_slots(): jnp.einsum('sji,sjf->sif', slot_vals, chosen, preferred_element_type=jnp....  14.2 us
    unnamed x1, blocking collectives  14.1 us
  transfers between devices with their start and end apart: 5, of which 5 were waited for; matrix products, arithmetic and copies ran while one was open for 5% of the time, Pallas kernels for 0%

commit v1 on v0

v1 whole, which is shorter than its diff:
```python
import math

import jax
import jax.numpy as jnp
from jax import lax
from jax.sharding import PartitionSpec as P


def silu_grad(preact):
    sig = jax.nn.sigmoid(preact)
    return sig * (1.0 + preact * (1.0 - sig))


def gather_rows(block, axis_name, parts):
    spread = jnp.broadcast_to(block[None], (parts,) + block.shape)
    got = lax.all_to_all(spread, axis_name, 0, 0, tiled=True)
    return got.reshape((parts * block.shape[0],) + block.shape[1:])


def reduce_rows(block, axis_name, parts):
    pieces = block.reshape((parts, block.shape[0] // parts) + block.shape[1:])
    got = lax.all_to_all(pieces, axis_name, 0, 0, tiled=True)
    return got.astype(jnp.float32).sum(0)


def per_device(features, grad_out, weight, root_weight, values, positions, counts):
    node_rows, feat_dev = features.shape
    slots, block_edge = values.shape[2], values.shape[-1]
    row_blocks = node_rows // block_edge
    col_count = lax.axis_size("col")
    row_count = lax.axis_size("row")
    col_index = lax.axis_index("col")

    live = (jnp.arange(slots, dtype=jnp.int32) < counts[0, 0]).astype(values.dtype)
    own_vals = (values[0, 0] * live[:, None, None]).reshape(slots * block_edge, block_edge)
    pos_row = jnp.zeros((16, block_edge), values.dtype)
    pos_row = lax.dynamic_update_slice(
        pos_row, positions[0, 0].astype(values.dtype).reshape(1, slots), (0, 0)
    )
    packed = jnp.concatenate([own_vals, pos_row], axis=0)
    all_packed = lax.all_gather(packed, "col", axis=0, tiled=True).reshape(
        col_count, slots * block_edge + 16, block_edge
    )
    tile_vals = all_packed[:, : slots * block_edge].reshape(
        col_count, slots, block_edge, block_edge
    )
    tile_pos = all_packed[:, slots * block_edge, :slots].astype(jnp.int32)
    cb = row_count * node_rows // col_count // block_edge
    n_pos = row_blocks * cb
    onehot = (tile_pos[:, :, None] == jnp.arange(n_pos, dtype=jnp.int32)[None, None, :]).astype(
        values.dtype
    )
    dense = jnp.einsum(
        "tsp,tsij->tpij", onehot, tile_vals, preferred_element_type=jnp.float32
    ).astype(values.dtype)
    dense = dense.reshape(col_count, row_blocks, cb, block_edge, block_edge)

    x_all = gather_rows(features, "row", row_count)
    x_tiles = x_all.reshape(col_count, cb, block_edge, feat_dev)
    agg_f32 = jnp.einsum("trcij,tcjf->rif", dense, x_tiles, preferred_element_type=jnp.float32)
    aggregated = agg_f32.reshape(node_rows, feat_dev).astype(jnp.bfloat16)

    agg_full = lax.all_gather(aggregated, "col", axis=1, tiled=True)
    feat_full = lax.all_gather(features, "col", axis=1, tiled=True)
    grad_full = lax.all_gather(grad_out, "col", axis=1, tiled=True)
    preact = jnp.dot(agg_full, weight, preferred_element_type=jnp.float32) + jnp.dot(
        feat_full, root_weight, preferred_element_type=jnp.float32
    )
    preact_own = lax.dynamic_slice_in_dim(preact, col_index * feat_dev, feat_dev, 1)
    activations = jax.nn.silu(preact_own).astype(jnp.bfloat16)
    preact_grad = (grad_full.astype(jnp.float32) * silu_grad(preact)).astype(jnp.bfloat16)

    contract_rows = (((0,), (0,)), ((), ()))
    weight_part = lax.dot_general(
        aggregated, preact_grad, contract_rows, preferred_element_type=jnp.float32
    )
    root_part = lax.dot_general(
        features, preact_grad, contract_rows, preferred_element_type=jnp.float32
    )
    both = jnp.concatenate([weight_part, root_part], axis=0)
    both_sum = reduce_rows(both, "row", row_count)
    both_all = gather_rows(both_sum, "row", row_count)
    nodes = row_count * node_rows
    grad_scale = 1.0 / math.sqrt(nodes)
    weight_sum = both_all[:feat_dev]
    root_sum = both_all[feat_dev:]

    w_rows = lax.dynamic_slice_in_dim(weight, col_index * feat_dev, feat_dev, 0)
    r_rows = lax.dynamic_slice_in_dim(root_weight, col_index * feat_dev, feat_dev, 0)
    contract_cols = (((1,), (1,)), ((), ()))
    aggregated_grad = lax.dot_general(
        preact_grad, w_rows, contract_cols, preferred_element_type=jnp.float32
    ).astype(jnp.bfloat16)
    own_grad = lax.dot_general(
        preact_grad, r_rows, contract_cols, preferred_element_type=jnp.float32
    )
    g_rows = aggregated_grad.reshape(row_blocks, block_edge, feat_dev)
    column_terms = jnp.einsum(
        "trcij,rif->tcjf", dense, g_rows, preferred_element_type=jnp.float32
    ).reshape(nodes, feat_dev)
    summed_cols = reduce_rows(column_terms.astype(jnp.bfloat16), "row", row_count)
    feature_grad = summed_cols + own_grad
    return (activations, feature_grad, weight_sum * grad_scale, root_sum * grad_scale)


def solution(mesh):
    in_specs = (
        P("row", "col"),
        P("row", "col"),
        P(),
        P(),
        P("row", "col", None, None, None),
        P("row", "col", None),
        P("row", "col"),
    )
    out_specs = (P("row", "col"), P("row", "col"), P("col", None), P("col", None))
    return jax.shard_map(
        per_device, mesh=mesh, in_specs=in_specs, out_specs=out_specs, check_vma=False
    )
```

time: 465 us -> 212 us (0.46)
  waiting for transfers between devices: 294 us -> 44.1 us
  matrix products: 60 us -> 16.4 us
  starting transfers between devices: 0.2 us -> 37.7 us
  blocking collectives: 44 us -> 69.6 us
  local copies, waits for them, and re-layouts: 37.4 us -> 17.2 us
    reduce_scatter x2 -> x0, waiting for transfers between devices: 121 us -> none  [the longest x1 84.6 us: per_device(): lax.psum_scatter(column_terms.astype(jnp.bfloat16), 'row', scatter_dimens...]
    psum x1 -> x0, waiting for transfers between devices: 116 us -> none  [per_device(): weight_sum, root_sum = lax.psum((weight_part, root_part), 'row')]
    all_gather x2 -> x1, waiting for transfers between devices: 54.8 us -> 0.01 us  [per_device(): lax.all_gather(packed, 'col', axis=0, tiled=True)]
    all_to_all x0 -> x4, waiting for transfers between devices: none -> 44 us  [the longest x2 31.4 us: reduce_rows(): got = lax.all_to_all(pieces, axis_name, 0, 0, tiled=True)]
    dot_general x54 -> x9, matrix products: 60 us -> 16.4 us  [the longest x1 4.75 us: per_device(): jnp.einsum('trcij,rif->tcjf', dense, g_rows, preferred_element_type=jnp.f...]
    all_gather x2 -> x3, blocking collectives: 29.9 us -> 69.6 us  [the longest x1 29 us: per_device(): feat_full = lax.all_gather(features, 'col', axis=1, tiled=True)]
    all_to_all x0 -> x4, starting transfers between devices: none -> 37.7 us  [the longest x2 23.9 us: reduce_rows(): got = lax.all_to_all(pieces, axis_name, 0, 0, tiled=True)]
    unnamed x1 -> x0, blocking collectives: 14.1 us -> none
  transfers between devices with their start and end apart: 5 -> 5, of which waited for: 5 -> 3; matrix products, arithmetic and copies ran while one was open for 5% -> 13% of each run, Pallas kernels for 0% -> 0%
where the time goes in v1:
time: 212 us; the launch traced here: 211 us
  blocking collectives  69.6 us (33%)
  waiting for transfers between devices  44.1 us (21%)
  starting transfers between devices  37.7 us (18%)
  local copies, waits for them, and re-layouts  17.2 us (8%)
  matrix products  16.4 us (8%)
  between operations  15 us (7%)
  other arithmetic  11.4 us (5%)
    all_to_all x2, waiting for transfers between devices, reduce_rows(): got = lax.all_to_all(pieces, axis_name, 0, 0, tiled=True)  31.4 us
    all_gather x1, blocking collectives, per_device(): feat_full = lax.all_gather(features, 'col', axis=1, tiled=True)  29 us
    all_to_all x2, starting transfers between devices, reduce_rows(): got = lax.all_to_all(pieces, axis_name, 0, 0, tiled=True)  23.9 us
    all_gather x1, blocking collectives, per_device(): grad_full = lax.all_gather(grad_out, 'col', axis=1, tiled=True)  22.2 us
    all_gather x1, blocking collectives, per_device(): agg_full = lax.all_gather(aggregated, 'col', axis=1, tiled=True)  18.4 us
    all_to_all x2, starting transfers between devices, gather_rows(): got = lax.all_to_all(spread, axis_name, 0, 0, tiled=True)  13.8 us
    all_to_all x2, waiting for transfers between devices, gather_rows(): got = lax.all_to_all(spread, axis_name, 0, 0, tiled=True)  12.6 us
    dot_general x1, local copies, waits for them, and re-layouts, per_device(): jnp.einsum('trcij,rif->tcjf', dense, g_rows, preferred_element_type=jnp.f...  6.6 us
  transfers between devices with their start and end apart: 5, of which 3 were waited for; matrix products, arithmetic and copies ran while one was open for 13% of the time, Pallas kernels for 0%

profile of v1, /device:TPU:1, one launch (start us, length us, event | category | flops | bytes accessed | tf_op | source)
XLA Modules:
  0.0 211.4 jit_solution(5465625973222556562)
XLA Ops:
  8.1 0.7 convert_bitcast_fusion
  8.8 1.1 bitcast_multiply_fusion
  9.9 0.7 fusion.13
  10.7 2.6 %broadcast_in_dim.4 = bf16[32,256,128]{2,1,0:T(8,128)(2,1)} broadcast(bf16[256,128]{1,0:T(8,128)(2,1)} %param.7), dimensions={1,2} | broadcast | bytes 2162688 | tf_op jit(solution)/shard_map/broadcast_in_dim | solution.py:15
  13.3 8.8 %all-to-all-start = ((bf16[32,256,128]{2,1,0:T(8,128)(2,1)}), bf16[32,256,128]{2,1,0:T(8,128)(2,1)}, u32[]{:S(2)}, u32[]{:S(2)}) async-start(bf16[32,256,128]{2,1,0:T(8,128)(2,1)} %broadcast_in_dim.4), calls=%async_computation | async-start | bytes 4194304 | tf_op jit(solution)/shard_map/all_to_all | solution.py:16
  22.1 29.0 %all_gather.14 = bf16[256,1024]{1,0:T(8,128)(2,1)S(1)} all-gather(bf16[256,128]{1,0:T(8,128)(2,1)S(1)} %copy-done.3), channel_id=1, replica_groups=mesh['row'=32,'col'=8] {'col'}, dimensions={1}, use_global_device_ids=true | all-gather | bytes 589824 | tf_op jit(solution)/shard_map/all_gather | solution.py:64
  51.1 22.2 %all_gather.15 = bf16[256,1024]{1,0:T(8,128)(2,1)} all-gather(bf16[256,128]{1,0:T(8,128)(2,1)S(1)} %copy-done.5), channel_id=1, replica_groups=mesh['row'=32,'col'=8] {'col'}, dimensions={1}, use_global_device_ids=true | all-gather | bytes 589824 | tf_op jit(solution)/shard_map/all_gather | solution.py:65
  73.3 1.7 slice.19
  75.1 0.7 slice_convert_fusion
  75.8 1.9 convolution_convert_fusion
  77.7 1.9 copy-done.1
  79.6 3.1 %copy.14 = bf16[2,128,8,128,8]{3,1,0,4,2:T(8,128)(2,1)} copy(bf16[2,128,8,128,8]{3,2,0,1,4:T(8,128)(2,1)S(1)} %bitcast.57) | data formatting | bytes 8388608 | tf_op jit(solution)/shard_map/trcij,tcjf->rif/dot_general | solution.py:60
  82.7 4.2 %fusion.7 = bf16[256,128]{1,0:T(8,128)(2,1)S(1)} fusion(bf16[256,8,128,8]{2,0,3,1:T(8,128)(2,1)} %bitcast.62, bf16[8,8,128,128]{3,2,1,0:T(8,128)(2,1)} %bitcast.12), kind=kOutput, calls=%fused_computation.12 | convolution fusion | flops 536903680 | bytes 6356992 | tf_op jit(solution)/shard_map/trcij,tcjf->rif/dot_general | solution.py:60
  87.0 18.4 %all_gather.13 = bf16[256,1024]{1,0:T(8,128)(2,1)S(1)} all-gather(bf16[256,128]{1,0:T(8,128)(2,1)S(1)} %fusion.7), channel_id=1, replica_groups=mesh['row'=32,'col'=8] {'col'}, dimensions={1}, use_global_device_ids=true | all-gather | bytes 589824 | tf_op jit(solution)/shard_map/all_gather | solution.py:63
  105.3 0.7 fusion.21
  106.1 2.1 multiply_convert_fusion
  108.7 1.1 maximum_bitcast_fusion
  109.8 19.3 %all-to-all-start.2 = ((f32[32,8,1024]{2,1,0:T(8,128)}), f32[32,8,1024]{2,1,0:T(8,128)}, u32[]{:S(2)}, u32[]{:S(2)}) async-start(f32[32,8,1024]{2,1,0:T(8,128)} %maximum_bitcast_fusion), calls=%async_computation.2 | async-start | bytes 2097152 | tf_op jit(solution)/shard_map/all_to_all | solution.py:22
  129.1 6.6 %copy.16 = bf16[8,8,128,128,2]{3,2,1,0,4:T(8,128)(2,1)} copy(bf16[8,8,128,128,2]{2,1,4,3,0:T(8,128)(2,1)} %bitcast.58) | data formatting | bytes 8388608 | tf_op jit(solution)/shard_map/trcij,rif->tcjf/dot_general | solution.py:98
  135.7 1.2 convolution_convert_fusion.1
  136.9 4.7 %fusion = bf16[8192,128]{1,0:T(8,128)(2,1)} fusion(bf16[8192,128,2]{1,0,2:T(8,128)(2,1)} %bitcast.59, bf16[2,128,128]{2,1,0:T(8,128)(2,1)S(1)} %bitcast.65), kind=kOutput, calls=%fused_computation.1 | convolution fusion | flops 537919488 | bytes 6356992 | tf_op jit(solution)/shard_map/trcij,rif->tcjf/dot_general | solution.py:98
  141.7 4.3 %all-to-all-done.2 = f32[32,8,1024]{2,1,0:T(8,128)} async-done(((f32[32,8,1024]{2,1,0:T(8,128)}), f32[32,8,1024]{2,1,0:T(8,128)}, u32[]{:S(2)}, u32[]{:S(2)}) %all-to-all-start.2) | async-done | bytes 1048608 | tf_op jit(solution)/shard_map/all_to_all | solution.py:22
  146.0 4.6 %all-to-all-start.1 = ((bf16[32,256,128]{2,1,0:T(8,128)(2,1)}), bf16[32,256,128]{2,1,0:T(8,128)(2,1)}, u32[]{:S(2)}, u32[]{:S(2)}) async-start(bf16[32,256,128]{2,1,0:T(8,128)(2,1)} %bitcast.60), calls=%async_computation.1 | async-start | bytes 4194304 | tf_op jit(solution)/shard_map/all_to_all | solution.py:22
  150.6 1.3 reduce_sum.19
  151.9 27.1 %all-to-all-done.1 = bf16[32,256,128]{2,1,0:T(8,128)(2,1)} async-done(((bf16[32,256,128]{2,1,0:T(8,128)(2,1)}), bf16[32,256,128]{2,1,0:T(8,128)(2,1)}, u32[]{:S(2)}, u32[]{:S(2)}) %all-to-all-start.1) | async-done | bytes 2097184 | tf_op jit(solution)/shard_map/all_to_all | solution.py:22
  179.0 1.1 broadcast_in_dim.5
  180.1 5.1 %all-to-all-start.3 = ((f32[32,8,1024]{2,1,0:T(8,128)}), f32[32,8,1024]{2,1,0:T(8,128)}, u32[]{:S(2)}, u32[]{:S(2)}) async-start(f32[32,8,1024]{2,1,0:T(8,128)} %broadcast_in_dim.5), calls=%async_computation.3 | async-start | bytes 2097152 | tf_op jit(solution)/shard_map/all_to_all | solution.py:16
  185.2 1.6 multiply_convert_fusion.1
  186.8 1.9 convert_reduce_fusion
  188.7 1.0 convolution_add_fusion.1
  189.6 12.6 %all-to-all-done.3 = f32[32,8,1024]{2,1,0:T(8,128)} async-done(((f32[32,8,1024]{2,1,0:T(8,128)}), f32[32,8,1024]{2,1,0:T(8,128)}, u32[]{:S(2)}, u32[]{:S(2)}) %all-to-all-start.3) | async-done | bytes 1048608 | tf_op jit(solution)/shard_map/all_to_all | solution.py:16
  202.2 2.3 %fusion.11 = (f32[128,1024]{1,0:T(8,128)}, f32[128,1024]{1,0:T(8,128)}) fusion(f32[32,8,1024]{2,1,0:T(8,128)} %all-to-all-done.3), kind=kLoop, calls=%fused_computation.18 | loop fusion | flops 262144 | bytes 2097152 | tf_op jit(solution)/shard_map/mul | solution.py:103
  (19 shorter events, 0.7 us)
Async XLA Ops:
  7.2 98.9 %copy-start = (bf16[1024,1024]{1,0:T(8,128)(2,1)S(1)}, bf16[1024,1024]{1,0:T(8,128)(2,1)}, u32[]{:S(2)}) copy-start(bf16[1024,1024]{1,0:T(8,128)(2,1)} %param.10) | copy-start | bytes 6291460
  7.2 66.2 %all-gather.2.cloned.1.call-start = ((), (), s32[]{:S(2)}) async-start(), calls=%async_computation.4 | async-start | bytes 2396160 | tf_op jit(solution)/shard_map/all_gather | solution.py:41
  13.3 8.8 %copy-start.3 = (bf16[256,128]{1,0:T(8,128)(2,1)S(1)}, bf16[256,128]{1,0:T(8,128)(2,1)}, u32[]{:S(2)}) copy-start(bf16[256,128]{1,0:T(8,128)(2,1)} %param.7) | copy-start | bytes 196612
  13.3 37.8 %copy-start.5 = (bf16[256,128]{1,0:T(8,128)(2,1)S(1)}, bf16[256,128]{1,0:T(8,128)(2,1)}, u32[]{:S(2)}) copy-start(bf16[256,128]{1,0:T(8,128)(2,1)} %param.8) | copy-start | bytes 196612
  13.3 69.4 %all-to-all-start = ((bf16[32,256,128]{2,1,0:T(8,128)(2,1)}), bf16[32,256,128]{2,1,0:T(8,128)(2,1)}, u32[]{:S(2)}, u32[]{:S(2)}) async-start(bf16[32,256,128]{2,1,0:T(8,128)(2,1)} %broadcast_in_dim.4), calls=%async_computation | async-start | bytes 4194304 | tf_op jit(solution)/shard_map/all_to_all | solution.py:16
  77.7 1.9 copy-start.1
  82.7 22.6 %copy-start.2 = (bf16[1024,1024]{1,0:T(8,128)(2,1)S(1)}, bf16[1024,1024]{1,0:T(8,128)(2,1)}, u32[]{:S(2)}) copy-start(bf16[1024,1024]{1,0:T(8,128)(2,1)} %param.9) | copy-start | bytes 6291460
  87.0 19.1 %copy-start.4 = (bf16[256,1024]{1,0:T(8,128)(2,1)S(1)}, bf16[256,1024]{1,0:T(8,128)(2,1)}, u32[]{:S(2)}) copy-start(bf16[256,1024]{1,0:T(8,128)(2,1)} %all_gather.15) | copy-start | bytes 1572868
  109.8 36.3 %all-to-all-start.2 = ((f32[32,8,1024]{2,1,0:T(8,128)}), f32[32,8,1024]{2,1,0:T(8,128)}, u32[]{:S(2)}, u32[]{:S(2)}) async-start(f32[32,8,1024]{2,1,0:T(8,128)} %maximum_bitcast_fusion), calls=%async_computation.2 | async-start | bytes 2097152 | tf_op jit(solution)/shard_map/all_to_all | solution.py:22
  146.0 32.9 %all-to-all-start.1 = ((bf16[32,256,128]{2,1,0:T(8,128)(2,1)}), bf16[32,256,128]{2,1,0:T(8,128)(2,1)}, u32[]{:S(2)}, u32[]{:S(2)}) async-start(bf16[32,256,128]{2,1,0:T(8,128)(2,1)} %bitcast.60), calls=%async_computation.1 | async-start | bytes 4194304 | tf_op jit(solution)/shard_map/all_to_all | solution.py:22
  180.1 22.1 %all-to-all-start.3 = ((f32[32,8,1024]{2,1,0:T(8,128)}), f32[32,8,1024]{2,1,0:T(8,128)}, u32[]{:S(2)}, u32[]{:S(2)}) async-start(f32[32,8,1024]{2,1,0:T(8,128)} %broadcast_in_dim.5), calls=%async_computation.3 | async-start | bytes 2097152 | tf_op jit(solution)/shard_map/all_to_all | solution.py:16
Sparse Core Ops, SparseCore 0:
  10.8 51.6 all-gather.1

commit v2 on v1

--- a/solution.py
+++ b/solution.py
@@ -60,9 +60,13 @@
     agg_f32 = jnp.einsum("trcij,tcjf->rif", dense, x_tiles, preferred_element_type=jnp.float32)
     aggregated = agg_f32.reshape(node_rows, feat_dev).astype(jnp.bfloat16)
 
-    agg_full = lax.all_gather(aggregated, "col", axis=1, tiled=True)
-    feat_full = lax.all_gather(features, "col", axis=1, tiled=True)
-    grad_full = lax.all_gather(grad_out, "col", axis=1, tiled=True)
+    agg_parts = gather_rows(aggregated, "col", col_count).reshape(col_count, node_rows, feat_dev)
+    agg_full = jnp.moveaxis(agg_parts, 0, 1).reshape(node_rows, col_count * feat_dev)
+    own_pair = jnp.concatenate([features, grad_out], axis=0)
+    pair_parts = gather_rows(own_pair, "col", col_count).reshape(col_count, 2, node_rows, feat_dev)
+    pair_full = jnp.moveaxis(pair_parts, 0, 2).reshape(2, node_rows, col_count * feat_dev)
+    feat_full = pair_full[0]
+    grad_full = pair_full[1]
     preact = jnp.dot(agg_full, weight, preferred_element_type=jnp.float32) + jnp.dot(
         feat_full, root_weight, preferred_element_type=jnp.float32
     )
@@ -79,7 +83,7 @@
     )
     both = jnp.concatenate([weight_part, root_part], axis=0)
     both_sum = reduce_rows(both, "row", row_count)
-    both_all = gather_rows(both_sum, "row", row_count)
+    both_all = lax.all_gather(both_sum, "row", axis=0, tiled=True)
     nodes = row_count * node_rows
     grad_scale = 1.0 / math.sqrt(nodes)
     weight_sum = both_all[:feat_dev]

time: 212 us -> 206 us (0.972)
  waiting for transfers between devices: 44.1 us -> 114 us
  blocking collectives: 69.6 us -> 0 us
  starting transfers between devices: 37.7 us -> 30.5 us
    all_gather x3 -> x0, blocking collectives: 69.6 us -> none  [the longest x1 29 us: per_device(): feat_full = lax.all_gather(features, 'col', axis=1, tiled=True)]
    all_to_all x2 -> x3, waiting for transfers between devices: 12.6 us -> 64.4 us  [gather_rows(): got = lax.all_to_all(spread, axis_name, 0, 0, tiled=True)]
    all_gather x0 -> x1, waiting for transfers between devices: none -> 19.6 us  [per_device(): both_all = lax.all_gather(both_sum, 'row', axis=0, tiled=True)]
    all_to_all x2, starting transfers between devices: 23.9 us -> 9.29 us  [reduce_rows(): got = lax.all_to_all(pieces, axis_name, 0, 0, tiled=True)]
    all_to_all x2 -> x3, starting transfers between devices: 13.8 us -> 21.1 us  [gather_rows(): got = lax.all_to_all(spread, axis_name, 0, 0, tiled=True)]
    broadcast_in_dim x2 -> x3, local copies, waits for them, and re-layouts: 3.76 us -> 4.62 us  [gather_rows(): spread = jnp.broadcast_to(block[None], (parts,) + block.shape)]
  transfers between devices with their start and end apart: 5 -> 7, of which waited for: 3 -> 6; matrix products, arithmetic and copies ran while one was open for 13% -> 16% of each run, Pallas kernels for 0% -> 0%
where the time goes in v2:
time: 206 us; the launch traced here: 205 us
  waiting for transfers between devices  114 us (55%)
  starting transfers between devices  30.5 us (15%)
  matrix products  16.9 us (8%)
  local copies, waits for them, and re-layouts  15.9 us (8%)
  between operations  15 us (7%)
  other arithmetic  13.1 us (6%)
    all_to_all x3, waiting for transfers between devices, gather_rows(): got = lax.all_to_all(spread, axis_name, 0, 0, tiled=True)  64.4 us
    all_to_all x2, waiting for transfers between devices, reduce_rows(): got = lax.all_to_all(pieces, axis_name, 0, 0, tiled=True)  29.6 us
    all_to_all x3, starting transfers between devices, gather_rows(): got = lax.all_to_all(spread, axis_name, 0, 0, tiled=True)  21.1 us
    all_gather x1, waiting for transfers between devices, per_device(): both_all = lax.all_gather(both_sum, 'row', axis=0, tiled=True)  19.6 us
    all_to_all x2, starting transfers between devices, reduce_rows(): got = lax.all_to_all(pieces, axis_name, 0, 0, tiled=True)  9.29 us
    dot_general x1, local copies, waits for them, and re-layouts, per_device(): jnp.einsum('trcij,rif->tcjf', dense, g_rows, preferred_element_type=jnp.f...  6.62 us
    dot_general x1, matrix products, per_device(): jnp.einsum('trcij,rif->tcjf', dense, g_rows, preferred_element_type=jnp.f...  4.78 us
    broadcast_in_dim x3, local copies, waits for them, and re-layouts, gather_rows(): spread = jnp.broadcast_to(block[None], (parts,) + block.shape)  4.62 us
  transfers between devices with their start and end apart: 7, of which 6 were waited for; matrix products, arithmetic and copies ran while one was open for 16% of the time, Pallas kernels for 0%

profile of v2, /device:TPU:1, one launch (start us, length us, event | category | flops | bytes accessed | tf_op | source)
XLA Modules:
  0.0 205.0 jit_solution(4761917431993116758)
XLA Ops:
  8.8 1.1 bitcast_multiply_fusion.1
  10.7 2.7 %broadcast_in_dim.6 = bf16[32,256,128]{2,1,0:T(8,128)(2,1)} broadcast(bf16[256,128]{1,0:T(8,128)(2,1)} %param.7), dimensions={1,2} | broadcast | bytes 2162688 | tf_op jit(solution)/shard_map/broadcast_in_dim | solution.py:15
  13.3 8.8 %all-to-all-start = ((bf16[32,256,128]{2,1,0:T(8,128)(2,1)}), bf16[32,256,128]{2,1,0:T(8,128)(2,1)}, u32[]{:S(2)}, u32[]{:S(2)}) async-start(bf16[32,256,128]{2,1,0:T(8,128)(2,1)} %broadcast_in_dim.6), calls=%async_computation | async-start | bytes 4194304 | tf_op jit(solution)/shard_map/all_to_all | solution.py:16
  22.1 28.4 %all-to-all-done = bf16[32,256,128]{2,1,0:T(8,128)(2,1)} async-done(((bf16[32,256,128]{2,1,0:T(8,128)(2,1)}), bf16[32,256,128]{2,1,0:T(8,128)(2,1)}, u32[]{:S(2)}, u32[]{:S(2)}) %all-to-all-start) | async-done | bytes 2097184 | tf_op jit(solution)/shard_map/all_to_all | solution.py:16
  50.5 1.1 broadcast_in_dim.8
  51.6 8.2 %all-to-all-start.2 = ((bf16[8,512,128]{2,1,0:T(8,128)(2,1)}), bf16[8,512,128]{2,1,0:T(8,128)(2,1)S(1)}, u32[]{:S(2)}, u32[]{:S(2)}) async-start(bf16[8,512,128]{2,1,0:T(8,128)(2,1)} %broadcast_in_dim.8), calls=%async_computation.2 | async-start | bytes 2097152 | tf_op jit(solution)/shard_map/all_to_all | solution.py:16
  59.8 1.7 slice.27
  62.3 1.9 convolution_convert_fusion
  64.2 1.1 copy.19
  65.3 0.9 copy-done.1
  66.2 2.8 %fusion.7 = bf16[256,128]{1,0:T(8,128)(2,1)S(1)} fusion(bf16[256,8,128,8]{2,0,3,1:T(8,128)(2,1)S(1)} %bitcast.77, bf16[8,8,128,128]{3,2,1,0:T(8,128)(2,1)} %bitcast.12), kind=kOutput, calls=%fused_computation.12 | convolution fusion | flops 536903680 | bytes 6356992 | tf_op jit(solution)/shard_map/trcij,tcjf->rif/dot_general | solution.py:60
  69.2 19.8 %all-to-all-done.2 = bf16[8,512,128]{2,1,0:T(8,128)(2,1)S(1)} async-done(((bf16[8,512,128]{2,1,0:T(8,128)(2,1)}), bf16[8,512,128]{2,1,0:T(8,128)(2,1)S(1)}, u32[]{:S(2)}, u32[]{:S(2)}) %all-to-all-start.2) | async-done | bytes 1048608 | tf_op jit(solution)/shard_map/all_to_all | solution.py:16
  89.0 0.8 broadcast_in_dim.7
  89.8 4.2 %all-to-all-start.1 = ((bf16[8,256,128]{1,2,0:T(8,128)(2,1)}), bf16[8,256,128]{1,2,0:T(8,128)(2,1)}, u32[]{:S(2)}, u32[]{:S(2)}) async-start(bf16[8,256,128]{1,2,0:T(8,128)(2,1)} %broadcast_in_dim.7), calls=%async_computation.1 | async-start | bytes 1048576 | tf_op jit(solution)/shard_map/all_to_all | solution.py:16
  94.7 1.1 slice_convert_fusion
  95.8 16.2 %all-to-all-done.1 = bf16[8,256,128]{1,2,0:T(8,128)(2,1)} async-done(((bf16[8,256,128]{1,2,0:T(8,128)(2,1)}), bf16[8,256,128]{1,2,0:T(8,128)(2,1)}, u32[]{:S(2)}, u32[]{:S(2)}) %all-to-all-start.1) | async-done | bytes 524320 | tf_op jit(solution)/shard_map/all_to_all | solution.py:16
  112.0 2.6 %fusion.22 = f32[256,1024]{1,0:T(8,128)S(1)} fusion(bf16[256,1024]{0,1:T(8,128)(2,1)} %bitcast.16, bf16[1024,1024]{1,0:T(8,128)(2,1)} %param.9), kind=kOutput, calls=%fused_computation.39 | convolution fusion | flops 536870912 | bytes 3670016 | tf_op jit(solution)/shard_map/dot_general | solution.py:70
  114.6 2.1 %fusion.10 = (bf16[256,1024]{1,0:T(8,128)(2,1)S(1)}, f32[256,1024]{1,0:T(8,128)}) fusion(f32[32,8,8,128]{3,2,1,0:T(8,128)S(1)} %bitcast.82, f32[256,1024]{1,0:T(8,128)S(1)} %fusion.22, bf16[1024,1024]{1,0:T(8,128)(2,1)S(1)} %copy-done, bf16[32,8,8,128]{3,2,1,0:T(8,128)(2,1)S(1)} %bitcast.83), kind=kOutput, calls=%fused_computation.14 | convolution fusion | flops 539492352 | bytes 6291456 | tf_op jit(solution)/shard_map/dot_general | solution.py:70
  117.2 1.1 maximum_bitcast_fusion
  118.2 4.7 %all-to-all-start.4 = ((f32[32,8,1024]{2,1,0:T(8,128)}), f32[32,8,1024]{2,1,0:T(8,128)}, u32[]{:S(2)}, u32[]{:S(2)}) async-start(f32[32,8,1024]{2,1,0:T(8,128)} %maximum_bitcast_fusion), calls=%async_computation.4 | async-start | bytes 2097152 | tf_op jit(solution)/shard_map/all_to_all | solution.py:22
  123.0 6.6 %copy.23 = bf16[8,8,128,128,2]{3,2,1,0,4:T(8,128)(2,1)} copy(bf16[8,8,128,128,2]{2,1,4,3,0:T(8,128)(2,1)} %bitcast.73) | data formatting | bytes 8388608 | tf_op jit(solution)/shard_map/trcij,rif->tcjf/dot_general | solution.py:102
  129.6 1.2 convolution_convert_fusion.1
  130.9 4.8 %fusion = bf16[8192,128]{1,0:T(8,128)(2,1)} fusion(bf16[8192,128,2]{1,0,2:T(8,128)(2,1)} %bitcast.74, bf16[2,128,128]{2,1,0:T(8,128)(2,1)S(1)} %bitcast.84), kind=kOutput, calls=%fused_computation.1 | convolution fusion | flops 537919488 | bytes 6356992 | tf_op jit(solution)/shard_map/trcij,rif->tcjf/dot_general | solution.py:102
  135.7 4.4 %all-to-all-done.4 = f32[32,8,1024]{2,1,0:T(8,128)} async-done(((f32[32,8,1024]{2,1,0:T(8,128)}), f32[32,8,1024]{2,1,0:T(8,128)}, u32[]{:S(2)}, u32[]{:S(2)}) %all-to-all-start.4) | async-done | bytes 1048608 | tf_op jit(solution)/shard_map/all_to_all | solution.py:22
  140.0 4.5 %all-to-all-start.3 = ((bf16[32,256,128]{2,1,0:T(8,128)(2,1)}), bf16[32,256,128]{2,1,0:T(8,128)(2,1)}, u32[]{:S(2)}, u32[]{:S(2)}) async-start(bf16[32,256,128]{2,1,0:T(8,128)(2,1)} %bitcast.75), calls=%async_computation.3 | async-start | bytes 4194304 | tf_op jit(solution)/shard_map/all_to_all | solution.py:22
  144.7 1.9 reduce_sum.19
  146.6 1.6 multiply_convert_fusion
  148.2 25.2 %all-to-all-done.3 = bf16[32,256,128]{2,1,0:T(8,128)(2,1)} async-done(((bf16[32,256,128]{2,1,0:T(8,128)(2,1)}), bf16[32,256,128]{2,1,0:T(8,128)(2,1)}, u32[]{:S(2)}, u32[]{:S(2)}) %all-to-all-start.3) | async-done | bytes 2097184 | tf_op jit(solution)/shard_map/all_to_all | solution.py:22
  173.4 1.9 convert_reduce_fusion
  175.2 1.0 convolution_add_fusion.1
  176.2 19.6 %all-gather.5.cloned.1.call-done = f32[256,1024]{1,0:T(8,128)} async-done(((f32[8,1024]{1,0:T(8,128)}), f32[256,1024]{1,0:T(8,128)}) %all-gather.5.cloned.1.call-update) | async-done | bytes 1048592 | tf_op jit(solution)/shard_map/all_gather | solution.py:86
  195.8 2.3 %slice_multiply_fusion = (f32[128,1024]{1,0:T(8,128)}, f32[128,1024]{1,0:T(8,128)}) fusion(f32[256,1024]{1,0:T(8,128)} %all-gather.5.cloned.1.call-done), kind=kLoop, calls=%fused_computation.21 | loop fusion | flops 262144 | bytes 2097152 | tf_op jit(solution)/shard_map/mul | solution.py:107
  (24 shorter events, 3.6 us)
Async XLA Ops:
  7.2 107.4 %copy-start = (bf16[1024,1024]{1,0:T(8,128)(2,1)S(1)}, bf16[1024,1024]{1,0:T(8,128)(2,1)}, u32[]{:S(2)}) copy-start(bf16[1024,1024]{1,0:T(8,128)(2,1)} %param.10) | copy-start | bytes 6291460
  7.2 52.6 %all-gather.3.cloned.1.call-start = ((), (), s32[]{:S(2)}) async-start(), calls=%async_computation.5 | async-start | bytes 2396160 | tf_op jit(solution)/shard_map/all_gather | solution.py:41
  13.3 8.8 %copy-start.3 = (bf16[256,128]{1,0:T(8,128)(2,1)S(1)}, bf16[256,128]{1,0:T(8,128)(2,1)}, u32[]{:S(2)}) copy-start(bf16[256,128]{1,0:T(8,128)(2,1)} %param.7) | copy-start | bytes 196612
  13.3 8.8 %copy-start.4 = (bf16[256,128]{1,0:T(8,128)(2,1)S(1)}, bf16[256,128]{1,0:T(8,128)(2,1)}, u32[]{:S(2)}) copy-start(bf16[256,128]{1,0:T(8,128)(2,1)} %param.8) | copy-start | bytes 196612
  13.3 37.2 %all-to-all-start = ((bf16[32,256,128]{2,1,0:T(8,128)(2,1)}), bf16[32,256,128]{2,1,0:T(8,128)(2,1)}, u32[]{:S(2)}, u32[]{:S(2)}) async-start(bf16[32,256,128]{2,1,0:T(8,128)(2,1)} %broadcast_in_dim.6), calls=%async_computation | async-start | bytes 4194304 | tf_op jit(solution)/shard_map/all_to_all | solution.py:16
  51.6 37.4 %all-to-all-start.2 = ((bf16[8,512,128]{2,1,0:T(8,128)(2,1)}), bf16[8,512,128]{2,1,0:T(8,128)(2,1)S(1)}, u32[]{:S(2)}, u32[]{:S(2)}) async-start(bf16[8,512,128]{2,1,0:T(8,128)(2,1)} %broadcast_in_dim.8), calls=%async_computation.2 | async-start | bytes 2097152 | tf_op jit(solution)/shard_map/all_to_all | solution.py:16
  64.2 2.0 copy-start.1
  89.8 22.1 %all-to-all-start.1 = ((bf16[8,256,128]{1,2,0:T(8,128)(2,1)}), bf16[8,256,128]{1,2,0:T(8,128)(2,1)}, u32[]{:S(2)}, u32[]{:S(2)}) async-start(bf16[8,256,128]{1,2,0:T(8,128)(2,1)} %broadcast_in_dim.7), calls=%async_computation.1 | async-start | bytes 1048576 | tf_op jit(solution)/shard_map/all_to_all | solution.py:16
  112.0 2.6 %copy-start.2 = (f32[1,256,8,128]{3,2,1,0:T(8,128)S(1)}, f32[1,256,8,128]{3,2,1,0:T(8,128)}, u32[]{:S(2)}) copy-start(f32[1,256,8,128]{3,2,1,0:T(8,128)} %get-tuple-element.6) | copy-start | bytes 3145732
  118.2 21.8 %all-to-all-start.4 = ((f32[32,8,1024]{2,1,0:T(8,128)}), f32[32,8,1024]{2,1,0:T(8,128)}, u32[]{:S(2)}, u32[]{:S(2)}) async-start(f32[32,8,1024]{2,1,0:T(8,128)} %maximum_bitcast_fusion), calls=%async_computation.4 | async-start | bytes 2097152 | tf_op jit(solution)/shard_map/all_to_all | solution.py:22
  140.0 33.3 %all-to-all-start.3 = ((bf16[32,256,128]{2,1,0:T(8,128)(2,1)}), bf16[32,256,128]{2,1,0:T(8,128)(2,1)}, u32[]{:S(2)}, u32[]{:S(2)}) async-start(bf16[32,256,128]{2,1,0:T(8,128)(2,1)} %bitcast.75), calls=%async_computation.3 | async-start | bytes 4194304 | tf_op jit(solution)/shard_map/all_to_all | solution.py:22
  144.6 51.2 %all-gather.5.cloned.1.call-start = ((), (), s32[]{:S(2)}) async-start(), calls=%async_computation.6 | async-start | bytes 1081344 | tf_op jit(solution)/shard_map/all_gather | solution.py:86
Sparse Core Ops, SparseCore 0:
  10.8 40.7 all-gather.2
  148.5 47.2 all-gather.4

commit v3 on v2

--- a/solution.py
+++ b/solution.py
@@ -63,7 +63,9 @@
     agg_parts = gather_rows(aggregated, "col", col_count).reshape(col_count, node_rows, feat_dev)
     agg_full = jnp.moveaxis(agg_parts, 0, 1).reshape(node_rows, col_count * feat_dev)
     own_pair = jnp.concatenate([features, grad_out], axis=0)
-    pair_parts = gather_rows(own_pair, "col", col_count).reshape(col_count, 2, node_rows, feat_dev)
+    pair_parts = lax.all_gather(own_pair, "col", axis=0, tiled=True).reshape(
+        col_count, 2, node_rows, feat_dev
+    )
     pair_full = jnp.moveaxis(pair_parts, 0, 2).reshape(2, node_rows, col_count * feat_dev)
     feat_full = pair_full[0]
     grad_full = pair_full[1]
@@ -83,11 +85,14 @@
     )
     both = jnp.concatenate([weight_part, root_part], axis=0)
     both_sum = reduce_rows(both, "row", row_count)
-    both_all = lax.all_gather(both_sum, "row", axis=0, tiled=True)
+    sum_high = both_sum.astype(jnp.bfloat16)
+    sum_low = (both_sum - sum_high.astype(jnp.float32)).astype(jnp.bfloat16)
+    sum_lanes = both_sum.size // block_edge
+    sum_pair = jnp.concatenate(
+        [sum_high.reshape(sum_lanes, block_edge), sum_low.reshape(sum_lanes, block_edge)], axis=0
+    )
     nodes = row_count * node_rows
     grad_scale = 1.0 / math.sqrt(nodes)
-    weight_sum = both_all[:feat_dev]
-    root_sum = both_all[feat_dev:]
 
     w_rows = lax.dynamic_slice_in_dim(weight, col_index * feat_dev, feat_dev, 0)
     r_rows = lax.dynamic_slice_in_dim(root_weight, col_index * feat_dev, feat_dev, 0)
@@ -102,7 +107,17 @@
     column_terms = jnp.einsum(
         "trcij,rif->tcjf", dense, g_rows, preferred_element_type=jnp.float32
     ).reshape(nodes, feat_dev)
-    summed_cols = reduce_rows(column_terms.astype(jnp.bfloat16), "row", row_count)
+    term_pieces = column_terms.astype(jnp.bfloat16).reshape(row_count, node_rows, feat_dev)
+    outgoing = jnp.concatenate(
+        [term_pieces, jnp.broadcast_to(sum_pair[None], (row_count,) + sum_pair.shape)], axis=1
+    )
+    incoming = lax.all_to_all(outgoing, "row", 0, 0, tiled=True)
+    summed_cols = incoming[:, :node_rows].astype(jnp.float32).sum(0)
+    got_high = incoming[:, node_rows : node_rows + sum_lanes].astype(jnp.float32)
+    got_low = incoming[:, node_rows + sum_lanes :].astype(jnp.float32)
+    both_all = (got_high + got_low).reshape(both.shape)
+    weight_sum = both_all[:feat_dev]
+    root_sum = both_all[feat_dev:]
     feature_grad = summed_cols + own_grad
     return (activations, feature_grad, weight_sum * grad_scale, root_sum * grad_scale)
 

time: 206 us -> 196 us (0.951)
  waiting for transfers between devices: 114 us -> 96.1 us
  local copies, waits for them, and re-layouts: 15.9 us -> 21 us
  other arithmetic: 13.1 us -> 15.9 us
    all_to_all x3 -> x2, waiting for transfers between devices: 64.4 us -> 0.01 us  [gather_rows(): got = lax.all_to_all(spread, axis_name, 0, 0, tiled=True)]
    all_to_all x0 -> x1, waiting for transfers between devices: none -> 38.2 us  [per_device(): incoming = lax.all_to_all(outgoing, 'row', 0, 0, tiled=True)]
    all_gather x1, waiting for transfers between devices: 0.01 us -> 28.7 us  [per_device(): lax.all_gather(packed, 'col', axis=0, tiled=True)]
    all_to_all x2 -> x1, waiting for transfers between devices: 29.6 us -> 4.26 us  [reduce_rows(): got = lax.all_to_all(pieces, axis_name, 0, 0, tiled=True)]
    all_to_all x3 -> x2, starting transfers between devices: 21.1 us -> 12.9 us  [gather_rows(): got = lax.all_to_all(spread, axis_name, 0, 0, tiled=True)]
    all_gather x1, waiting for transfers between devices: 19.6 us -> 24.9 us  [per_device(): lax.all_gather(own_pair, 'col', axis=0, tiled=True)]
    all_to_all x0 -> x1, starting transfers between devices: none -> 4.6 us  [per_device(): incoming = lax.all_to_all(outgoing, 'row', 0, 0, tiled=True)]
    concatenate x0 -> x2, other arithmetic: none -> 3.55 us  [the longest x1 3.54 us: per_device(): jnp.concatenate([term_pieces, jnp.broadcast_to(sum_pair[None], (row_count...]
  transfers between devices with their start and end apart: 7 -> 6, of which waited for: 6 -> 4; matrix products, arithmetic and copies ran while one was open for 16% -> 17% of each run, Pallas kernels for 0% -> 0%
where the time goes in v3:
time: 196 us; the launch traced here: 195 us
  waiting for transfers between devices  96.1 us (49%)
  starting transfers between devices  29.2 us (15%)
  local copies, waits for them, and re-layouts  21 us (11%)
  matrix products  18 us (9%)
  other arithmetic  15.9 us (8%)
  between operations  15 us (8%)
    all_to_all x1, waiting for transfers between devices, per_device(): incoming = lax.all_to_all(outgoing, 'row', 0, 0, tiled=True)  38.2 us
    all_gather x1, waiting for transfers between devices, per_device(): lax.all_gather(packed, 'col', axis=0, tiled=True)  28.7 us
    all_gather x1, waiting for transfers between devices, per_device(): lax.all_gather(own_pair, 'col', axis=0, tiled=True)  24.9 us
    all_to_all x2, starting transfers between devices, gather_rows(): got = lax.all_to_all(spread, axis_name, 0, 0, tiled=True)  12.9 us
    all_to_all x1, starting transfers between devices, reduce_rows(): got = lax.all_to_all(pieces, axis_name, 0, 0, tiled=True)  11.6 us
    dot_general x1, local copies, waits for them, and re-layouts, per_device(): jnp.einsum('trcij,rif->tcjf', dense, g_rows, preferred_element_type=jnp.f...  6.61 us
    dot_general x1, matrix products, per_device(): jnp.einsum('trcij,rif->tcjf', dense, g_rows, preferred_element_type=jnp.f...  4.82 us
    all_to_all x1, starting transfers between devices, per_device(): incoming = lax.all_to_all(outgoing, 'row', 0, 0, tiled=True)  4.6 us
  transfers between devices with their start and end apart: 6, of which 4 were waited for; matrix products, arithmetic and copies ran while one was open for 17% of the time, Pallas kernels for 0%

profile of v3, /device:TPU:1, one launch (start us, length us, event | category | flops | bytes accessed | tf_op | source)
XLA Modules:
  0.0 195.2 jit_solution(14429576040830148164)
XLA Ops:
  8.8 1.1 bitcast_multiply_fusion.1
  10.7 2.6 %broadcast_in_dim.6 = bf16[32,256,128]{2,1,0:T(8,128)(2,1)} broadcast(bf16[256,128]{1,0:T(8,128)(2,1)} %param.7), dimensions={1,2} | broadcast | bytes 2162688 | tf_op jit(solution)/shard_map/broadcast_in_dim | solution.py:15
  13.3 8.8 %all-to-all-start = ((bf16[32,256,128]{2,1,0:T(8,128)(2,1)}), bf16[32,256,128]{2,1,0:T(8,128)(2,1)}, u32[]{:S(2)}, u32[]{:S(2)}) async-start(bf16[32,256,128]{2,1,0:T(8,128)(2,1)} %broadcast_in_dim.6), calls=%async_computation | async-start | bytes 4194304 | tf_op jit(solution)/shard_map/all_to_all | solution.py:16
  22.8 28.7 %all-gather.3.cloned.1.call-done = bf16[8320,128]{1,0:T(8,128)(2,1)} async-done(((bf16[1040,128]{1,0:T(8,128)(2,1)}), bf16[8320,128]{1,0:T(8,128)(2,1)}) %all-gather.3.cloned.1.call-update) | async-done | bytes 2129936 | tf_op jit(solution)/shard_map/all_gather | solution.py:41
  51.6 1.7 slice.41
  54.0 1.9 convolution_convert_fusion
  55.9 2.0 %copy-done.1 = bf16[8,16,128,128]{3,1,2,0:T(8,128)(2,1)} copy-done((bf16[8,16,128,128]{3,1,2,0:T(8,128)(2,1)}, bf16[8,16,128,128]{3,1,2,0:T(8,128)(2,1)S(1)}, u32[]{:S(2)}) %copy-start.1) | copy-done | bytes 4194328
  57.8 3.1 %copy.15 = bf16[2,128,8,128,8]{3,1,0,4,2:T(8,128)(2,1)} copy(bf16[2,128,8,128,8]{3,2,0,1,4:T(8,128)(2,1)S(1)} %bitcast.72) | data formatting | bytes 8388608 | tf_op jit(solution)/shard_map/trcij,tcjf->rif/dot_general | solution.py:60
  60.9 4.1 %fusion.7 = bf16[256,128]{1,0:T(8,128)(2,1)S(1)} fusion(bf16[256,8,128,8]{2,0,3,1:T(8,128)(2,1)} %bitcast.77, bf16[8,8,128,128]{3,2,1,0:T(8,128)(2,1)} %bitcast.12), kind=kOutput, calls=%fused_computation.13 | convolution fusion | flops 536903680 | bytes 6356992 | tf_op jit(solution)/shard_map/trcij,tcjf->rif/dot_general | solution.py:60
  65.2 0.8 broadcast_in_dim.7
  66.0 4.1 %all-to-all-start.1 = ((bf16[8,256,128]{1,2,0:T(8,128)(2,1)}), bf16[8,256,128]{1,2,0:T(8,128)(2,1)S(1)}, u32[]{:S(2)}, u32[]{:S(2)}) async-start(bf16[8,256,128]{1,2,0:T(8,128)(2,1)} %broadcast_in_dim.7), calls=%async_computation.1 | async-start | bytes 1048576 | tf_op jit(solution)/shard_map/all_to_all | solution.py:16
  70.1 24.9 %all-gather.5.cloned.1.call-done = bf16[4096,128]{1,0:T(8,128)(2,1)} async-done(((bf16[512,128]{1,0:T(8,128)(2,1)}), bf16[4096,128]{1,0:T(8,128)(2,1)}) %all-gather.5.cloned.1.call-update) | async-done | bytes 1048592 | tf_op jit(solution)/shard_map/all_gather | solution.py:66
  95.0 1.9 copy.40
  96.9 1.1 slice_convert_fusion
  98.0 2.4 %fusion.22 = f32[256,1024]{1,0:T(8,128)S(1)} fusion(bf16[256,1024]{0,1:T(8,128)(2,1)S(1)} %bitcast.79, bf16[1024,1024]{1,0:T(8,128)(2,1)} %param.9), kind=kOutput, calls=%fused_computation.43 | convolution fusion | flops 536870912 | bytes 3670016 | tf_op jit(solution)/shard_map/dot_general | solution.py:72
  100.4 2.0 %fusion.10 = (bf16[256,1024]{1,0:T(8,128)(2,1)S(1)}, f32[256,1024]{1,0:T(8,128)}) fusion(f32[32,8,8,128]{3,2,1,0:T(8,128)S(1)} %bitcast.83, f32[256,1024]{1,0:T(8,128)S(1)} %fusion.22, bf16[1024,1024]{1,0:T(8,128)(2,1)S(1)} %copy-done, bf16[32,8,8,128]{3,2,1,0:T(8,128)(2,1)S(1)} %bitcast.84), kind=kOutput, calls=%fused_computation.15 | convolution fusion | flops 539492352 | bytes 6291456 | tf_op jit(solution)/shard_map/dot_general | solution.py:72
  103.0 1.1 maximum_bitcast_fusion
  104.1 11.6 %all-to-all-start.2 = ((f32[32,8,1024]{2,1,0:T(8,128)}), f32[32,8,1024]{2,1,0:T(8,128)}, u32[]{:S(2)}, u32[]{:S(2)}) async-start(f32[32,8,1024]{2,1,0:T(8,128)} %maximum_bitcast_fusion), calls=%async_computation.2 | async-start | bytes 2097152 | tf_op jit(solution)/shard_map/all_to_all | solution.py:22
  115.7 6.6 %copy.19 = bf16[8,8,128,128,2]{3,2,1,0,4:T(8,128)(2,1)} copy(bf16[8,8,128,128,2]{2,1,4,3,0:T(8,128)(2,1)} %bitcast.73) | data formatting | bytes 8388608 | tf_op jit(solution)/shard_map/trcij,rif->tcjf/dot_general | solution.py:107
  122.3 1.2 convolution_convert_fusion.1
  123.6 4.8 %fusion = bf16[8192,128]{1,0:T(8,128)(2,1)} fusion(bf16[8192,128,2]{1,0,2:T(8,128)(2,1)} %bitcast.74, bf16[2,128,128]{2,1,0:T(8,128)(2,1)S(1)} %bitcast.85), kind=kOutput, calls=%fused_computation.1 | convolution fusion | flops 537919488 | bytes 6356992 | tf_op jit(solution)/shard_map/trcij,rif->tcjf/dot_general | solution.py:107
  128.4 4.3 %all-to-all-done.2 = f32[32,8,1024]{2,1,0:T(8,128)} async-done(((f32[32,8,1024]{2,1,0:T(8,128)}), f32[32,8,1024]{2,1,0:T(8,128)}, u32[]{:S(2)}, u32[]{:S(2)}) %all-to-all-start.2) | async-done | bytes 1048608 | tf_op jit(solution)/shard_map/all_to_all | solution.py:22
  132.7 1.3 reduce_sum.20
  134.2 3.5 %pad_maximum_fusion = bf16[32,384,128]{2,1,0:T(8,128)(2,1)} fusion(bf16[32,128,128]{2,1,0:T(8,128)(2,1)S(1)} %broadcast_in_dim.8, bf16[32,256,128]{2,1,0:T(8,128)(2,1)} %bitcast.75), kind=kLoop, calls=%fused_computation.3 | loop fusion | flops 6291456 | bytes 6291456 | tf_op jit(solution)/shard_map/concatenate | solution.py:111
  137.8 4.6 %all-to-all-start.3 = ((bf16[32,384,128]{2,1,0:T(8,128)(2,1)}), bf16[32,384,128]{2,1,0:T(8,128)(2,1)}, u32[]{:S(2)}, u32[]{:S(2)}) async-start(bf16[32,384,128]{2,1,0:T(8,128)(2,1)} %pad_maximum_fusion), calls=%async_computation.3 | async-start | bytes 6291456 | tf_op jit(solution)/shard_map/all_to_all | solution.py:114
  142.4 1.6 multiply_convert_fusion
  144.0 38.2 %all-to-all-done.3 = bf16[32,384,128]{2,1,0:T(8,128)(2,1)} async-done(((bf16[32,384,128]{2,1,0:T(8,128)(2,1)}), bf16[32,384,128]{2,1,0:T(8,128)(2,1)}, u32[]{:S(2)}, u32[]{:S(2)}) %all-to-all-start.3) | async-done | bytes 3145760 | tf_op jit(solution)/shard_map/all_to_all | solution.py:114
  182.2 1.9 convert_reduce_fusion
  184.1 1.0 convolution_add_fusion.1
  185.1 1.4 convert_add_fusion
  186.6 0.9 mul.53
  187.5 0.9 mul.55
  (29 shorter events, 4.0 us)
Async XLA Ops:
  7.2 93.2 %copy-start = (bf16[1024,1024]{1,0:T(8,128)(2,1)S(1)}, bf16[1024,1024]{1,0:T(8,128)(2,1)}, u32[]{:S(2)}) copy-start(bf16[1024,1024]{1,0:T(8,128)(2,1)} %param.10) | copy-start | bytes 6291460
  7.2 44.4 %all-gather.3.cloned.1.call-start = ((), (), s32[]{:S(2)}) async-start(), calls=%async_computation.4 | async-start | bytes 2396160 | tf_op jit(solution)/shard_map/all_gather | solution.py:41
  13.3 8.8 %copy-start.3 = (bf16[256,128]{1,0:T(8,128)(2,1)S(1)}, bf16[256,128]{1,0:T(8,128)(2,1)}, u32[]{:S(2)}) copy-start(bf16[256,128]{1,0:T(8,128)(2,1)} %param.7) | copy-start | bytes 196612
  13.3 8.8 %copy-start.4 = (bf16[256,128]{1,0:T(8,128)(2,1)S(1)}, bf16[256,128]{1,0:T(8,128)(2,1)}, u32[]{:S(2)}) copy-start(bf16[256,128]{1,0:T(8,128)(2,1)} %param.8) | copy-start | bytes 196612
  13.3 47.6 %all-to-all-start = ((bf16[32,256,128]{2,1,0:T(8,128)(2,1)}), bf16[32,256,128]{2,1,0:T(8,128)(2,1)}, u32[]{:S(2)}, u32[]{:S(2)}) async-start(bf16[32,256,128]{2,1,0:T(8,128)(2,1)} %broadcast_in_dim.6), calls=%async_computation | async-start | bytes 4194304 | tf_op jit(solution)/shard_map/all_to_all | solution.py:16
  22.1 72.9 %all-gather.5.cloned.1.call-start = ((), (), s32[]{:S(2)}) async-start(), calls=%async_computation.5 | async-start | bytes 1179648 | tf_op jit(solution)/shard_map/all_gather | solution.py:66
  55.9 2.0 %copy-start.1 = (bf16[8,16,128,128]{3,1,2,0:T(8,128)(2,1)}, bf16[8,16,128,128]{3,1,2,0:T(8,128)(2,1)S(1)}, u32[]{:S(2)}) copy-start(bf16[8,16,128,128]{3,1,2,0:T(8,128)(2,1)S(1)} %convolution_convert_fusion) | copy-start | bytes 12582916
  66.0 32.0 %all-to-all-start.1 = ((bf16[8,256,128]{1,2,0:T(8,128)(2,1)}), bf16[8,256,128]{1,2,0:T(8,128)(2,1)S(1)}, u32[]{:S(2)}, u32[]{:S(2)}) async-start(bf16[8,256,128]{1,2,0:T(8,128)(2,1)} %broadcast_in_dim.7), calls=%async_computation.1 | async-start | bytes 1048576 | tf_op jit(solution)/shard_map/all_to_all | solution.py:16
  98.0 2.4 %copy-start.2 = (f32[1,256,8,128]{3,2,1,0:T(8,128)S(1)}, f32[1,256,8,128]{3,2,1,0:T(8,128)}, u32[]{:S(2)}) copy-start(f32[1,256,8,128]{3,2,1,0:T(8,128)} %get-tuple-element.8) | copy-start | bytes 3145732
  104.1 28.6 %all-to-all-start.2 = ((f32[32,8,1024]{2,1,0:T(8,128)}), f32[32,8,1024]{2,1,0:T(8,128)}, u32[]{:S(2)}, u32[]{:S(2)}) async-start(f32[32,8,1024]{2,1,0:T(8,128)} %maximum_bitcast_fusion), calls=%async_computation.2 | async-start | bytes 2097152 | tf_op jit(solution)/shard_map/all_to_all | solution.py:22
  137.8 44.4 %all-to-all-start.3 = ((bf16[32,384,128]{2,1,0:T(8,128)(2,1)}), bf16[32,384,128]{2,1,0:T(8,128)(2,1)}, u32[]{:S(2)}, u32[]{:S(2)}) async-start(bf16[32,384,128]{2,1,0:T(8,128)(2,1)} %pad_maximum_fusion), calls=%async_computation.3 | async-start | bytes 6291456 | tf_op jit(solution)/shard_map/all_to_all | solution.py:114
Sparse Core Ops, SparseCore 0:
  10.8 40.7 all-gather.2
  53.9 41.0 all-gather.4

commit v4 on v3

--- a/solution.py
+++ b/solution.py
@@ -83,16 +83,17 @@
     root_part = lax.dot_general(
         features, preact_grad, contract_rows, preferred_element_type=jnp.float32
     )
-    both = jnp.concatenate([weight_part, root_part], axis=0)
+    nodes = row_count * node_rows
+    grad_scale = 1.0 / math.sqrt(nodes)
+    both = jnp.concatenate([weight_part, root_part], axis=0) * grad_scale
     both_sum = reduce_rows(both, "row", row_count)
-    sum_high = both_sum.astype(jnp.bfloat16)
-    sum_low = (both_sum - sum_high.astype(jnp.float32)).astype(jnp.bfloat16)
+    high_f32 = lax.reduce_precision(both_sum, exponent_bits=8, mantissa_bits=7)
+    sum_high = high_f32.astype(jnp.bfloat16)
+    sum_low = (both_sum - high_f32).astype(jnp.bfloat16)
     sum_lanes = both_sum.size // block_edge
     sum_pair = jnp.concatenate(
         [sum_high.reshape(sum_lanes, block_edge), sum_low.reshape(sum_lanes, block_edge)], axis=0
     )
-    nodes = row_count * node_rows
-    grad_scale = 1.0 / math.sqrt(nodes)
 
     w_rows = lax.dynamic_slice_in_dim(weight, col_index * feat_dev, feat_dev, 0)
     r_rows = lax.dynamic_slice_in_dim(root_weight, col_index * feat_dev, feat_dev, 0)
@@ -111,6 +112,7 @@
     outgoing = jnp.concatenate(
         [term_pieces, jnp.broadcast_to(sum_pair[None], (row_count,) + sum_pair.shape)], axis=1
     )
+    outgoing, own_grad = lax.optimization_barrier((outgoing, own_grad))
     incoming = lax.all_to_all(outgoing, "row", 0, 0, tiled=True)
     summed_cols = incoming[:, :node_rows].astype(jnp.float32).sum(0)
     got_high = incoming[:, node_rows : node_rows + sum_lanes].astype(jnp.float32)
@@ -119,7 +121,7 @@
     weight_sum = both_all[:feat_dev]
     root_sum = both_all[feat_dev:]
     feature_grad = summed_cols + own_grad
-    return (activations, feature_grad, weight_sum * grad_scale, root_sum * grad_scale)
+    return (activations, feature_grad, weight_sum, root_sum)
 
 
 def solution(mesh):

time: 196 us -> 196 us (level)
  no operation moved by 1% of the time
where the time goes in v4:
time: 196 us; the launch traced here: 195 us
  waiting for transfers between devices  95.8 us (49%)
  starting transfers between devices  29.2 us (15%)
  local copies, waits for them, and re-layouts  21 us (11%)
  matrix products  17.3 us (9%)
  other arithmetic  16.5 us (8%)
  between operations  15 us (8%)
    all_to_all x1, waiting for transfers between devices, per_device(): incoming = lax.all_to_all(outgoing, 'row', 0, 0, tiled=True)  38.2 us
    all_gather x1, waiting for transfers between devices, per_device(): lax.all_gather(packed, 'col', axis=0, tiled=True)  28.7 us
    all_gather x1, waiting for transfers between devices, per_device(): lax.all_gather(own_pair, 'col', axis=0, tiled=True)  24.9 us
    all_to_all x2, starting transfers between devices, gather_rows(): got = lax.all_to_all(spread, axis_name, 0, 0, tiled=True)  12.9 us
    all_to_all x1, starting transfers between devices, reduce_rows(): got = lax.all_to_all(pieces, axis_name, 0, 0, tiled=True)  11.6 us
    dot_general x1, local copies, waits for them, and re-layouts, per_device(): jnp.einsum('trcij,rif->tcjf', dense, g_rows, preferred_element_type=jnp.f...  6.61 us
    dot_general x1, matrix products, per_device(): jnp.einsum('trcij,rif->tcjf', dense, g_rows, preferred_element_type=jnp.f...  4.82 us
    all_to_all x1, starting transfers between devices, per_device(): incoming = lax.all_to_all(outgoing, 'row', 0, 0, tiled=True)  4.6 us
  transfers between devices with their start and end apart: 6, of which 4 were waited for; matrix products, arithmetic and copies ran while one was open for 17% of the time, Pallas kernels for 0%

profile of v4, /device:TPU:1, one launch (start us, length us, event | category | flops | bytes accessed | tf_op | source)
XLA Modules:
  0.0 194.9 jit_solution(17060304707076260827)
XLA Ops:
  8.8 1.1 bitcast_multiply_fusion.1
  10.7 2.6 %broadcast_in_dim.6 = bf16[32,256,128]{2,1,0:T(8,128)(2,1)} broadcast(bf16[256,128]{1,0:T(8,128)(2,1)} %param.7), dimensions={1,2} | broadcast | bytes 2162688 | tf_op jit(solution)/shard_map/broadcast_in_dim | solution.py:15
  13.3 8.8 %all-to-all-start = ((bf16[32,256,128]{2,1,0:T(8,128)(2,1)}), bf16[32,256,128]{2,1,0:T(8,128)(2,1)}, u32[]{:S(2)}, u32[]{:S(2)}) async-start(bf16[32,256,128]{2,1,0:T(8,128)(2,1)} %broadcast_in_dim.6), calls=%async_computation | async-start | bytes 4194304 | tf_op jit(solution)/shard_map/all_to_all | solution.py:16
  22.8 28.7 %all-gather.3.cloned.1.call-done = bf16[8320,128]{1,0:T(8,128)(2,1)} async-done(((bf16[1040,128]{1,0:T(8,128)(2,1)}), bf16[8320,128]{1,0:T(8,128)(2,1)}) %all-gather.3.cloned.1.call-update) | async-done | bytes 2129936 | tf_op jit(solution)/shard_map/all_gather | solution.py:41
  51.6 1.7 slice.47
  53.3 0.7 slice_convert_fusion.1
  54.0 1.9 convolution_convert_fusion
  55.9 2.0 %copy-done.1 = bf16[8,16,128,128]{3,1,2,0:T(8,128)(2,1)} copy-done((bf16[8,16,128,128]{3,1,2,0:T(8,128)(2,1)}, bf16[8,16,128,128]{3,1,2,0:T(8,128)(2,1)S(1)}, u32[]{:S(2)}) %copy-start.1) | copy-done | bytes 4194328
  57.8 3.1 %copy.15 = bf16[2,128,8,128,8]{3,1,0,4,2:T(8,128)(2,1)} copy(bf16[2,128,8,128,8]{3,2,0,1,4:T(8,128)(2,1)S(1)} %bitcast.72) | data formatting | bytes 8388608 | tf_op jit(solution)/shard_map/trcij,tcjf->rif/dot_general | solution.py:60
  60.9 4.1 %fusion.7 = bf16[256,128]{1,0:T(8,128)(2,1)S(1)} fusion(bf16[256,8,128,8]{2,0,3,1:T(8,128)(2,1)} %bitcast.77, bf16[8,8,128,128]{3,2,1,0:T(8,128)(2,1)} %bitcast.12), kind=kOutput, calls=%fused_computation.12 | convolution fusion | flops 536903680 | bytes 6356992 | tf_op jit(solution)/shard_map/trcij,tcjf->rif/dot_general | solution.py:60
  65.2 0.8 broadcast_in_dim.7
  66.0 4.1 %all-to-all-start.1 = ((bf16[8,256,128]{1,2,0:T(8,128)(2,1)}), bf16[8,256,128]{1,2,0:T(8,128)(2,1)S(1)}, u32[]{:S(2)}, u32[]{:S(2)}) async-start(bf16[8,256,128]{1,2,0:T(8,128)(2,1)} %broadcast_in_dim.7), calls=%async_computation.1 | async-start | bytes 1048576 | tf_op jit(solution)/shard_map/all_to_all | solution.py:16
  70.1 24.9 %all-gather.5.cloned.1.call-done = bf16[4096,128]{1,0:T(8,128)(2,1)} async-done(((bf16[512,128]{1,0:T(8,128)(2,1)}), bf16[4096,128]{1,0:T(8,128)(2,1)}) %all-gather.5.cloned.1.call-update) | async-done | bytes 1048592 | tf_op jit(solution)/shard_map/all_gather | solution.py:66
  95.0 1.9 copy.40
  96.9 1.1 slice_convert_fusion
  98.0 2.4 %fusion.26 = f32[256,1024]{1,0:T(8,128)S(1)} fusion(bf16[256,1024]{0,1:T(8,128)(2,1)S(1)} %bitcast.79, bf16[1024,1024]{1,0:T(8,128)(2,1)} %param.9), kind=kOutput, calls=%fused_computation.45 | convolution fusion | flops 536870912 | bytes 3670016 | tf_op jit(solution)/shard_map/dot_general | solution.py:72
  100.4 2.0 %fusion.10 = (bf16[256,1024]{1,0:T(8,128)(2,1)S(1)}, f32[256,1024]{1,0:T(8,128)}) fusion(f32[32,8,8,128]{3,2,1,0:T(8,128)S(1)} %bitcast.83, f32[256,1024]{1,0:T(8,128)S(1)} %fusion.26, bf16[1024,1024]{1,0:T(8,128)(2,1)S(1)} %copy-done, bf16[32,8,8,128]{3,2,1,0:T(8,128)(2,1)S(1)} %bitcast.84), kind=kOutput, calls=%fused_computation.14 | convolution fusion | flops 539492352 | bytes 6291456 | tf_op jit(solution)/shard_map/dot_general | solution.py:72
  103.0 1.1 fusion.11
  104.1 11.6 %all-to-all-start.2 = ((f32[32,8,1024]{2,1,0:T(8,128)}), f32[32,8,1024]{2,1,0:T(8,128)}, u32[]{:S(2)}, u32[]{:S(2)}) async-start(f32[32,8,1024]{2,1,0:T(8,128)} %fusion.11), calls=%async_computation.2 | async-start | bytes 2097152 | tf_op jit(solution)/shard_map/all_to_all | solution.py:22
  115.7 6.6 %copy.19 = bf16[8,8,128,128,2]{3,2,1,0,4:T(8,128)(2,1)} copy(bf16[8,8,128,128,2]{2,1,4,3,0:T(8,128)(2,1)} %bitcast.73) | data formatting | bytes 8388608 | tf_op jit(solution)/shard_map/trcij,rif->tcjf/dot_general | solution.py:108
  122.4 1.2 convolution_convert_fusion.1
  123.9 4.8 %fusion = bf16[8192,128]{1,0:T(8,128)(2,1)} fusion(bf16[8192,128,2]{1,0,2:T(8,128)(2,1)} %bitcast.74, bf16[2,128,128]{2,1,0:T(8,128)(2,1)S(1)} %bitcast.85), kind=kOutput, calls=%fused_computation.1 | convolution fusion | flops 537919488 | bytes 6356992 | tf_op jit(solution)/shard_map/trcij,rif->tcjf/dot_general | solution.py:108
  128.8 3.9 %all-to-all-done.2 = f32[32,8,1024]{2,1,0:T(8,128)} async-done(((f32[32,8,1024]{2,1,0:T(8,128)}), f32[32,8,1024]{2,1,0:T(8,128)}, u32[]{:S(2)}, u32[]{:S(2)}) %all-to-all-start.2) | async-done | bytes 1048608 | tf_op jit(solution)/shard_map/all_to_all | solution.py:22
  132.7 1.3 reduce_sum.20
  134.3 3.5 %pad_maximum_fusion = bf16[32,384,128]{2,1,0:T(8,128)(2,1)} fusion(bf16[32,128,128]{2,1,0:T(8,128)(2,1)S(1)} %broadcast_in_dim.8, bf16[32,256,128]{2,1,0:T(8,128)(2,1)} %bitcast.75), kind=kLoop, calls=%fused_computation.3 | loop fusion | flops 6291456 | bytes 6291456 | tf_op jit(solution)/shard_map/concatenate | solution.py:112
  137.8 4.6 %all-to-all-start.3 = ((bf16[32,384,128]{2,1,0:T(8,128)(2,1)}), bf16[32,384,128]{2,1,0:T(8,128)(2,1)}, u32[]{:S(2)}, u32[]{:S(2)}) async-start(bf16[32,384,128]{2,1,0:T(8,128)(2,1)} %pad_maximum_fusion), calls=%async_computation.3 | async-start | bytes 6291456 | tf_op jit(solution)/shard_map/all_to_all | solution.py:116
  142.4 1.6 multiply_convert_fusion
  144.0 38.2 %all-to-all-done.3 = bf16[32,384,128]{2,1,0:T(8,128)(2,1)} async-done(((bf16[32,384,128]{2,1,0:T(8,128)(2,1)}), bf16[32,384,128]{2,1,0:T(8,128)(2,1)}, u32[]{:S(2)}, u32[]{:S(2)}) %all-to-all-start.3) | async-done | bytes 3145760 | tf_op jit(solution)/shard_map/all_to_all | solution.py:116
  182.3 1.4 convert_add_fusion
  183.7 0.9 slice.43
  184.6 0.9 slice.45
  185.5 1.9 convert_reduce_fusion
  (30 shorter events, 4.2 us)
Async XLA Ops:
  7.2 93.2 %copy-start = (bf16[1024,1024]{1,0:T(8,128)(2,1)S(1)}, bf16[1024,1024]{1,0:T(8,128)(2,1)}, u32[]{:S(2)}) copy-start(bf16[1024,1024]{1,0:T(8,128)(2,1)} %param.10) | copy-start | bytes 6291460
  7.2 44.4 %all-gather.3.cloned.1.call-start = ((), (), s32[]{:S(2)}) async-start(), calls=%async_computation.4 | async-start | bytes 2396160 | tf_op jit(solution)/shard_map/all_gather | solution.py:41
  13.3 8.8 %copy-start.3 = (bf16[256,128]{1,0:T(8,128)(2,1)S(1)}, bf16[256,128]{1,0:T(8,128)(2,1)}, u32[]{:S(2)}) copy-start(bf16[256,128]{1,0:T(8,128)(2,1)} %param.7) | copy-start | bytes 196612
  13.3 8.8 %copy-start.4 = (bf16[256,128]{1,0:T(8,128)(2,1)S(1)}, bf16[256,128]{1,0:T(8,128)(2,1)}, u32[]{:S(2)}) copy-start(bf16[256,128]{1,0:T(8,128)(2,1)} %param.8) | copy-start | bytes 196612
  13.3 47.6 %all-to-all-start = ((bf16[32,256,128]{2,1,0:T(8,128)(2,1)}), bf16[32,256,128]{2,1,0:T(8,128)(2,1)}, u32[]{:S(2)}, u32[]{:S(2)}) async-start(bf16[32,256,128]{2,1,0:T(8,128)(2,1)} %broadcast_in_dim.6), calls=%async_computation | async-start | bytes 4194304 | tf_op jit(solution)/shard_map/all_to_all | solution.py:16
  22.1 72.9 %all-gather.5.cloned.1.call-start = ((), (), s32[]{:S(2)}) async-start(), calls=%async_computation.5 | async-start | bytes 1179648 | tf_op jit(solution)/shard_map/all_gather | solution.py:66
  55.9 2.0 %copy-start.1 = (bf16[8,16,128,128]{3,1,2,0:T(8,128)(2,1)}, bf16[8,16,128,128]{3,1,2,0:T(8,128)(2,1)S(1)}, u32[]{:S(2)}) copy-start(bf16[8,16,128,128]{3,1,2,0:T(8,128)(2,1)S(1)} %convolution_convert_fusion) | copy-start | bytes 12582916
  66.0 32.0 %all-to-all-start.1 = ((bf16[8,256,128]{1,2,0:T(8,128)(2,1)}), bf16[8,256,128]{1,2,0:T(8,128)(2,1)S(1)}, u32[]{:S(2)}, u32[]{:S(2)}) async-start(bf16[8,256,128]{1,2,0:T(8,128)(2,1)} %broadcast_in_dim.7), calls=%async_computation.1 | async-start | bytes 1048576 | tf_op jit(solution)/shard_map/all_to_all | solution.py:16
  98.0 2.4 %copy-start.2 = (f32[1,256,8,128]{3,2,1,0:T(8,128)S(1)}, f32[1,256,8,128]{3,2,1,0:T(8,128)}, u32[]{:S(2)}) copy-start(f32[1,256,8,128]{3,2,1,0:T(8,128)} %get-tuple-element.10) | copy-start | bytes 3145732
  104.1 28.6 %all-to-all-start.2 = ((f32[32,8,1024]{2,1,0:T(8,128)}), f32[32,8,1024]{2,1,0:T(8,128)}, u32[]{:S(2)}, u32[]{:S(2)}) async-start(f32[32,8,1024]{2,1,0:T(8,128)} %fusion.11), calls=%async_computation.2 | async-start | bytes 2097152 | tf_op jit(solution)/shard_map/all_to_all | solution.py:22
  137.8 44.4 %all-to-all-start.3 = ((bf16[32,384,128]{2,1,0:T(8,128)(2,1)}), bf16[32,384,128]{2,1,0:T(8,128)(2,1)}, u32[]{:S(2)}, u32[]{:S(2)}) async-start(bf16[32,384,128]{2,1,0:T(8,128)(2,1)} %pad_maximum_fusion), calls=%async_computation.3 | async-start | bytes 6291456 | tf_op jit(solution)/shard_map/all_to_all | solution.py:116
Sparse Core Ops, SparseCore 0:
  10.8 40.7 all-gather.2
  53.9 41.0 all-gather.4

commit v5 on v4

--- a/solution.py
+++ b/solution.py
@@ -63,9 +63,12 @@
     agg_parts = gather_rows(aggregated, "col", col_count).reshape(col_count, node_rows, feat_dev)
     agg_full = jnp.moveaxis(agg_parts, 0, 1).reshape(node_rows, col_count * feat_dev)
     own_pair = jnp.concatenate([features, grad_out], axis=0)
-    pair_parts = lax.all_gather(own_pair, "col", axis=0, tiled=True).reshape(
-        col_count, 2, node_rows, feat_dev
-    )
+    shifted = [own_pair] + [
+        lax.ppermute(own_pair, "col", [(i, (i + k) % col_count) for i in range(col_count)])
+        for k in range(1, col_count)
+    ]
+    by_source = (col_index - jnp.arange(col_count, dtype=jnp.int32)) % col_count
+    pair_parts = jnp.stack(shifted)[by_source].reshape(col_count, 2, node_rows, feat_dev)
     pair_full = jnp.moveaxis(pair_parts, 0, 2).reshape(2, node_rows, col_count * feat_dev)
     feat_full = pair_full[0]
     grad_full = pair_full[1]

time: 196 us -> 205 us (1.046)
  starting transfers between devices: 29.2 us -> 42.6 us
  waiting for transfers between devices: 95.8 us -> 85.6 us
  local copies, waits for them, and re-layouts: 21 us -> 27.1 us
    all_gather x1 -> x0, waiting for transfers between devices: 24.9 us -> none  [per_device(): lax.all_gather(own_pair, 'col', axis=0, tiled=True)]
    ppermute x0 -> x7, waiting for transfers between devices: none -> 17.1 us  [per_device(): lax.ppermute(own_pair, 'col', [(i, (i + k) % col_count) for i in range(co...]
    ppermute x0 -> x7, starting transfers between devices: none -> 16.1 us  [per_device(): lax.ppermute(own_pair, 'col', [(i, (i + k) % col_count) for i in range(co...]
    all_gather x1, waiting for transfers between devices: 28.7 us -> 15.9 us  [per_device(): lax.all_gather(packed, 'col', axis=0, tiled=True)]
    all_to_all x2, waiting for transfers between devices: 0.01 us -> 10.5 us  [gather_rows(): got = lax.all_to_all(spread, axis_name, 0, 0, tiled=True)]
    unnamed x10 -> x18, local copies, waits for them, and re-layouts: 1.98 us -> 6.58 us
    all_to_all x1, starting transfers between devices: 11.6 us -> 8.76 us  [reduce_rows(): got = lax.all_to_all(pieces, axis_name, 0, 0, tiled=True)]
  transfers between devices with their start and end apart: 6 -> 12, of which waited for: 4 -> 7; matrix products, arithmetic and copies ran while one was open for 17% -> 19% of each run, Pallas kernels for 0% -> 0%
where the time goes in v5:
time: 205 us; the launch traced here: 204 us
  waiting for transfers between devices  85.6 us (42%)
  starting transfers between devices  42.6 us (21%)
  local copies, waits for them, and re-layouts  27.1 us (13%)
  matrix products  17.5 us (9%)
  other arithmetic  15.9 us (8%)
  between operations  15.1 us (7%)
    all_to_all x1, waiting for transfers between devices, per_device(): incoming = lax.all_to_all(outgoing, 'row', 0, 0, tiled=True)  38.2 us
    ppermute x7, waiting for transfers between devices, per_device(): lax.ppermute(own_pair, 'col', [(i, (i + k) % col_count) for i in range(co...  17.1 us
    ppermute x7, starting transfers between devices, per_device(): lax.ppermute(own_pair, 'col', [(i, (i + k) % col_count) for i in range(co...  16.1 us
    all_gather x1, waiting for transfers between devices, per_device(): lax.all_gather(packed, 'col', axis=0, tiled=True)  15.9 us
    all_to_all x2, starting transfers between devices, gather_rows(): got = lax.all_to_all(spread, axis_name, 0, 0, tiled=True)  13.1 us
    all_to_all x2, waiting for transfers between devices, gather_rows(): got = lax.all_to_all(spread, axis_name, 0, 0, tiled=True)  10.5 us
    all_to_all x1, starting transfers between devices, reduce_rows(): got = lax.all_to_all(pieces, axis_name, 0, 0, tiled=True)  8.76 us
    dot_general x1, local copies, waits for them, and re-layouts, per_device(): jnp.einsum('trcij,rif->tcjf', dense, g_rows, preferred_element_type=jnp.f...  6.61 us
  transfers between devices with their start and end apart: 12, of which 7 were waited for; matrix products, arithmetic and copies ran while one was open for 19% of the time, Pallas kernels for 0%

profile of v5, /device:TPU:1, one launch (start us, length us, event | category | flops | bytes accessed | tf_op | source)
XLA Modules:
  0.0 203.6 jit_solution(13568781306424068090)
XLA Ops:
  10.7 2.6 %broadcast_in_dim.6 = bf16[32,256,128]{2,1,0:T(8,128)(2,1)} broadcast(bf16[256,128]{1,0:T(8,128)(2,1)} %param.7), dimensions={1,2} | broadcast | bytes 2162688 | tf_op jit(solution)/shard_map/broadcast_in_dim | solution.py:15
  13.3 8.8 %all-to-all-start = ((bf16[32,256,128]{2,1,0:T(8,128)(2,1)}), bf16[32,256,128]{2,1,0:T(8,128)(2,1)}, u32[]{:S(2)}, u32[]{:S(2)}) async-start(bf16[32,256,128]{2,1,0:T(8,128)(2,1)} %broadcast_in_dim.6), calls=%async_computation | async-start | bytes 4194304 | tf_op jit(solution)/shard_map/all_to_all | solution.py:16
  22.1 1.7 collective-permute-start
  23.8 3.0 %collective-permute-start.1 = (bf16[512,128]{1,0:T(8,128)(2,1)S(1)}, bf16[512,128]{1,0:T(8,128)(2,1)S(1)}, u32[]{:S(2)}, u32[]{:S(2)}) collective-permute-start(bf16[512,128]{1,0:T(8,128)(2,1)S(1)} %constant_dynamic-update-slice_fusion), channel_id=1, source_target_pairs={{0,2},{1,3},{2,4},{3,5},{4,6},{5,7},{6,0},{7,1},{8,10},{9,11},{10,... | collective-permute-start | bytes 393224 | tf_op jit(solution)/shard_map/ppermute | solution.py:67
  26.8 3.8 %collective-permute-start.2 = (bf16[512,128]{1,0:T(8,128)(2,1)S(1)}, bf16[512,128]{1,0:T(8,128)(2,1)S(1)}, u32[]{:S(2)}, u32[]{:S(2)}) collective-permute-start(bf16[512,128]{1,0:T(8,128)(2,1)S(1)} %constant_dynamic-update-slice_fusion), channel_id=1, source_target_pairs={{0,3},{1,4},{2,5},{3,6},{4,7},{5,0},{6,1},{7,2},{8,11},{9,12},{10,... | collective-permute-start | bytes 393224 | tf_op jit(solution)/shard_map/ppermute | solution.py:67
  31.1 4.5 %collective-permute-start.4 = (bf16[512,128]{1,0:T(8,128)(2,1)S(1)}, bf16[512,128]{1,0:T(8,128)(2,1)S(1)}, u32[]{:S(2)}, u32[]{:S(2)}) collective-permute-start(bf16[512,128]{1,0:T(8,128)(2,1)S(1)} %constant_dynamic-update-slice_fusion), channel_id=1, source_target_pairs={{0,5},{1,6},{2,7},{3,0},{4,1},{5,2},{6,3},{7,4},{8,13},{9,14},{10,... | collective-permute-start | bytes 393224 | tf_op jit(solution)/shard_map/ppermute | solution.py:67
  36.2 2.5 %collective-permute-start.5 = (bf16[512,128]{1,0:T(8,128)(2,1)S(1)}, bf16[512,128]{1,0:T(8,128)(2,1)S(1)}, u32[]{:S(2)}, u32[]{:S(2)}) collective-permute-start(bf16[512,128]{1,0:T(8,128)(2,1)S(1)} %constant_dynamic-update-slice_fusion), channel_id=1, source_target_pairs={{0,6},{1,7},{2,0},{3,1},{4,2},{5,3},{6,4},{7,5},{8,14},{9,15},{10,... | collective-permute-start | bytes 393224 | tf_op jit(solution)/shard_map/ppermute | solution.py:67
  39.4 3.7 %collective-permute-done.1 = bf16[512,128]{1,0:T(8,128)(2,1)S(1)} collective-permute-done((bf16[512,128]{1,0:T(8,128)(2,1)S(1)}, bf16[512,128]{1,0:T(8,128)(2,1)S(1)}, u32[]{:S(2)}, u32[]{:S(2)}) %collective-permute-start.1) | collective-permute-done | bytes 131104 | tf_op jit(solution)/shard_map/ppermute | solution.py:67
  43.9 8.0 %collective-permute-done.2 = bf16[512,128]{1,0:T(8,128)(2,1)S(1)} collective-permute-done((bf16[512,128]{1,0:T(8,128)(2,1)S(1)}, bf16[512,128]{1,0:T(8,128)(2,1)S(1)}, u32[]{:S(2)}, u32[]{:S(2)}) %collective-permute-start.2) | collective-permute-done | bytes 131104 | tf_op jit(solution)/shard_map/ppermute | solution.py:67
  52.5 5.4 %collective-permute-done.3 = bf16[512,128]{1,0:T(8,128)(2,1)S(1)} collective-permute-done((bf16[512,128]{1,0:T(8,128)(2,1)S(1)}, bf16[512,128]{1,0:T(8,128)(2,1)S(1)}, u32[]{:S(2)}, u32[]{:S(2)}) %collective-permute-start.3) | collective-permute-done | bytes 131104 | tf_op jit(solution)/shard_map/ppermute | solution.py:67
  58.6 15.9 %all-gather.2.cloned.1.call-done = bf16[8320,128]{1,0:T(8,128)(2,1)} async-done(((bf16[1040,128]{1,0:T(8,128)(2,1)}), bf16[8320,128]{1,0:T(8,128)(2,1)}) %all-gather.2.cloned.1.call-update) | async-done | bytes 2129936 | tf_op jit(solution)/shard_map/all_gather | solution.py:41
  74.4 1.7 slice.49
  76.9 1.9 convolution_convert_fusion
  78.8 1.9 copy-done.1
  80.7 3.1 %copy.15 = bf16[2,128,8,128,8]{3,1,0,4,2:T(8,128)(2,1)} copy(bf16[2,128,8,128,8]{3,2,0,1,4:T(8,128)(2,1)S(1)} %bitcast.90) | data formatting | bytes 8388608 | tf_op jit(solution)/shard_map/trcij,tcjf->rif/dot_general | solution.py:60
  83.8 4.1 %fusion.7 = bf16[256,128]{1,0:T(8,128)(2,1)S(1)} fusion(bf16[256,8,128,8]{2,0,3,1:T(8,128)(2,1)} %bitcast.96, bf16[8,8,128,128]{3,2,1,0:T(8,128)(2,1)} %bitcast.12), kind=kOutput, calls=%fused_computation.13 | convolution fusion | flops 536903680 | bytes 6356992 | tf_op jit(solution)/shard_map/trcij,tcjf->rif/dot_general | solution.py:60
  88.9 4.3 %all-to-all-start.1 = ((bf16[8,256,128]{1,2,0:T(8,128)(2,1)}), bf16[8,256,128]{1,2,0:T(8,128)(2,1)}, u32[]{:S(2)}, u32[]{:S(2)}) async-start(bf16[8,256,128]{1,2,0:T(8,128)(2,1)} %broadcast_in_dim.7), calls=%async_computation.1 | async-start | bytes 1048576 | tf_op jit(solution)/shard_map/all_to_all | solution.py:16
  95.2 2.0 gather_fusion
  99.0 10.5 %all-to-all-done.1 = bf16[8,256,128]{1,2,0:T(8,128)(2,1)} async-done(((bf16[8,256,128]{1,2,0:T(8,128)(2,1)}), bf16[8,256,128]{1,2,0:T(8,128)(2,1)}, u32[]{:S(2)}, u32[]{:S(2)}) %all-to-all-start.1) | async-done | bytes 524320 | tf_op jit(solution)/shard_map/all_to_all | solution.py:16
  109.4 2.6 %fusion.28 = f32[256,1024]{1,0:T(8,128)S(1)} fusion(bf16[256,1024]{0,1:T(8,128)(2,1)} %bitcast.16, bf16[1024,1024]{1,0:T(8,128)(2,1)} %param.9), kind=kOutput, calls=%fused_computation.62 | convolution fusion | flops 536870912 | bytes 3670016 | tf_op jit(solution)/shard_map/dot_general | solution.py:75
  112.0 2.0 %fusion.10 = (bf16[256,1024]{1,0:T(8,128)(2,1)S(1)}, f32[256,1024]{1,0:T(8,128)}) fusion(f32[32,8,8,128]{3,2,1,0:T(8,128)S(1)} %bitcast.100, f32[256,1024]{1,0:T(8,128)S(1)} %fusion.28, bf16[1024,1024]{1,0:T(8,128)(2,1)S(1)} %copy-done, bf16[32,8,8,128]{3,2,1,0:T(8,128)(2,1)S(1)} %bitcast.101), kind=kOutput, calls=%fused_computation.15 | convolution fusion | flops 539492352 | bytes 6291456 | tf_op jit(solution)/shard_map/dot_general | solution.py:75
  115.7 8.8 %all-to-all-start.2 = ((f32[32,8,1024]{2,1,0:T(8,128)}), f32[32,8,1024]{2,1,0:T(8,128)}, u32[]{:S(2)}, u32[]{:S(2)}) async-start(f32[32,8,1024]{2,1,0:T(8,128)} %fusion.11), calls=%async_computation.2 | async-start | bytes 2097152 | tf_op jit(solution)/shard_map/all_to_all | solution.py:22
  124.5 6.6 %copy.19 = bf16[8,8,128,128,2]{3,2,1,0,4:T(8,128)(2,1)} copy(bf16[8,8,128,128,2]{2,1,4,3,0:T(8,128)(2,1)} %bitcast.91) | data formatting | bytes 8388608 | tf_op jit(solution)/shard_map/trcij,rif->tcjf/dot_general | solution.py:111
  132.7 4.8 %fusion = bf16[8192,128]{1,0:T(8,128)(2,1)} fusion(bf16[8192,128,2]{1,0,2:T(8,128)(2,1)} %bitcast.92, bf16[2,128,128]{2,1,0:T(8,128)(2,1)S(1)} %bitcast.102), kind=kOutput, calls=%fused_computation.2 | convolution fusion | flops 537919488 | bytes 6356992 | tf_op jit(solution)/shard_map/trcij,rif->tcjf/dot_general | solution.py:111
  137.5 3.9 %all-to-all-done.2 = f32[32,8,1024]{2,1,0:T(8,128)} async-done(((f32[32,8,1024]{2,1,0:T(8,128)}), f32[32,8,1024]{2,1,0:T(8,128)}, u32[]{:S(2)}, u32[]{:S(2)}) %all-to-all-start.2) | async-done | bytes 1048608 | tf_op jit(solution)/shard_map/all_to_all | solution.py:22
  141.4 1.3 reduce_sum.20
  143.0 3.5 %pad_maximum_fusion = bf16[32,384,128]{2,1,0:T(8,128)(2,1)} fusion(bf16[32,128,128]{2,1,0:T(8,128)(2,1)S(1)} %broadcast_in_dim.8, bf16[32,256,128]{2,1,0:T(8,128)(2,1)} %bitcast.93), kind=kLoop, calls=%fused_computation.4 | loop fusion | flops 6291456 | bytes 6291456 | tf_op jit(solution)/shard_map/concatenate | solution.py:115
  146.6 4.6 %all-to-all-start.3 = ((bf16[32,384,128]{2,1,0:T(8,128)(2,1)}), bf16[32,384,128]{2,1,0:T(8,128)(2,1)}, u32[]{:S(2)}, u32[]{:S(2)}) async-start(bf16[32,384,128]{2,1,0:T(8,128)(2,1)} %pad_maximum_fusion), calls=%async_computation.3 | async-start | bytes 6291456 | tf_op jit(solution)/shard_map/all_to_all | solution.py:119
  151.2 1.6 multiply_convert_fusion
  152.8 38.2 %all-to-all-done.3 = bf16[32,384,128]{2,1,0:T(8,128)(2,1)} async-done(((bf16[32,384,128]{2,1,0:T(8,128)(2,1)}), bf16[32,384,128]{2,1,0:T(8,128)(2,1)}, u32[]{:S(2)}, u32[]{:S(2)}) %all-to-all-start.3) | async-done | bytes 3145760 | tf_op jit(solution)/shard_map/all_to_all | solution.py:119
  191.0 1.4 convert_add_fusion
  194.2 1.9 convert_reduce_fusion
  (53 shorter events, 18.0 us)
Async XLA Ops:
  7.2 104.8 %copy-start = (bf16[1024,1024]{1,0:T(8,128)(2,1)S(1)}, bf16[1024,1024]{1,0:T(8,128)(2,1)}, u32[]{:S(2)}) copy-start(bf16[1024,1024]{1,0:T(8,128)(2,1)} %param.10) | copy-start | bytes 6291460
  7.2 67.3 %all-gather.2.cloned.1.call-start = ((), (), s32[]{:S(2)}) async-start(), calls=%async_computation.4 | async-start | bytes 2396160 | tf_op jit(solution)/shard_map/all_gather | solution.py:41
  13.3 8.8 %copy-start.3 = (bf16[256,128]{1,0:T(8,128)(2,1)S(1)}, bf16[256,128]{1,0:T(8,128)(2,1)}, u32[]{:S(2)}) copy-start(bf16[256,128]{1,0:T(8,128)(2,1)} %param.7) | copy-start | bytes 196612
  13.3 8.8 %copy-start.4 = (bf16[256,128]{1,0:T(8,128)(2,1)S(1)}, bf16[256,128]{1,0:T(8,128)(2,1)}, u32[]{:S(2)}) copy-start(bf16[256,128]{1,0:T(8,128)(2,1)} %param.8) | copy-start | bytes 196612
  13.3 70.5 %all-to-all-start = ((bf16[32,256,128]{2,1,0:T(8,128)(2,1)}), bf16[32,256,128]{2,1,0:T(8,128)(2,1)}, u32[]{:S(2)}, u32[]{:S(2)}) async-start(bf16[32,256,128]{2,1,0:T(8,128)(2,1)} %broadcast_in_dim.6), calls=%async_computation | async-start | bytes 4194304 | tf_op jit(solution)/shard_map/all_to_all | solution.py:16
  22.1 14.1 %collective-permute-start = (bf16[512,128]{1,0:T(8,128)(2,1)S(1)}, bf16[512,128]{1,0:T(8,128)(2,1)S(1)}, u32[]{:S(2)}, u32[]{:S(2)}) collective-permute-start(bf16[512,128]{1,0:T(8,128)(2,1)S(1)} %constant_dynamic-update-slice_fusion), channel_id=1, source_target_pairs={{0,1},{1,2},{2,3},{3,4},{4,5},{5,6},{6,7},{7,0},{8,9},{9,10},{10,1... | collective-permute-start | bytes 393224 | tf_op jit(solution)/shard_map/ppermute | solution.py:67
  23.8 19.2 %collective-permute-start.1 = (bf16[512,128]{1,0:T(8,128)(2,1)S(1)}, bf16[512,128]{1,0:T(8,128)(2,1)S(1)}, u32[]{:S(2)}, u32[]{:S(2)}) collective-permute-start(bf16[512,128]{1,0:T(8,128)(2,1)S(1)} %constant_dynamic-update-slice_fusion), channel_id=1, source_target_pairs={{0,2},{1,3},{2,4},{3,5},{4,6},{5,7},{6,0},{7,1},{8,10},{9,11},{10,... | collective-permute-start | bytes 393224 | tf_op jit(solution)/shard_map/ppermute | solution.py:67
  26.8 25.0 %collective-permute-start.2 = (bf16[512,128]{1,0:T(8,128)(2,1)S(1)}, bf16[512,128]{1,0:T(8,128)(2,1)S(1)}, u32[]{:S(2)}, u32[]{:S(2)}) collective-permute-start(bf16[512,128]{1,0:T(8,128)(2,1)S(1)} %constant_dynamic-update-slice_fusion), channel_id=1, source_target_pairs={{0,3},{1,4},{2,5},{3,6},{4,7},{5,0},{6,1},{7,2},{8,11},{9,12},{10,... | collective-permute-start | bytes 393224 | tf_op jit(solution)/shard_map/ppermute | solution.py:67
  30.6 27.3 %collective-permute-start.3 = (bf16[512,128]{1,0:T(8,128)(2,1)S(1)}, bf16[512,128]{1,0:T(8,128)(2,1)S(1)}, u32[]{:S(2)}, u32[]{:S(2)}) collective-permute-start(bf16[512,128]{1,0:T(8,128)(2,1)S(1)} %constant_dynamic-update-slice_fusion), channel_id=1, source_target_pairs={{0,4},{1,5},{2,6},{3,7},{4,0},{5,1},{6,2},{7,3},{8,12},{9,13},{10,... | collective-permute-start | bytes 393224 | tf_op jit(solution)/shard_map/ppermute | solution.py:67
  31.1 62.2 %collective-permute-start.4 = (bf16[512,128]{1,0:T(8,128)(2,1)S(1)}, bf16[512,128]{1,0:T(8,128)(2,1)S(1)}, u32[]{:S(2)}, u32[]{:S(2)}) collective-permute-start(bf16[512,128]{1,0:T(8,128)(2,1)S(1)} %constant_dynamic-update-slice_fusion), channel_id=1, source_target_pairs={{0,5},{1,6},{2,7},{3,0},{4,1},{5,2},{6,3},{7,4},{8,13},{9,14},{10,... | collective-permute-start | bytes 393224 | tf_op jit(solution)/shard_map/ppermute | solution.py:67
  36.2 57.7 %collective-permute-start.5 = (bf16[512,128]{1,0:T(8,128)(2,1)S(1)}, bf16[512,128]{1,0:T(8,128)(2,1)S(1)}, u32[]{:S(2)}, u32[]{:S(2)}) collective-permute-start(bf16[512,128]{1,0:T(8,128)(2,1)S(1)} %constant_dynamic-update-slice_fusion), channel_id=1, source_target_pairs={{0,6},{1,7},{2,0},{3,1},{4,2},{5,3},{6,4},{7,5},{8,14},{9,15},{10,... | collective-permute-start | bytes 393224 | tf_op jit(solution)/shard_map/ppermute | solution.py:67
  43.0 51.5 %collective-permute-start.6 = (bf16[512,128]{1,0:T(8,128)(2,1)S(1)}, bf16[512,128]{1,0:T(8,128)(2,1)S(1)}, u32[]{:S(2)}, u32[]{:S(2)}) collective-permute-start(bf16[512,128]{1,0:T(8,128)(2,1)S(1)} %constant_dynamic-update-slice_fusion), channel_id=1, source_target_pairs={{0,7},{1,0},{2,1},{3,2},{4,3},{5,4},{6,5},{7,6},{8,15},{9,8},{10,9... | collective-permute-start | bytes 393224 | tf_op jit(solution)/shard_map/ppermute | solution.py:67
  78.8 1.9 copy-start.1
  88.9 20.6 %all-to-all-start.1 = ((bf16[8,256,128]{1,2,0:T(8,128)(2,1)}), bf16[8,256,128]{1,2,0:T(8,128)(2,1)}, u32[]{:S(2)}, u32[]{:S(2)}) async-start(bf16[8,256,128]{1,2,0:T(8,128)(2,1)} %broadcast_in_dim.7), calls=%async_computation.1 | async-start | bytes 1048576 | tf_op jit(solution)/shard_map/all_to_all | solution.py:16
  109.4 2.6 %copy-start.2 = (f32[1,256,8,128]{3,2,1,0:T(8,128)S(1)}, f32[1,256,8,128]{3,2,1,0:T(8,128)}, u32[]{:S(2)}) copy-start(f32[1,256,8,128]{3,2,1,0:T(8,128)} %get-tuple-element.10) | copy-start | bytes 3145732
  115.7 25.7 %all-to-all-start.2 = ((f32[32,8,1024]{2,1,0:T(8,128)}), f32[32,8,1024]{2,1,0:T(8,128)}, u32[]{:S(2)}, u32[]{:S(2)}) async-start(f32[32,8,1024]{2,1,0:T(8,128)} %fusion.11), calls=%async_computation.2 | async-start | bytes 2097152 | tf_op jit(solution)/shard_map/all_to_all | solution.py:22
  146.6 44.4 %all-to-all-start.3 = ((bf16[32,384,128]{2,1,0:T(8,128)(2,1)}), bf16[32,384,128]{2,1,0:T(8,128)(2,1)}, u32[]{:S(2)}, u32[]{:S(2)}) async-start(bf16[32,384,128]{2,1,0:T(8,128)(2,1)} %pad_maximum_fusion), calls=%async_computation.3 | async-start | bytes 6291456 | tf_op jit(solution)/shard_map/all_to_all | solution.py:119
Sparse Core Ops, SparseCore 0:
  10.8 63.6 all-gather.1

commit v6 on v4

--- a/solution.py
+++ b/solution.py
@@ -109,17 +109,19 @@
         "trcij,rif->tcjf", dense, g_rows, preferred_element_type=jnp.float32
     ).reshape(nodes, feat_dev)
     term_pieces = column_terms.astype(jnp.bfloat16).reshape(row_count, node_rows, feat_dev)
-    outgoing = jnp.concatenate(
-        [term_pieces, jnp.broadcast_to(sum_pair[None], (row_count,) + sum_pair.shape)], axis=1
+    room = jnp.zeros((row_count,) + sum_pair.shape, term_pieces.dtype)
+    outgoing = jnp.concatenate([term_pieces, room], axis=1)
+    outgoing, own_grad = lax.optimization_barrier((outgoing, own_grad))
+    outgoing = lax.dynamic_update_slice(
+        outgoing, jnp.broadcast_to(sum_pair[None], room.shape), (0, node_rows, 0)
     )
-    outgoing, own_grad = lax.optimization_barrier((outgoing, own_grad))
     incoming = lax.all_to_all(outgoing, "row", 0, 0, tiled=True)
     summed_cols = incoming[:, :node_rows].astype(jnp.float32).sum(0)
     got_high = incoming[:, node_rows : node_rows + sum_lanes].astype(jnp.float32)
     got_low = incoming[:, node_rows + sum_lanes :].astype(jnp.float32)
-    both_all = (got_high + got_low).reshape(both.shape)
-    weight_sum = both_all[:feat_dev]
-    root_sum = both_all[feat_dev:]
+    half = row_count // 2
+    weight_sum = (got_high[:half] + got_low[:half]).reshape(feat_dev, -1)
+    root_sum = (got_high[half:] + got_low[half:]).reshape(feat_dev, -1)
     feature_grad = summed_cols + own_grad
     return (activations, feature_grad, weight_sum, root_sum)
 

time: 196 us -> 193 us (0.985)
  other arithmetic: 16.5 us -> 13.2 us
  local copies, waits for them, and re-layouts: 21 us -> 24.1 us
    concatenate x1 -> x0, other arithmetic: 3.54 us -> none  [per_device(): jnp.concatenate([term_pieces, jnp.broadcast_to(sum_pair[None], (row_count...]
    concatenate x0 -> x1, local copies, waits for them, and re-layouts: none -> 2.12 us  [per_device(): outgoing = jnp.concatenate([term_pieces, room], axis=1)]
  transfers between devices with their start and end apart: 6 -> 6, of which waited for: 4 -> 4; matrix products, arithmetic and copies ran while one was open for 17% -> 18% of each run, Pallas kernels for 0% -> 0%
where the time goes in v6:
time: 193 us; the launch traced here: 192 us
  waiting for transfers between devices  95 us (49%)
  starting transfers between devices  29.2 us (15%)
  local copies, waits for them, and re-layouts  24.1 us (12%)
  matrix products  16 us (8%)
  between operations  15 us (8%)
  other arithmetic  13.2 us (7%)
    all_to_all x1, waiting for transfers between devices, per_device(): incoming = lax.all_to_all(outgoing, 'row', 0, 0, tiled=True)  38.2 us
    all_gather x1, waiting for transfers between devices, per_device(): lax.all_gather(packed, 'col', axis=0, tiled=True)  28.7 us
    all_gather x1, waiting for transfers between devices, per_device(): lax.all_gather(own_pair, 'col', axis=0, tiled=True)  24.8 us
    all_to_all x2, starting transfers between devices, gather_rows(): got = lax.all_to_all(spread, axis_name, 0, 0, tiled=True)  12.9 us
    all_to_all x1, starting transfers between devices, reduce_rows(): got = lax.all_to_all(pieces, axis_name, 0, 0, tiled=True)  11.7 us
    dot_general x1, local copies, waits for them, and re-layouts, per_device(): jnp.einsum('trcij,rif->tcjf', dense, g_rows, preferred_element_type=jnp.f...  6.62 us
    all_to_all x1, starting transfers between devices, per_device(): incoming = lax.all_to_all(outgoing, 'row', 0, 0, tiled=True)  4.61 us
    dot_general x1, matrix products, per_device(): jnp.einsum('trcij,tcjf->rif', dense, x_tiles, preferred_element_type=jnp....  4.11 us
  transfers between devices with their start and end apart: 6, of which 4 were waited for; matrix products, arithmetic and copies ran while one was open for 18% of the time, Pallas kernels for 0%

profile of v6, /device:TPU:1, one launch (start us, length us, event | category | flops | bytes accessed | tf_op | source)
XLA Modules:
  0.0 192.5 jit_solution(17929466812775012333)
XLA Ops:
  8.8 1.1 bitcast_multiply_fusion.1
  10.7 2.6 %broadcast_in_dim.6 = bf16[32,256,128]{2,1,0:T(8,128)(2,1)} broadcast(bf16[256,128]{1,0:T(8,128)(2,1)} %param.7), dimensions={1,2} | broadcast | bytes 2162688 | tf_op jit(solution)/shard_map/broadcast_in_dim | solution.py:15
  13.3 8.8 %all-to-all-start = ((bf16[32,256,128]{2,1,0:T(8,128)(2,1)}), bf16[32,256,128]{2,1,0:T(8,128)(2,1)}, u32[]{:S(2)}, u32[]{:S(2)}) async-start(bf16[32,256,128]{2,1,0:T(8,128)(2,1)} %broadcast_in_dim.6), calls=%async_computation | async-start | bytes 4194304 | tf_op jit(solution)/shard_map/all_to_all | solution.py:16
  22.8 28.7 %all-gather.3.cloned.1.call-done = bf16[8320,128]{1,0:T(8,128)(2,1)} async-done(((bf16[1040,128]{1,0:T(8,128)(2,1)}), bf16[8320,128]{1,0:T(8,128)(2,1)}) %all-gather.3.cloned.1.call-update) | async-done | bytes 2129936 | tf_op jit(solution)/shard_map/all_gather | solution.py:41
  51.6 1.7 slice.47
  54.0 1.9 convolution_convert_fusion
  55.9 1.9 %copy-done.1 = bf16[8,16,128,128]{3,1,2,0:T(8,128)(2,1)} copy-done((bf16[8,16,128,128]{3,1,2,0:T(8,128)(2,1)}, bf16[8,16,128,128]{3,1,2,0:T(8,128)(2,1)S(1)}, u32[]{:S(2)}) %copy-start.1) | copy-done | bytes 4194328
  57.8 3.1 %copy.15 = bf16[2,128,8,128,8]{3,1,0,4,2:T(8,128)(2,1)} copy(bf16[2,128,8,128,8]{3,2,0,1,4:T(8,128)(2,1)S(1)} %bitcast.72) | data formatting | bytes 8388608 | tf_op jit(solution)/shard_map/trcij,tcjf->rif/dot_general | solution.py:60
  60.9 4.1 %fusion.7 = bf16[256,128]{1,0:T(8,128)(2,1)S(1)} fusion(bf16[256,8,128,8]{2,0,3,1:T(8,128)(2,1)} %bitcast.77, bf16[8,8,128,128]{3,2,1,0:T(8,128)(2,1)} %bitcast.12), kind=kOutput, calls=%fused_computation.11 | convolution fusion | flops 536903680 | bytes 6356992 | tf_op jit(solution)/shard_map/trcij,tcjf->rif/dot_general | solution.py:60
  65.2 0.8 broadcast_in_dim.7
  66.0 4.1 %all-to-all-start.1 = ((bf16[8,256,128]{1,2,0:T(8,128)(2,1)}), bf16[8,256,128]{1,2,0:T(8,128)(2,1)S(1)}, u32[]{:S(2)}, u32[]{:S(2)}) async-start(bf16[8,256,128]{1,2,0:T(8,128)(2,1)} %broadcast_in_dim.7), calls=%async_computation.1 | async-start | bytes 1048576 | tf_op jit(solution)/shard_map/all_to_all | solution.py:16
  70.1 24.8 %all-gather.5.cloned.1.call-done = bf16[4096,128]{1,0:T(8,128)(2,1)} async-done(((bf16[512,128]{1,0:T(8,128)(2,1)}), bf16[4096,128]{1,0:T(8,128)(2,1)}) %all-gather.5.cloned.1.call-update) | async-done | bytes 1048592 | tf_op jit(solution)/shard_map/all_gather | solution.py:66
  94.9 1.9 copy.40
  96.8 1.1 slice_convert_fusion.2
  97.9 2.4 %fusion.25 = f32[256,1024]{1,0:T(8,128)S(1)} fusion(bf16[256,1024]{0,1:T(8,128)(2,1)S(1)} %bitcast.79, bf16[1024,1024]{1,0:T(8,128)(2,1)} %param.9), kind=kOutput, calls=%fused_computation.47 | convolution fusion | flops 536870912 | bytes 3670016 | tf_op jit(solution)/shard_map/dot_general | solution.py:72
  100.3 2.1 %fusion.10 = (bf16[256,1024]{1,0:T(8,128)(2,1)S(1)}, f32[256,1024]{1,0:T(8,128)}) fusion(f32[32,8,8,128]{3,2,1,0:T(8,128)S(1)} %bitcast.83, f32[256,1024]{1,0:T(8,128)S(1)} %fusion.25, bf16[1024,1024]{1,0:T(8,128)(2,1)S(1)} %copy-done, bf16[32,8,8,128]{3,2,1,0:T(8,128)(2,1)S(1)} %bitcast.84), kind=kOutput, calls=%fused_computation.13 | convolution fusion | flops 539492352 | bytes 6291456 | tf_op jit(solution)/shard_map/dot_general | solution.py:72
  102.9 1.1 fusion.11
  104.0 11.7 %all-to-all-start.2 = ((f32[32,8,1024]{2,1,0:T(8,128)}), f32[32,8,1024]{2,1,0:T(8,128)}, u32[]{:S(2)}, u32[]{:S(2)}) async-start(f32[32,8,1024]{2,1,0:T(8,128)} %fusion.11), calls=%async_computation.2 | async-start | bytes 2097152 | tf_op jit(solution)/shard_map/all_to_all | solution.py:22
  115.7 6.6 %copy.19 = bf16[8,8,128,128,2]{3,2,1,0,4:T(8,128)(2,1)} copy(bf16[8,8,128,128,2]{2,1,4,3,0:T(8,128)(2,1)} %bitcast.73) | data formatting | bytes 8388608 | tf_op jit(solution)/shard_map/trcij,rif->tcjf/dot_general | solution.py:108
  122.3 1.2 convolution_convert_fusion.1
  123.6 3.4 %fusion = bf16[8192,128]{1,0:T(8,128)(2,1)S(1)} fusion(bf16[8192,128,2]{1,0,2:T(8,128)(2,1)} %bitcast.74, bf16[2,128,128]{2,1,0:T(8,128)(2,1)S(1)} %bitcast.85), kind=kOutput, calls=%fused_computation.1 | convolution fusion | flops 537919488 | bytes 6356992 | tf_op jit(solution)/shard_map/trcij,rif->tcjf/dot_general | solution.py:108
  127.0 2.1 %concatenate.17 = bf16[32,384,128]{2,1,0:T(8,128)(2,1)} pad(bf16[32,256,128]{2,1,0:T(8,128)(2,1)S(1)} %bitcast.75, bf16[]{:T(256)} %constant.9.clone.1), padding=0_0x0_128x0_0 | pad | bytes 5242882 | tf_op jit(solution)/shard_map/concatenate | solution.py:113
  129.5 3.2 %all-to-all-done.2 = f32[32,8,1024]{2,1,0:T(8,128)} async-done(((f32[32,8,1024]{2,1,0:T(8,128)}), f32[32,8,1024]{2,1,0:T(8,128)}, u32[]{:S(2)}, u32[]{:S(2)}) %all-to-all-start.2) | async-done | bytes 1048608 | tf_op jit(solution)/shard_map/all_to_all | solution.py:22
  132.7 1.3 reduce_sum.20
  134.0 1.2 broadcast_dynamic-update-slice_fusion
  135.2 4.6 %all-to-all-start.3 = ((bf16[32,384,128]{2,1,0:T(8,128)(2,1)}), bf16[32,384,128]{2,1,0:T(8,128)(2,1)}, u32[]{:S(2)}, u32[]{:S(2)}) async-start(bf16[32,384,128]{2,1,0:T(8,128)(2,1)} %broadcast_dynamic-update-slice_fusion), calls=%async_computation.3 | async-start | bytes 6291456 | tf_op jit(solution)/shard_map/all_to_all | solution.py:118
  139.8 1.6 multiply_convert_fusion
  141.4 38.2 %all-to-all-done.3 = bf16[32,384,128]{2,1,0:T(8,128)(2,1)} async-done(((bf16[32,384,128]{2,1,0:T(8,128)(2,1)}), bf16[32,384,128]{2,1,0:T(8,128)(2,1)}, u32[]{:S(2)}, u32[]{:S(2)}) %all-to-all-start.3) | async-done | bytes 3145760 | tf_op jit(solution)/shard_map/all_to_all | solution.py:118
  179.7 1.4 slice_convert_fusion.1
  181.3 0.9 reshape.91
  182.2 0.9 reshape.92
  183.1 1.9 convert_reduce_fusion
  (30 shorter events, 4.8 us)
Async XLA Ops:
  7.2 93.1 %copy-start = (bf16[1024,1024]{1,0:T(8,128)(2,1)S(1)}, bf16[1024,1024]{1,0:T(8,128)(2,1)}, u32[]{:S(2)}) copy-start(bf16[1024,1024]{1,0:T(8,128)(2,1)} %param.10) | copy-start | bytes 6291460
  7.2 44.4 %all-gather.3.cloned.1.call-start = ((), (), s32[]{:S(2)}) async-start(), calls=%async_computation.4 | async-start | bytes 2396160 | tf_op jit(solution)/shard_map/all_gather | solution.py:41
  13.3 8.8 %copy-start.3 = (bf16[256,128]{1,0:T(8,128)(2,1)S(1)}, bf16[256,128]{1,0:T(8,128)(2,1)}, u32[]{:S(2)}) copy-start(bf16[256,128]{1,0:T(8,128)(2,1)} %param.7) | copy-start | bytes 196612
  13.3 8.8 %copy-start.4 = (bf16[256,128]{1,0:T(8,128)(2,1)S(1)}, bf16[256,128]{1,0:T(8,128)(2,1)}, u32[]{:S(2)}) copy-start(bf16[256,128]{1,0:T(8,128)(2,1)} %param.8) | copy-start | bytes 196612
  13.3 47.6 %all-to-all-start = ((bf16[32,256,128]{2,1,0:T(8,128)(2,1)}), bf16[32,256,128]{2,1,0:T(8,128)(2,1)}, u32[]{:S(2)}, u32[]{:S(2)}) async-start(bf16[32,256,128]{2,1,0:T(8,128)(2,1)} %broadcast_in_dim.6), calls=%async_computation | async-start | bytes 4194304 | tf_op jit(solution)/shard_map/all_to_all | solution.py:16
  22.1 72.8 %all-gather.5.cloned.1.call-start = ((), (), s32[]{:S(2)}) async-start(), calls=%async_computation.5 | async-start | bytes 1179648 | tf_op jit(solution)/shard_map/all_gather | solution.py:66
  55.9 2.0 %copy-start.1 = (bf16[8,16,128,128]{3,1,2,0:T(8,128)(2,1)}, bf16[8,16,128,128]{3,1,2,0:T(8,128)(2,1)S(1)}, u32[]{:S(2)}) copy-start(bf16[8,16,128,128]{3,1,2,0:T(8,128)(2,1)S(1)} %convolution_convert_fusion) | copy-start | bytes 12582916
  66.0 31.9 %all-to-all-start.1 = ((bf16[8,256,128]{1,2,0:T(8,128)(2,1)}), bf16[8,256,128]{1,2,0:T(8,128)(2,1)S(1)}, u32[]{:S(2)}, u32[]{:S(2)}) async-start(bf16[8,256,128]{1,2,0:T(8,128)(2,1)} %broadcast_in_dim.7), calls=%async_computation.1 | async-start | bytes 1048576 | tf_op jit(solution)/shard_map/all_to_all | solution.py:16
  97.9 2.4 %copy-start.2 = (f32[1,256,8,128]{3,2,1,0:T(8,128)S(1)}, f32[1,256,8,128]{3,2,1,0:T(8,128)}, u32[]{:S(2)}) copy-start(f32[1,256,8,128]{3,2,1,0:T(8,128)} %get-tuple-element.12) | copy-start | bytes 3145732
  104.0 28.6 %all-to-all-start.2 = ((f32[32,8,1024]{2,1,0:T(8,128)}), f32[32,8,1024]{2,1,0:T(8,128)}, u32[]{:S(2)}, u32[]{:S(2)}) async-start(f32[32,8,1024]{2,1,0:T(8,128)} %fusion.11), calls=%async_computation.2 | async-start | bytes 2097152 | tf_op jit(solution)/shard_map/all_to_all | solution.py:22
  135.2 44.5 %all-to-all-start.3 = ((bf16[32,384,128]{2,1,0:T(8,128)(2,1)}), bf16[32,384,128]{2,1,0:T(8,128)(2,1)}, u32[]{:S(2)}, u32[]{:S(2)}) async-start(bf16[32,384,128]{2,1,0:T(8,128)(2,1)} %broadcast_dynamic-update-slice_fusion), calls=%async_computation.3 | async-start | bytes 6291456 | tf_op jit(solution)/shard_map/all_to_all | solution.py:118
Sparse Core Ops, SparseCore 0:
  10.8 40.7 all-gather.2
  53.9 40.9 all-gather.4

commit v7 on v6

--- a/solution.py
+++ b/solution.py
@@ -37,9 +37,9 @@
     pos_row = lax.dynamic_update_slice(
         pos_row, positions[0, 0].astype(values.dtype).reshape(1, slots), (0, 0)
     )
-    packed = jnp.concatenate([own_vals, pos_row], axis=0)
+    packed = jnp.concatenate([own_vals, pos_row, features, grad_out], axis=0)
     all_packed = lax.all_gather(packed, "col", axis=0, tiled=True).reshape(
-        col_count, slots * block_edge + 16, block_edge
+        col_count, packed.shape[0], block_edge
     )
     tile_vals = all_packed[:, : slots * block_edge].reshape(
         col_count, slots, block_edge, block_edge
@@ -62,8 +62,7 @@
 
     agg_parts = gather_rows(aggregated, "col", col_count).reshape(col_count, node_rows, feat_dev)
     agg_full = jnp.moveaxis(agg_parts, 0, 1).reshape(node_rows, col_count * feat_dev)
-    own_pair = jnp.concatenate([features, grad_out], axis=0)
-    pair_parts = lax.all_gather(own_pair, "col", axis=0, tiled=True).reshape(
+    pair_parts = all_packed[:, slots * block_edge + 16 :].reshape(
         col_count, 2, node_rows, feat_dev
     )
     pair_full = jnp.moveaxis(pair_parts, 0, 2).reshape(2, node_rows, col_count * feat_dev)

time: 193 us -> 188 us (0.974)
  starting transfers between devices: 29.2 us -> 25.6 us
    all_gather x1 -> x0, waiting for transfers between devices: 24.8 us -> none  [per_device(): lax.all_gather(own_pair, 'col', axis=0, tiled=True)]
    all_to_all x2, waiting for transfers between devices: 0.01 us -> 14 us  [gather_rows(): got = lax.all_to_all(spread, axis_name, 0, 0, tiled=True)]
    all_gather x1, waiting for transfers between devices: 28.7 us -> 37.7 us  [per_device(): lax.all_gather(packed, 'col', axis=0, tiled=True)]
    all_to_all x1, starting transfers between devices: 11.7 us -> 8.29 us  [reduce_rows(): got = lax.all_to_all(pieces, axis_name, 0, 0, tiled=True)]
  transfers between devices with their start and end apart: 6 -> 5, of which waited for: 4 -> 4; matrix products, arithmetic and copies ran while one was open for 18% -> 15% of each run, Pallas kernels for 0% -> 0%
where the time goes in v7:
time: 188 us; the launch traced here: 187 us
  waiting for transfers between devices  93.2 us (50%)
  starting transfers between devices  25.6 us (14%)
  local copies, waits for them, and re-layouts  24.1 us (13%)
  matrix products  16 us (9%)
  between operations  14.9 us (8%)
  other arithmetic  13.6 us (7%)
    all_to_all x1, waiting for transfers between devices, per_device(): incoming = lax.all_to_all(outgoing, 'row', 0, 0, tiled=True)  38.2 us
    all_gather x1, waiting for transfers between devices, per_device(): lax.all_gather(packed, 'col', axis=0, tiled=True)  37.7 us
    all_to_all x2, waiting for transfers between devices, gather_rows(): got = lax.all_to_all(spread, axis_name, 0, 0, tiled=True)  14 us
    all_to_all x2, starting transfers between devices, gather_rows(): got = lax.all_to_all(spread, axis_name, 0, 0, tiled=True)  12.6 us
    all_to_all x1, starting transfers between devices, reduce_rows(): got = lax.all_to_all(pieces, axis_name, 0, 0, tiled=True)  8.29 us
    dot_general x1, local copies, waits for them, and re-layouts, per_device(): jnp.einsum('trcij,rif->tcjf', dense, g_rows, preferred_element_type=jnp.f...  6.61 us
    all_to_all x1, starting transfers between devices, per_device(): incoming = lax.all_to_all(outgoing, 'row', 0, 0, tiled=True)  4.6 us
    dot_general x1, matrix products, per_device(): jnp.einsum('trcij,tcjf->rif', dense, x_tiles, preferred_element_type=jnp....  4.11 us
  transfers between devices with their start and end apart: 5, of which 4 were waited for; matrix products, arithmetic and copies ran while one was open for 15% of the time, Pallas kernels for 0%

profile of v7, /device:TPU:1, one launch (start us, length us, event | category | flops | bytes accessed | tf_op | source)
XLA Modules:
  0.0 187.4 jit_solution(9861692391292863549)
XLA Ops:
  8.8 1.1 bitcast_multiply_fusion.1
  9.9 1.6 fusion.18
  11.6 2.6 %broadcast_in_dim.6 = bf16[32,256,128]{2,1,0:T(8,128)(2,1)} broadcast(bf16[256,128]{1,0:T(8,128)(2,1)} %param.7), dimensions={1,2} | broadcast | bytes 2162688 | tf_op jit(solution)/shard_map/broadcast_in_dim | solution.py:15
  14.2 8.6 %all-to-all-start = ((bf16[32,256,128]{2,1,0:T(8,128)(2,1)}), bf16[32,256,128]{2,1,0:T(8,128)(2,1)}, u32[]{:S(2)}, u32[]{:S(2)}) async-start(bf16[32,256,128]{2,1,0:T(8,128)(2,1)} %broadcast_in_dim.6), calls=%async_computation | async-start | bytes 4194304 | tf_op jit(solution)/shard_map/all_to_all | solution.py:16
  22.8 37.7 %all-gather.2.cloned.1.call-done = bf16[12416,128]{1,0:T(8,128)(2,1)} async-done(((bf16[1552,128]{1,0:T(8,128)(2,1)}), bf16[12416,128]{1,0:T(8,128)(2,1)}) %all-gather.2.cloned.1.call-update) | async-done | bytes 3178512 | tf_op jit(solution)/shard_map/all_gather | solution.py:41
  60.6 1.7 slice.51
  63.0 1.9 convolution_convert_fusion
  64.9 1.9 %copy-done.1 = bf16[8,16,128,128]{3,1,2,0:T(8,128)(2,1)} copy-done((bf16[8,16,128,128]{3,1,2,0:T(8,128)(2,1)}, bf16[8,16,128,128]{3,1,2,0:T(8,128)(2,1)S(1)}, u32[]{:S(2)}) %copy-start.1) | copy-done | bytes 4194328
  66.8 3.1 %copy.14 = bf16[2,128,8,128,8]{3,1,0,4,2:T(8,128)(2,1)} copy(bf16[2,128,8,128,8]{3,2,0,1,4:T(8,128)(2,1)S(1)} %bitcast.72) | data formatting | bytes 8388608 | tf_op jit(solution)/shard_map/trcij,tcjf->rif/dot_general | solution.py:60
  69.9 4.1 %fusion.7 = bf16[256,128]{1,0:T(8,128)(2,1)S(1)} fusion(bf16[256,8,128,8]{2,0,3,1:T(8,128)(2,1)} %bitcast.77, bf16[8,8,128,128]{3,2,1,0:T(8,128)(2,1)} %bitcast.12), kind=kOutput, calls=%fused_computation.13 | convolution fusion | flops 536903680 | bytes 6356992 | tf_op jit(solution)/shard_map/trcij,tcjf->rif/dot_general | solution.py:60
  75.0 4.0 %all-to-all-start.1 = ((bf16[8,256,128]{1,2,0:T(8,128)(2,1)}), bf16[8,256,128]{1,2,0:T(8,128)(2,1)S(1)}, u32[]{:S(2)}, u32[]{:S(2)}) async-start(bf16[8,256,128]{1,2,0:T(8,128)(2,1)} %broadcast_in_dim.7), calls=%async_computation.1 | async-start | bytes 1048576 | tf_op jit(solution)/shard_map/all_to_all | solution.py:16
  79.0 1.3 slice.52
  81.0 1.1 slice_convert_fusion.2
  82.1 14.0 %all-to-all-done.1 = bf16[8,256,128]{1,2,0:T(8,128)(2,1)S(1)} async-done(((bf16[8,256,128]{1,2,0:T(8,128)(2,1)}), bf16[8,256,128]{1,2,0:T(8,128)(2,1)S(1)}, u32[]{:S(2)}, u32[]{:S(2)}) %all-to-all-start.1) | async-done | bytes 524320 | tf_op jit(solution)/shard_map/all_to_all | solution.py:16
  96.1 2.4 %fusion.28 = f32[256,1024]{1,0:T(8,128)S(1)} fusion(bf16[256,1024]{0,1:T(8,128)(2,1)S(1)} %bitcast.83, bf16[1024,1024]{1,0:T(8,128)(2,1)} %param.9), kind=kOutput, calls=%fused_computation.50 | convolution fusion | flops 536870912 | bytes 3670016 | tf_op jit(solution)/shard_map/dot_general | solution.py:71
  98.5 2.1 %fusion.10 = (bf16[256,1024]{1,0:T(8,128)(2,1)S(1)}, f32[256,1024]{1,0:T(8,128)}) fusion(f32[32,8,8,128]{3,2,1,0:T(8,128)S(1)} %bitcast.84, f32[256,1024]{1,0:T(8,128)S(1)} %fusion.28, bf16[1024,1024]{1,0:T(8,128)(2,1)S(1)} %copy-done, bf16[32,8,8,128]{3,2,1,0:T(8,128)(2,1)S(1)} %bitcast.85), kind=kOutput, calls=%fused_computation.15 | convolution fusion | flops 539492352 | bytes 6291456 | tf_op jit(solution)/shard_map/dot_general | solution.py:71
  101.2 1.1 fusion.11
  102.3 8.3 %all-to-all-start.2 = ((f32[32,8,1024]{2,1,0:T(8,128)}), f32[32,8,1024]{2,1,0:T(8,128)}, u32[]{:S(2)}, u32[]{:S(2)}) async-start(f32[32,8,1024]{2,1,0:T(8,128)} %fusion.11), calls=%async_computation.2 | async-start | bytes 2097152 | tf_op jit(solution)/shard_map/all_to_all | solution.py:22
  110.6 6.6 %copy.18 = bf16[8,8,128,128,2]{3,2,1,0,4:T(8,128)(2,1)} copy(bf16[8,8,128,128,2]{2,1,4,3,0:T(8,128)(2,1)} %bitcast.73) | data formatting | bytes 8388608 | tf_op jit(solution)/shard_map/trcij,rif->tcjf/dot_general | solution.py:107
  117.2 1.2 convolution_convert_fusion.1
  118.4 3.4 %fusion = bf16[8192,128]{1,0:T(8,128)(2,1)S(1)} fusion(bf16[8192,128,2]{1,0,2:T(8,128)(2,1)} %bitcast.74, bf16[2,128,128]{2,1,0:T(8,128)(2,1)S(1)} %bitcast.86), kind=kOutput, calls=%fused_computation.1 | convolution fusion | flops 537919488 | bytes 6356992 | tf_op jit(solution)/shard_map/trcij,rif->tcjf/dot_general | solution.py:107
  121.9 2.1 %concatenate.13 = bf16[32,384,128]{2,1,0:T(8,128)(2,1)} pad(bf16[32,256,128]{2,1,0:T(8,128)(2,1)S(1)} %bitcast.75, bf16[]{:T(256)} %constant.9.clone.1), padding=0_0x0_128x0_0 | pad | bytes 5242882 | tf_op jit(solution)/shard_map/concatenate | solution.py:112
  124.3 3.2 %all-to-all-done.2 = f32[32,8,1024]{2,1,0:T(8,128)} async-done(((f32[32,8,1024]{2,1,0:T(8,128)}), f32[32,8,1024]{2,1,0:T(8,128)}, u32[]{:S(2)}, u32[]{:S(2)}) %all-to-all-start.2) | async-done | bytes 1048608 | tf_op jit(solution)/shard_map/all_to_all | solution.py:22
  127.5 1.3 reduce_sum.20
  128.9 1.3 broadcast_dynamic-update-slice_fusion
  130.1 4.6 %all-to-all-start.3 = ((bf16[32,384,128]{2,1,0:T(8,128)(2,1)}), bf16[32,384,128]{2,1,0:T(8,128)(2,1)}, u32[]{:S(2)}, u32[]{:S(2)}) async-start(bf16[32,384,128]{2,1,0:T(8,128)(2,1)} %broadcast_dynamic-update-slice_fusion), calls=%async_computation.3 | async-start | bytes 6291456 | tf_op jit(solution)/shard_map/all_to_all | solution.py:117
  134.8 1.6 multiply_convert_fusion
  136.3 38.2 %all-to-all-done.3 = bf16[32,384,128]{2,1,0:T(8,128)(2,1)} async-done(((bf16[32,384,128]{2,1,0:T(8,128)(2,1)}), bf16[32,384,128]{2,1,0:T(8,128)(2,1)}, u32[]{:S(2)}, u32[]{:S(2)}) %all-to-all-start.3) | async-done | bytes 3145760 | tf_op jit(solution)/shard_map/all_to_all | solution.py:117
  174.6 1.4 slice_convert_fusion.1
  176.2 0.9 reshape.91
  177.1 0.9 reshape.92
  178.0 1.9 %convert_reduce_fusion = f32[256,128]{1,0:T(8,128)S(1)} fusion(bf16[32,384,128]{2,1,0:T(8,128)(2,1)} %all-to-all-done.3), kind=kLoop, calls=%fused_computation.2 | loop fusion | flops 2064384 | bytes 2228224 | tf_op jit(solution)/shard_map/reduce_sum | solution.py:118
  (25 shorter events, 5.0 us)
Async XLA Ops:
  7.2 91.3 %copy-start = (bf16[1024,1024]{1,0:T(8,128)(2,1)S(1)}, bf16[1024,1024]{1,0:T(8,128)(2,1)}, u32[]{:S(2)}) copy-start(bf16[1024,1024]{1,0:T(8,128)(2,1)} %param.10) | copy-start | bytes 6291460
  7.2 53.4 %all-gather.2.cloned.1.call-start = ((), (), s32[]{:S(2)}) async-start(), calls=%async_computation.4 | async-start | bytes 3575808 | tf_op jit(solution)/shard_map/all_gather | solution.py:41
  14.2 55.7 %all-to-all-start = ((bf16[32,256,128]{2,1,0:T(8,128)(2,1)}), bf16[32,256,128]{2,1,0:T(8,128)(2,1)}, u32[]{:S(2)}, u32[]{:S(2)}) async-start(bf16[32,256,128]{2,1,0:T(8,128)(2,1)} %broadcast_in_dim.6), calls=%async_computation | async-start | bytes 4194304 | tf_op jit(solution)/shard_map/all_to_all | solution.py:16
  64.9 1.9 %copy-start.1 = (bf16[8,16,128,128]{3,1,2,0:T(8,128)(2,1)}, bf16[8,16,128,128]{3,1,2,0:T(8,128)(2,1)S(1)}, u32[]{:S(2)}) copy-start(bf16[8,16,128,128]{3,1,2,0:T(8,128)(2,1)S(1)} %convolution_convert_fusion) | copy-start | bytes 12582916
  75.0 21.1 %all-to-all-start.1 = ((bf16[8,256,128]{1,2,0:T(8,128)(2,1)}), bf16[8,256,128]{1,2,0:T(8,128)(2,1)S(1)}, u32[]{:S(2)}, u32[]{:S(2)}) async-start(bf16[8,256,128]{1,2,0:T(8,128)(2,1)} %broadcast_in_dim.7), calls=%async_computation.1 | async-start | bytes 1048576 | tf_op jit(solution)/shard_map/all_to_all | solution.py:16
  96.1 2.4 %copy-start.2 = (f32[1,256,8,128]{3,2,1,0:T(8,128)S(1)}, f32[1,256,8,128]{3,2,1,0:T(8,128)}, u32[]{:S(2)}) copy-start(f32[1,256,8,128]{3,2,1,0:T(8,128)} %get-tuple-element.12) | copy-start | bytes 3145732
  98.5 2.2 %copy-start.3 = (bf16[256,128]{1,0:T(8,128)(2,1)S(1)}, bf16[256,128]{1,0:T(8,128)(2,1)}, u32[]{:S(2)}) copy-start(bf16[256,128]{1,0:T(8,128)(2,1)} %param.7) | copy-start | bytes 196612
  102.3 25.3 %all-to-all-start.2 = ((f32[32,8,1024]{2,1,0:T(8,128)}), f32[32,8,1024]{2,1,0:T(8,128)}, u32[]{:S(2)}, u32[]{:S(2)}) async-start(f32[32,8,1024]{2,1,0:T(8,128)} %fusion.11), calls=%async_computation.2 | async-start | bytes 2097152 | tf_op jit(solution)/shard_map/all_to_all | solution.py:22
  130.1 44.4 %all-to-all-start.3 = ((bf16[32,384,128]{2,1,0:T(8,128)(2,1)}), bf16[32,384,128]{2,1,0:T(8,128)(2,1)}, u32[]{:S(2)}, u32[]{:S(2)}) async-start(bf16[32,384,128]{2,1,0:T(8,128)(2,1)} %broadcast_dynamic-update-slice_fusion), calls=%async_computation.3 | async-start | bytes 6291456 | tf_op jit(solution)/shard_map/all_to_all | solution.py:117
Sparse Core Ops, SparseCore 0:
  11.7 48.8 all-gather.1

commit v8 on v7

--- a/solution.py
+++ b/solution.py
@@ -57,7 +57,19 @@
 
     x_all = gather_rows(features, "row", row_count)
     x_tiles = x_all.reshape(col_count, cb, block_edge, feat_dev)
-    agg_f32 = jnp.einsum("trcij,tcjf->rif", dense, x_tiles, preferred_element_type=jnp.float32)
+    col_hot = (
+        (tile_pos % cb)[:, :, None] == jnp.arange(cb, dtype=jnp.int32)[None, None, :]
+    ).astype(values.dtype)
+    row_hot = (
+        (tile_pos // cb)[:, :, None] == jnp.arange(row_blocks, dtype=jnp.int32)[None, None, :]
+    ).astype(jnp.float32)
+    chosen = jnp.einsum(
+        "tsc,tcjf->tsjf", col_hot, x_tiles, preferred_element_type=jnp.float32
+    ).astype(values.dtype)
+    products = jnp.einsum(
+        "tsij,tsjf->tsif", tile_vals, chosen, preferred_element_type=jnp.float32
+    )
+    agg_f32 = jnp.einsum("tsr,tsif->rif", row_hot, products, precision=lax.Precision.HIGHEST)
     aggregated = agg_f32.reshape(node_rows, feat_dev).astype(jnp.bfloat16)
 
     agg_parts = gather_rows(aggregated, "col", col_count).reshape(col_count, node_rows, feat_dev)

time: 188 us -> 192 us (1.021)
  matrix products: 16 us -> 23.4 us
  local copies, waits for them, and re-layouts: 24.1 us -> 20.6 us
  waiting for transfers between devices: 93.2 us -> 89.9 us
  starting transfers between devices: 25.6 us -> 28.4 us
    dot_general x1 -> x3, matrix products: 4.11 us -> 7.99 us  [the longest x1 4.21 us: per_device(): jnp.einsum('tsr,tsif->rif', row_hot, products, precision=lax.Precision.HI...]
    dot_general x1, matrix products: 1.85 us -> 5.37 us  [per_device(): jnp.einsum('tsp,tsij->tpij', onehot, tile_vals, preferred_element_type=jn...]
    all_to_all x1, waiting for transfers between devices: 3.23 us -> 0.01 us  [reduce_rows(): got = lax.all_to_all(pieces, axis_name, 0, 0, tiled=True)]
    dot_general x1 -> x0, local copies, waits for them, and re-layouts: 3.08 us -> none  [per_device(): jnp.einsum('trcij,tcjf->rif', dense, x_tiles, preferred_element_type=jnp....]
    all_to_all x1, starting transfers between devices: 4.6 us -> 7.44 us  [per_device(): incoming = lax.all_to_all(outgoing, 'row', 0, 0, tiled=True)]
    unnamed x8, local copies, waits for them, and re-layouts: 1.96 us -> 0.02 us
  transfers between devices with their start and end apart: 5 -> 5, of which waited for: 4 -> 3; matrix products, arithmetic and copies ran while one was open for 15% -> 16% of each run, Pallas kernels for 0% -> 0%
where the time goes in v8:
time: 192 us; the launch traced here: 191 us
  waiting for transfers between devices  89.9 us (47%)
  starting transfers between devices  28.4 us (15%)
  matrix products  23.4 us (12%)
  local copies, waits for them, and re-layouts  20.6 us (11%)
  between operations  15 us (8%)
  other arithmetic  13.4 us (7%)
    all_to_all x1, waiting for transfers between devices, per_device(): incoming = lax.all_to_all(outgoing, 'row', 0, 0, tiled=True)  38.2 us
    all_gather x1, waiting for transfers between devices, per_device(): lax.all_gather(packed, 'col', axis=0, tiled=True)  37.6 us
    all_to_all x2, waiting for transfers between devices, gather_rows(): got = lax.all_to_all(spread, axis_name, 0, 0, tiled=True)  14 us
    all_to_all x2, starting transfers between devices, gather_rows(): got = lax.all_to_all(spread, axis_name, 0, 0, tiled=True)  12.6 us
    all_to_all x1, starting transfers between devices, reduce_rows(): got = lax.all_to_all(pieces, axis_name, 0, 0, tiled=True)  8.3 us
    all_to_all x1, starting transfers between devices, per_device(): incoming = lax.all_to_all(outgoing, 'row', 0, 0, tiled=True)  7.44 us
    dot_general x1, local copies, waits for them, and re-layouts, per_device(): jnp.einsum('trcij,rif->tcjf', dense, g_rows, preferred_element_type=jnp.f...  6.61 us
    dot_general x1, matrix products, per_device(): jnp.einsum('tsp,tsij->tpij', onehot, tile_vals, preferred_element_type=jn...  5.37 us
  transfers between devices with their start and end apart: 5, of which 3 were waited for; matrix products, arithmetic and copies ran while one was open for 16% of the time, Pallas kernels for 0%

profile of v8, /device:TPU:1, one launch (start us, length us, event | category | flops | bytes accessed | tf_op | source)
XLA Modules:
  0.0 190.7 jit_solution(17582453802253115533)
XLA Ops:
  8.8 1.1 bitcast_multiply_fusion.1
  9.9 1.6 fusion.21
  11.6 2.7 %broadcast_in_dim.6 = bf16[32,256,128]{2,1,0:T(8,128)(2,1)} broadcast(bf16[256,128]{1,0:T(8,128)(2,1)} %param.7), dimensions={1,2} | broadcast | bytes 2162688 | tf_op jit(solution)/shard_map/broadcast_in_dim | solution.py:15
  14.3 8.6 %all-to-all-start = ((bf16[32,256,128]{2,1,0:T(8,128)(2,1)}), bf16[32,256,128]{2,1,0:T(8,128)(2,1)}, u32[]{:S(2)}, u32[]{:S(2)}) async-start(bf16[32,256,128]{2,1,0:T(8,128)(2,1)} %broadcast_in_dim.6), calls=%async_computation | async-start | bytes 4194304 | tf_op jit(solution)/shard_map/all_to_all | solution.py:16
  22.9 37.6 %all-gather.2.cloned.1.call-done = bf16[12416,128]{1,0:T(8,128)(2,1)} async-done(((bf16[1552,128]{1,0:T(8,128)(2,1)}), bf16[12416,128]{1,0:T(8,128)(2,1)}) %all-gather.2.cloned.1.call-update) | async-done | bytes 3178512 | tf_op jit(solution)/shard_map/all_gather | solution.py:41
  60.6 3.1 %slice.51 = bf16[8,1024,128]{2,1,0:T(8,128)(2,1)} slice(bf16[8,1552,128]{2,1,0:T(8,128)(2,1)} %bitcast.84), slice={[0:8], [0:1024], [0:128]} | slice | bytes 4194304 | tf_op jit(solution)/shard_map/slice | solution.py:44
  63.6 0.7 slice_convert_fusion.3
  64.5 3.1 %fusion.4 = bf16[8,8,128,128]{3,1,2,0:T(8,128)(2,1)S(1)} fusion(bf16[8,8,128,128]{3,2,1,0:T(8,128)(2,1)} %bitcast.10, s32[8,8]{1,0:T(8,128)S(1)} %get-tuple-element.17), kind=kOutput, calls=%fused_computation.8 | convolution fusion | flops 16777728 | bytes 4194560 | tf_op jit(solution)/shard_map/tsc,tcjf->tsjf/dot_general | solution.py:66
  68.3 4.2 %fusion.10 = bf16[2,128,128]{2,0,1:T(2,128)(2,1)S(1)} fusion(f32[8,8,128,128]{3,2,1,0:T(8,128)S(1)} %fusion.3, s32[8,8]{0,1:T(8,128)S(1)} %copy.13), kind=kOutput, calls=%fused_computation.16 | convolution fusion | flops 25198720 | bytes 4260096 | tf_op jit(solution)/shard_map/tsr,tsif->rif/dot_general | solution.py:72
  72.6 0.8 broadcast_in_dim.7
  73.4 4.0 %all-to-all-start.1 = ((bf16[8,256,128]{1,2,0:T(8,128)(2,1)}), bf16[8,256,128]{1,2,0:T(8,128)(2,1)S(1)}, u32[]{:S(2)}, u32[]{:S(2)}) async-start(bf16[8,256,128]{1,2,0:T(8,128)(2,1)} %broadcast_in_dim.7), calls=%async_computation.1 | async-start | bytes 1048576 | tf_op jit(solution)/shard_map/all_to_all | solution.py:16
  77.5 1.3 slice.52
  79.4 1.1 slice_convert_fusion.2
  80.5 14.0 %all-to-all-done.1 = bf16[8,256,128]{1,2,0:T(8,128)(2,1)S(1)} async-done(((bf16[8,256,128]{1,2,0:T(8,128)(2,1)}), bf16[8,256,128]{1,2,0:T(8,128)(2,1)S(1)}, u32[]{:S(2)}, u32[]{:S(2)}) %all-to-all-start.1) | async-done | bytes 524320 | tf_op jit(solution)/shard_map/all_to_all | solution.py:16
  94.5 2.4 %fusion.40 = f32[256,1024]{1,0:T(8,128)S(1)} fusion(bf16[256,1024]{0,1:T(8,128)(2,1)S(1)} %bitcast.87, bf16[1024,1024]{1,0:T(8,128)(2,1)} %param.9), kind=kOutput, calls=%fused_computation.69 | convolution fusion | flops 536870912 | bytes 3670016 | tf_op jit(solution)/shard_map/dot_general | solution.py:83
  97.0 2.1 %fusion.13 = (bf16[256,1024]{1,0:T(8,128)(2,1)S(1)}, f32[256,1024]{1,0:T(8,128)}) fusion(f32[32,8,8,128]{3,2,1,0:T(8,128)S(1)} %bitcast.88, f32[256,1024]{1,0:T(8,128)S(1)} %fusion.40, bf16[1024,1024]{1,0:T(8,128)(2,1)S(1)} %copy-done, bf16[32,8,8,128]{3,2,1,0:T(8,128)(2,1)S(1)} %bitcast.91), kind=kOutput, calls=%fused_computation.19 | convolution fusion | flops 539492352 | bytes 6291456 | tf_op jit(solution)/shard_map/dot_general | solution.py:83
  99.6 1.1 fusion.14
  100.7 8.3 %all-to-all-start.2 = ((f32[32,8,1024]{2,1,0:T(8,128)}), f32[32,8,1024]{2,1,0:T(8,128)}, u32[]{:S(2)}, u32[]{:S(2)}) async-start(f32[32,8,1024]{2,1,0:T(8,128)} %fusion.14), calls=%async_computation.2 | async-start | bytes 2097152 | tf_op jit(solution)/shard_map/all_to_all | solution.py:22
  109.0 5.4 %convert_bitcast_fusion = bf16[8,8,128,128,2]{2,1,4,3,0:T(8,128)(2,1)} fusion(bf16[8,8,128,128]{3,2,1,0:T(8,128)(2,1)} %bitcast.79, s32[8,8]{1,0:T(8,128)S(1)} %bitcast.94), kind=kOutput, calls=%fused_computation.6 | convolution fusion | flops 35652608 | bytes 6291712 | tf_op jit(solution)/shard_map/tsp,tsij->tpij/dot_general | solution.py:53
  114.4 6.6 %copy.18 = bf16[8,8,128,128,2]{3,2,1,0,4:T(8,128)(2,1)} copy(bf16[8,8,128,128,2]{2,1,4,3,0:T(8,128)(2,1)} %convert_bitcast_fusion) | data formatting | bytes 8388608 | tf_op jit(solution)/shard_map/trcij,rif->tcjf/dot_general | solution.py:119
  121.0 1.2 convolution_convert_fusion
  122.2 3.4 %fusion = bf16[8192,128]{1,0:T(8,128)(2,1)S(1)} fusion(bf16[8192,128,2]{1,0,2:T(8,128)(2,1)} %bitcast.78, bf16[2,128,128]{2,1,0:T(8,128)(2,1)S(1)} %bitcast.92), kind=kOutput, calls=%fused_computation.1 | convolution fusion | flops 537919488 | bytes 6356992 | tf_op jit(solution)/shard_map/trcij,rif->tcjf/dot_general | solution.py:119
  125.7 2.1 %concatenate.13 = bf16[32,384,128]{2,1,0:T(8,128)(2,1)} pad(bf16[32,256,128]{2,1,0:T(8,128)(2,1)S(1)} %bitcast.81, bf16[]{:T(256)} %constant.36.clone.1), padding=0_0x0_128x0_0 | pad | bytes 5242882 | tf_op jit(solution)/shard_map/concatenate | solution.py:124
  128.1 1.3 reduce_sum.20
  129.5 1.2 broadcast_dynamic-update-slice_fusion
  130.7 7.4 %all-to-all-start.3 = ((bf16[32,384,128]{2,1,0:T(8,128)(2,1)}), bf16[32,384,128]{2,1,0:T(8,128)(2,1)}, u32[]{:S(2)}, u32[]{:S(2)}) async-start(bf16[32,384,128]{2,1,0:T(8,128)(2,1)} %broadcast_dynamic-update-slice_fusion), calls=%async_computation.3 | async-start | bytes 6291456 | tf_op jit(solution)/shard_map/all_to_all | solution.py:129
  138.1 1.6 multiply_convert_fusion
  139.7 38.2 %all-to-all-done.3 = bf16[32,384,128]{2,1,0:T(8,128)(2,1)} async-done(((bf16[32,384,128]{2,1,0:T(8,128)(2,1)}), bf16[32,384,128]{2,1,0:T(8,128)(2,1)}, u32[]{:S(2)}, u32[]{:S(2)}) %all-to-all-start.3) | async-done | bytes 3145760 | tf_op jit(solution)/shard_map/all_to_all | solution.py:129
  177.9 1.4 slice_convert_fusion.1
  179.6 0.9 reshape.128
  180.4 0.9 reshape.127
  181.3 1.9 convert_reduce_fusion
  (29 shorter events, 4.1 us)
Async XLA Ops:
  7.2 89.8 %copy-start = (bf16[1024,1024]{1,0:T(8,128)(2,1)S(1)}, bf16[1024,1024]{1,0:T(8,128)(2,1)}, u32[]{:S(2)}) copy-start(bf16[1024,1024]{1,0:T(8,128)(2,1)} %param.10) | copy-start | bytes 6291460
  7.2 53.4 %all-gather.2.cloned.1.call-start = ((), (), s32[]{:S(2)}) async-start(), calls=%async_computation.4 | async-start | bytes 3575808 | tf_op jit(solution)/shard_map/all_gather | solution.py:41
  14.3 50.2 %all-to-all-start = ((bf16[32,256,128]{2,1,0:T(8,128)(2,1)}), bf16[32,256,128]{2,1,0:T(8,128)(2,1)}, u32[]{:S(2)}, u32[]{:S(2)}) async-start(bf16[32,256,128]{2,1,0:T(8,128)(2,1)} %broadcast_in_dim.6), calls=%async_computation | async-start | bytes 4194304 | tf_op jit(solution)/shard_map/all_to_all | solution.py:16
  64.5 3.1 %copy-start.1 = (bf16[8,1024,128]{2,1,0:T(8,128)(2,1)S(1)}, bf16[8,1024,128]{2,1,0:T(8,128)(2,1)}, u32[]{:S(2)}) copy-start(bf16[8,1024,128]{2,1,0:T(8,128)(2,1)} %slice.51) | copy-start | bytes 6291460
  73.4 21.1 %all-to-all-start.1 = ((bf16[8,256,128]{1,2,0:T(8,128)(2,1)}), bf16[8,256,128]{1,2,0:T(8,128)(2,1)S(1)}, u32[]{:S(2)}, u32[]{:S(2)}) async-start(bf16[8,256,128]{1,2,0:T(8,128)(2,1)} %broadcast_in_dim.7), calls=%async_computation.1 | async-start | bytes 1048576 | tf_op jit(solution)/shard_map/all_to_all | solution.py:16
  94.5 2.4 %copy-start.2 = (f32[1,256,8,128]{3,2,1,0:T(8,128)S(1)}, f32[1,256,8,128]{3,2,1,0:T(8,128)}, u32[]{:S(2)}) copy-start(f32[1,256,8,128]{3,2,1,0:T(8,128)} %get-tuple-element.12) | copy-start | bytes 3145732
  97.0 2.4 %copy-start.3 = (bf16[256,128]{1,0:T(8,128)(2,1)S(1)}, bf16[256,128]{1,0:T(8,128)(2,1)}, u32[]{:S(2)}) copy-start(bf16[256,128]{1,0:T(8,128)(2,1)} %param.7) | copy-start | bytes 196612
  100.7 27.4 %all-to-all-start.2 = ((f32[32,8,1024]{2,1,0:T(8,128)}), f32[32,8,1024]{2,1,0:T(8,128)}, u32[]{:S(2)}, u32[]{:S(2)}) async-start(f32[32,8,1024]{2,1,0:T(8,128)} %fusion.14), calls=%async_computation.2 | async-start | bytes 2097152 | tf_op jit(solution)/shard_map/all_to_all | solution.py:22
  130.7 47.2 %all-to-all-start.3 = ((bf16[32,384,128]{2,1,0:T(8,128)(2,1)}), bf16[32,384,128]{2,1,0:T(8,128)(2,1)}, u32[]{:S(2)}, u32[]{:S(2)}) async-start(bf16[32,384,128]{2,1,0:T(8,128)(2,1)} %broadcast_dynamic-update-slice_fusion), calls=%async_computation.3 | async-start | bytes 6291456 | tf_op jit(solution)/shard_map/all_to_all | solution.py:129
Sparse Core Ops, SparseCore 0:
  11.7 48.8 all-gather.1

commit v9 on v8

--- a/solution.py
+++ b/solution.py
@@ -73,6 +73,9 @@
     aggregated = agg_f32.reshape(node_rows, feat_dev).astype(jnp.bfloat16)
 
     agg_parts = gather_rows(aggregated, "col", col_count).reshape(col_count, node_rows, feat_dev)
+    nodes = row_count * node_rows
+    dense_t = jnp.transpose(dense, (0, 2, 4, 1, 3)).reshape(nodes, node_rows)
+    agg_parts, dense_t = lax.optimization_barrier((agg_parts, dense_t))
     agg_full = jnp.moveaxis(agg_parts, 0, 1).reshape(node_rows, col_count * feat_dev)
     pair_parts = all_packed[:, slots * block_edge + 16 :].reshape(
         col_count, 2, node_rows, feat_dev
@@ -94,7 +97,6 @@
     root_part = lax.dot_general(
         features, preact_grad, contract_rows, preferred_element_type=jnp.float32
     )
-    nodes = row_count * node_rows
     grad_scale = 1.0 / math.sqrt(nodes)
     both = jnp.concatenate([weight_part, root_part], axis=0) * grad_scale
     both_sum = reduce_rows(both, "row", row_count)
@@ -115,10 +117,7 @@
     own_grad = lax.dot_general(
         preact_grad, r_rows, contract_cols, preferred_element_type=jnp.float32
     )
-    g_rows = aggregated_grad.reshape(row_blocks, block_edge, feat_dev)
-    column_terms = jnp.einsum(
-        "trcij,rif->tcjf", dense, g_rows, preferred_element_type=jnp.float32
-    ).reshape(nodes, feat_dev)
+    column_terms = jnp.dot(dense_t, aggregated_grad, preferred_element_type=jnp.float32)
     term_pieces = column_terms.astype(jnp.bfloat16).reshape(row_count, node_rows, feat_dev)
     room = jnp.zeros((row_count,) + sum_pair.shape, term_pieces.dtype)
     outgoing = jnp.concatenate([term_pieces, room], axis=1)

time: 192 us -> 186 us (0.969)
  waiting for transfers between devices: 89.9 us -> 83.7 us
  local copies, waits for them, and re-layouts: 20.6 us -> 26.6 us
  starting transfers between devices: 28.4 us -> 25.1 us
  matrix products: 23.4 us -> 20.9 us
    all_to_all x2, waiting for transfers between devices: 14 us -> 1.19 us  [gather_rows(): got = lax.all_to_all(spread, axis_name, 0, 0, tiled=True)]
    reshape x0 -> x2, local copies, waits for them, and re-layouts: none -> 10.5 us  [the longest x1 7.3 us: per_device(): dense_t = jnp.transpose(dense, (0, 2, 4, 1, 3)).reshape(nodes, node_rows)]
    all_to_all x1, waiting for transfers between devices: 0.01 us -> 6.66 us  [reduce_rows(): got = lax.all_to_all(pieces, axis_name, 0, 0, tiled=True)]
    dot_general x1 -> x0, local copies, waits for them, and re-layouts: 6.61 us -> none  [per_device(): jnp.einsum('trcij,rif->tcjf', dense, g_rows, preferred_element_type=jnp.f...]
    dot_general x1, matrix products: 5.37 us -> 1.87 us  [per_device(): jnp.einsum('tsp,tsij->tpij', onehot, tile_vals, preferred_element_type=jn...]
    all_to_all x1, starting transfers between devices: 7.44 us -> 4.61 us  [per_device(): incoming = lax.all_to_all(outgoing, 'row', 0, 0, tiled=True)]
    dot_general x2 -> x1, matrix products: 4.68 us -> 5.32 us  [per_device(): jnp.dot(dense_t, aggregated_grad, preferred_element_type=jnp.float32)]
  transfers between devices with their start and end apart: 5 -> 5, of which waited for: 3 -> 4; matrix products, arithmetic and copies ran while one was open for 16% -> 19% of each run, Pallas kernels for 0% -> 0%
where the time goes in v9:
time: 186 us; the launch traced here: 185 us
  waiting for transfers between devices  83.7 us (45%)
  local copies, waits for them, and re-layouts  26.6 us (14%)
  starting transfers between devices  25.1 us (13%)
  matrix products  20.9 us (11%)
  between operations  15 us (8%)
  other arithmetic  13.7 us (7%)
    all_to_all x1, waiting for transfers between devices, per_device(): incoming = lax.all_to_all(outgoing, 'row', 0, 0, tiled=True)  38.2 us
    all_gather x1, waiting for transfers between devices, per_device(): lax.all_gather(packed, 'col', axis=0, tiled=True)  37.6 us
    all_to_all x2, starting transfers between devices, gather_rows(): got = lax.all_to_all(spread, axis_name, 0, 0, tiled=True)  13 us
    all_to_all x1, starting transfers between devices, reduce_rows(): got = lax.all_to_all(pieces, axis_name, 0, 0, tiled=True)  7.47 us
    reshape x1, local copies, waits for them, and re-layouts, per_device(): dense_t = jnp.transpose(dense, (0, 2, 4, 1, 3)).reshape(nodes, node_rows)  7.3 us
    all_to_all x1, waiting for transfers between devices, reduce_rows(): got = lax.all_to_all(pieces, axis_name, 0, 0, tiled=True)  6.66 us
    dot_general x1, matrix products, per_device(): jnp.dot(dense_t, aggregated_grad, preferred_element_type=jnp.float32)  5.32 us
    all_to_all x1, starting transfers between devices, per_device(): incoming = lax.all_to_all(outgoing, 'row', 0, 0, tiled=True)  4.61 us
  transfers between devices with their start and end apart: 5, of which 4 were waited for; matrix products, arithmetic and copies ran while one was open for 19% of the time, Pallas kernels for 0%

profile of v9, /device:TPU:1, one launch (start us, length us, event | category | flops | bytes accessed | tf_op | source)
XLA Modules:
  0.0 185.0 jit_solution(13552469554120482591)
XLA Ops:
  8.8 1.1 bitcast_multiply_fusion.1
  9.9 1.6 fusion.20
  11.6 2.7 %broadcast_in_dim.6 = bf16[32,256,128]{2,1,0:T(8,128)(2,1)} broadcast(bf16[256,128]{1,0:T(8,128)(2,1)} %param.7), dimensions={1,2} | broadcast | bytes 2162688 | tf_op jit(solution)/shard_map/broadcast_in_dim | solution.py:15
  14.3 8.6 %all-to-all-start = ((bf16[32,256,128]{2,1,0:T(8,128)(2,1)}), bf16[32,256,128]{2,1,0:T(8,128)(2,1)}, u32[]{:S(2)}, u32[]{:S(2)}) async-start(bf16[32,256,128]{2,1,0:T(8,128)(2,1)} %broadcast_in_dim.6), calls=%async_computation | async-start | bytes 4194304 | tf_op jit(solution)/shard_map/all_to_all | solution.py:16
  22.9 37.6 %all-gather.2.cloned.1.call-done = bf16[12416,128]{1,0:T(8,128)(2,1)} async-done(((bf16[1552,128]{1,0:T(8,128)(2,1)}), bf16[12416,128]{1,0:T(8,128)(2,1)}) %all-gather.2.cloned.1.call-update) | async-done | bytes 3178512 | tf_op jit(solution)/shard_map/all_gather | solution.py:41
  60.6 3.1 %slice.51 = bf16[8,1024,128]{2,1,0:T(8,128)(2,1)} slice(bf16[8,1552,128]{2,1,0:T(8,128)(2,1)} %bitcast.82), slice={[0:8], [0:1024], [0:128]} | slice | bytes 4194304 | tf_op jit(solution)/shard_map/slice | solution.py:44
  64.5 3.1 %fusion.3 = bf16[8,8,128,128]{3,1,2,0:T(8,128)(2,1)S(1)} fusion(bf16[8,8,128,128]{3,2,1,0:T(8,128)(2,1)} %bitcast.10, s32[8,8]{1,0:T(8,128)S(1)} %get-tuple-element.21), kind=kOutput, calls=%fused_computation.8 | convolution fusion | flops 16777728 | bytes 4194560 | tf_op jit(solution)/shard_map/tsc,tcjf->tsjf/dot_general | solution.py:66
  68.3 4.2 %fusion.9 = bf16[2,128,128]{2,0,1:T(2,128)(2,1)S(1)} fusion(f32[8,8,128,128]{3,2,1,0:T(8,128)S(1)} %fusion.2, s32[8,8]{0,1:T(8,128)S(1)} %copy.12), kind=kOutput, calls=%fused_computation.16 | convolution fusion | flops 25198720 | bytes 4260096 | tf_op jit(solution)/shard_map/tsr,tsif->rif/dot_general | solution.py:72
  73.4 4.3 %all-to-all-start.1 = ((bf16[8,256,128]{1,2,0:T(8,128)(2,1)}), bf16[8,256,128]{1,2,0:T(8,128)(2,1)}, u32[]{:S(2)}, u32[]{:S(2)}) async-start(bf16[8,256,128]{1,2,0:T(8,128)(2,1)} %broadcast_in_dim.7), calls=%async_computation.1 | async-start | bytes 1048576 | tf_op jit(solution)/shard_map/all_to_all | solution.py:16
  77.8 1.4 slice.52
  79.9 1.9 %convert_bitcast_fusion = bf16[8,2,8,128,128]{4,2,1,3,0:T(8,128)(2,1)S(1)} fusion(bf16[8,8,128,128]{3,2,1,0:T(8,128)(2,1)S(1)} %bitcast.77, s32[8,8]{1,0:T(8,128)S(1)} %bitcast.90), kind=kOutput, calls=%fused_computation.6 | convolution fusion | flops 35652608 | bytes 6291712 | tf_op jit(solution)/shard_map/tsp,tsij->tpij/dot_general | solution.py:53
  81.8 3.2 %copy.47 = bf16[8,2,8,128,128]{4,2,0,3,1:T(8,128)(2,1)} copy(bf16[8,2,8,128,128]{4,2,1,3,0:T(8,128)(2,1)S(1)} %convert_bitcast_fusion) | data formatting | bytes 8388608 | tf_op jit(solution)/shard_map/reshape | solution.py:56
  85.0 7.3 %reshape.121 = bf16[8192,256]{0,1:T(8,128)(2,1)} reshape(bf16[8,8,128,2,128]{2,1,0,4,3:T(8,128)(2,1)} %bitcast.78) | data formatting | bytes 8388608 | tf_op jit(solution)/shard_map/reshape | solution.py:77
  92.3 1.2 slice_convert_fusion.2
  93.6 1.2 all-to-all-done.1
  94.8 1.9 %fusion.41 = f32[256,1024]{1,0:T(8,128)S(1)} fusion(bf16[256,1024]{0,1:T(8,128)(2,1)} %bitcast.19, bf16[1024,1024]{1,0:T(8,128)(2,1)S(1)} %copy-done), kind=kOutput, calls=%fused_computation.69 | convolution fusion | flops 536870912 | bytes 3670016 | tf_op jit(solution)/shard_map/dot_general | solution.py:86
  97.0 2.0 %fusion.12 = (bf16[256,1024]{1,0:T(8,128)(2,1)S(1)}, f32[256,1024]{1,0:T(8,128)}) fusion(f32[32,8,8,128]{3,2,1,0:T(8,128)S(1)} %bitcast.85, f32[256,1024]{1,0:T(8,128)S(1)} %fusion.41, bf16[1024,1024]{1,0:T(8,128)(2,1)S(1)} %copy-done.6, bf16[32,8,8,128]{3,2,1,0:T(8,128)(2,1)S(1)} %bitcast.88), kind=kOutput, calls=%fused_computation.19 | convolution fusion | flops 539492352 | bytes 6291456 | tf_op jit(solution)/shard_map/dot_general | solution.py:86
  99.6 1.1 fusion.13
  100.7 7.5 %all-to-all-start.2 = ((f32[32,8,1024]{2,1,0:T(8,128)}), f32[32,8,1024]{2,1,0:T(8,128)}, u32[]{:S(2)}, u32[]{:S(2)}) async-start(f32[32,8,1024]{2,1,0:T(8,128)} %fusion.13), calls=%async_computation.2 | async-start | bytes 2097152 | tf_op jit(solution)/shard_map/all_to_all | solution.py:22
  108.2 5.3 %convolution_convert_fusion = bf16[8192,128]{1,0:T(8,128)(2,1)} fusion(bf16[8192,256]{0,1:T(8,128)(2,1)} %reshape.121, bf16[256,1024]{1,0:T(8,128)(2,1)S(1)} %get-tuple-element.22, bf16[1024,1024]{1,0:T(8,128)(2,1)S(1)} %copy-done, s32[]{:T(128)S(6)} %select_n.27), kind=kOutput, calls=%fused_computation | convolution fusion | flops 605061120 | bytes 7077892 | tf_op jit(solution)/shard_map/dot_general | solution.py:120
  113.5 3.7 %concatenate.13 = bf16[32,384,128]{2,1,0:T(8,128)(2,1)} pad(bf16[32,256,128]{2,1,0:T(8,128)(2,1)} %bitcast.79, bf16[]{:T(256)} %constant.36.clone.1), padding=0_0x0_128x0_0 | pad | bytes 5242882 | tf_op jit(solution)/shard_map/concatenate | solution.py:123
  117.2 1.2 fusion.21
  118.5 6.7 %all-to-all-done.2 = f32[32,8,1024]{2,1,0:T(8,128)} async-done(((f32[32,8,1024]{2,1,0:T(8,128)}), f32[32,8,1024]{2,1,0:T(8,128)}, u32[]{:S(2)}, u32[]{:S(2)}) %all-to-all-start.2) | async-done | bytes 1048608 | tf_op jit(solution)/shard_map/all_to_all | solution.py:22
  125.2 1.3 reduce_sum.20
  126.5 1.2 broadcast_dynamic-update-slice_fusion
  127.7 4.6 %all-to-all-start.3 = ((bf16[32,384,128]{2,1,0:T(8,128)(2,1)}), bf16[32,384,128]{2,1,0:T(8,128)(2,1)}, u32[]{:S(2)}, u32[]{:S(2)}) async-start(bf16[32,384,128]{2,1,0:T(8,128)(2,1)} %broadcast_dynamic-update-slice_fusion), calls=%async_computation.3 | async-start | bytes 6291456 | tf_op jit(solution)/shard_map/all_to_all | solution.py:128
  132.4 1.6 multiply_convert_fusion
  133.9 38.2 %all-to-all-done.3 = bf16[32,384,128]{2,1,0:T(8,128)(2,1)} async-done(((bf16[32,384,128]{2,1,0:T(8,128)(2,1)}), bf16[32,384,128]{2,1,0:T(8,128)(2,1)}, u32[]{:S(2)}, u32[]{:S(2)}) %all-to-all-start.3) | async-done | bytes 3145760 | tf_op jit(solution)/shard_map/all_to_all | solution.py:128
  172.2 1.4 slice_convert_fusion.1
  173.8 0.9 reshape.126
  174.7 0.9 reshape.125
  175.6 1.9 %convert_reduce_fusion = f32[256,128]{1,0:T(8,128)S(1)} fusion(bf16[32,384,128]{2,1,0:T(8,128)(2,1)} %all-to-all-done.3), kind=kLoop, calls=%fused_computation.5 | loop fusion | flops 2064384 | bytes 2228224 | tf_op jit(solution)/shard_map/reduce_sum | solution.py:129
  (35 shorter events, 5.6 us)
Async XLA Ops:
  7.2 87.6 %copy-start = (bf16[1024,1024]{1,0:T(8,128)(2,1)S(1)}, bf16[1024,1024]{1,0:T(8,128)(2,1)}, u32[]{:S(2)}) copy-start(bf16[1024,1024]{1,0:T(8,128)(2,1)} %param.9) | copy-start | bytes 6291460
  7.2 53.4 %all-gather.2.cloned.1.call-start = ((), (), s32[]{:S(2)}) async-start(), calls=%async_computation.4 | async-start | bytes 3575808 | tf_op jit(solution)/shard_map/all_gather | solution.py:41
  14.3 50.2 %all-to-all-start = ((bf16[32,256,128]{2,1,0:T(8,128)(2,1)}), bf16[32,256,128]{2,1,0:T(8,128)(2,1)}, u32[]{:S(2)}, u32[]{:S(2)}) async-start(bf16[32,256,128]{2,1,0:T(8,128)(2,1)} %broadcast_in_dim.6), calls=%async_computation | async-start | bytes 4194304 | tf_op jit(solution)/shard_map/all_to_all | solution.py:16
  64.5 3.1 %copy-start.1 = (bf16[8,1024,128]{2,1,0:T(8,128)(2,1)S(1)}, bf16[8,1024,128]{2,1,0:T(8,128)(2,1)}, u32[]{:S(2)}) copy-start(bf16[8,1024,128]{2,1,0:T(8,128)(2,1)} %slice.51) | copy-start | bytes 6291460
  73.4 21.3 %all-to-all-start.1 = ((bf16[8,256,128]{1,2,0:T(8,128)(2,1)}), bf16[8,256,128]{1,2,0:T(8,128)(2,1)}, u32[]{:S(2)}, u32[]{:S(2)}) async-start(bf16[8,256,128]{1,2,0:T(8,128)(2,1)} %broadcast_in_dim.7), calls=%async_computation.1 | async-start | bytes 1048576 | tf_op jit(solution)/shard_map/all_to_all | solution.py:16
  77.8 2.2 %copy-start.2 = (bf16[8,1024,128]{2,1,0:T(8,128)(2,1)S(1)}, bf16[8,1024,128]{2,1,0:T(8,128)(2,1)}, u32[]{:S(2)}) copy-start(bf16[8,1024,128]{2,1,0:T(8,128)(2,1)} %slice.51) | copy-start | bytes 6291460
  94.8 1.9 %copy-start.3 = (f32[1,256,8,128]{3,2,1,0:T(8,128)S(1)}, f32[1,256,8,128]{3,2,1,0:T(8,128)}, u32[]{:S(2)}) copy-start(f32[1,256,8,128]{3,2,1,0:T(8,128)} %get-tuple-element.16) | copy-start | bytes 3145732
  94.8 1.9 %copy-start.5 = (bf16[1,256,8,128]{3,2,1,0:T(8,128)(2,1)S(1)}, bf16[1,256,8,128]{3,2,1,0:T(8,128)(2,1)}, u32[]{:S(2)}) copy-start(bf16[1,256,8,128]{3,2,1,0:T(8,128)(2,1)} %get-tuple-element.17) | copy-start | bytes 1572868
  94.8 2.2 %copy-start.6 = (bf16[1024,1024]{1,0:T(8,128)(2,1)S(1)}, bf16[1024,1024]{1,0:T(8,128)(2,1)}, u32[]{:S(2)}) copy-start(bf16[1024,1024]{1,0:T(8,128)(2,1)} %param.10) | copy-start | bytes 6291460
  97.0 2.3 %copy-start.4 = (bf16[256,128]{1,0:T(8,128)(2,1)S(1)}, bf16[256,128]{1,0:T(8,128)(2,1)}, u32[]{:S(2)}) copy-start(bf16[256,128]{1,0:T(8,128)(2,1)} %param.7) | copy-start | bytes 196612
  100.7 24.4 %all-to-all-start.2 = ((f32[32,8,1024]{2,1,0:T(8,128)}), f32[32,8,1024]{2,1,0:T(8,128)}, u32[]{:S(2)}, u32[]{:S(2)}) async-start(f32[32,8,1024]{2,1,0:T(8,128)} %fusion.13), calls=%async_computation.2 | async-start | bytes 2097152 | tf_op jit(solution)/shard_map/all_to_all | solution.py:22
  127.7 44.5 %all-to-all-start.3 = ((bf16[32,384,128]{2,1,0:T(8,128)(2,1)}), bf16[32,384,128]{2,1,0:T(8,128)(2,1)}, u32[]{:S(2)}, u32[]{:S(2)}) async-start(bf16[32,384,128]{2,1,0:T(8,128)(2,1)} %broadcast_dynamic-update-slice_fusion), calls=%async_computation.3 | async-start | bytes 6291456 | tf_op jit(solution)/shard_map/all_to_all | solution.py:128
Sparse Core Ops, SparseCore 0:
  11.7 48.8 all-gather.1

commit v10 on v9

--- a/solution.py
+++ b/solution.py
@@ -100,13 +100,8 @@
     grad_scale = 1.0 / math.sqrt(nodes)
     both = jnp.concatenate([weight_part, root_part], axis=0) * grad_scale
     both_sum = reduce_rows(both, "row", row_count)
-    high_f32 = lax.reduce_precision(both_sum, exponent_bits=8, mantissa_bits=7)
-    sum_high = high_f32.astype(jnp.bfloat16)
-    sum_low = (both_sum - high_f32).astype(jnp.bfloat16)
     sum_lanes = both_sum.size // block_edge
-    sum_pair = jnp.concatenate(
-        [sum_high.reshape(sum_lanes, block_edge), sum_low.reshape(sum_lanes, block_edge)], axis=0
-    )
+    sum_pair = both_sum.astype(jnp.bfloat16).reshape(sum_lanes, block_edge)
 
     w_rows = lax.dynamic_slice_in_dim(weight, col_index * feat_dev, feat_dev, 0)
     r_rows = lax.dynamic_slice_in_dim(root_weight, col_index * feat_dev, feat_dev, 0)
@@ -127,11 +122,10 @@
     )
     incoming = lax.all_to_all(outgoing, "row", 0, 0, tiled=True)
     summed_cols = incoming[:, :node_rows].astype(jnp.float32).sum(0)
-    got_high = incoming[:, node_rows : node_rows + sum_lanes].astype(jnp.float32)
-    got_low = incoming[:, node_rows + sum_lanes :].astype(jnp.float32)
+    got_sums = incoming[:, node_rows:].astype(jnp.float32)
     half = row_count // 2
-    weight_sum = (got_high[:half] + got_low[:half]).reshape(feat_dev, -1)
-    root_sum = (got_high[half:] + got_low[half:]).reshape(feat_dev, -1)
+    weight_sum = got_sums[:half].reshape(feat_dev, -1)
+    root_sum = got_sums[half:].reshape(feat_dev, -1)
     feature_grad = summed_cols + own_grad
     return (activations, feature_grad, weight_sum, root_sum)
 

time: 186 us -> 179 us (0.962)
  waiting for transfers between devices: 83.7 us -> 78.2 us
    all_to_all x1, waiting for transfers between devices: 38.2 us -> 32.4 us  [per_device(): incoming = lax.all_to_all(outgoing, 'row', 0, 0, tiled=True)]
where the time goes in v10:
time: 179 us; the launch traced here: 178 us
  waiting for transfers between devices  78.2 us (44%)
  local copies, waits for them, and re-layouts  26 us (15%)
  starting transfers between devices  25.1 us (14%)
  matrix products  20.9 us (12%)
  between operations  15 us (8%)
  other arithmetic  13.2 us (7%)
    all_gather x1, waiting for transfers between devices, per_device(): lax.all_gather(packed, 'col', axis=0, tiled=True)  37.6 us
    all_to_all x1, waiting for transfers between devices, per_device(): incoming = lax.all_to_all(outgoing, 'row', 0, 0, tiled=True)  32.4 us
    all_to_all x2, starting transfers between devices, gather_rows(): got = lax.all_to_all(spread, axis_name, 0, 0, tiled=True)  13 us
    all_to_all x1, starting transfers between devices, reduce_rows(): got = lax.all_to_all(pieces, axis_name, 0, 0, tiled=True)  7.47 us
    reshape x1, local copies, waits for them, and re-layouts, per_device(): dense_t = jnp.transpose(dense, (0, 2, 4, 1, 3)).reshape(nodes, node_rows)  7.32 us
    all_to_all x1, waiting for transfers between devices, reduce_rows(): got = lax.all_to_all(pieces, axis_name, 0, 0, tiled=True)  6.95 us
    dot_general x1, matrix products, per_device(): jnp.dot(dense_t, aggregated_grad, preferred_element_type=jnp.float32)  5.32 us
    all_to_all x1, starting transfers between devices, per_device(): incoming = lax.all_to_all(outgoing, 'row', 0, 0, tiled=True)  4.59 us
  transfers between devices with their start and end apart: 5, of which 4 were waited for; matrix products, arithmetic and copies ran while one was open for 19% of the time, Pallas kernels for 0%

profile of v10, /device:TPU:1, one launch (start us, length us, event | category | flops | bytes accessed | tf_op | source)
XLA Modules:
  0.0 178.4 jit_solution(6216260726535091166)
XLA Ops:
  8.8 1.1 bitcast_multiply_fusion.1
  9.9 1.6 fusion.20
  11.6 2.7 %broadcast_in_dim.6 = bf16[32,256,128]{2,1,0:T(8,128)(2,1)} broadcast(bf16[256,128]{1,0:T(8,128)(2,1)} %param.7), dimensions={1,2} | broadcast | bytes 2162688 | tf_op jit(solution)/shard_map/broadcast_in_dim | solution.py:15
  14.3 8.6 %all-to-all-start = ((bf16[32,256,128]{2,1,0:T(8,128)(2,1)}), bf16[32,256,128]{2,1,0:T(8,128)(2,1)}, u32[]{:S(2)}, u32[]{:S(2)}) async-start(bf16[32,256,128]{2,1,0:T(8,128)(2,1)} %broadcast_in_dim.6), calls=%async_computation | async-start | bytes 4194304 | tf_op jit(solution)/shard_map/all_to_all | solution.py:16
  22.9 37.6 %all-gather.2.cloned.1.call-done = bf16[12416,128]{1,0:T(8,128)(2,1)} async-done(((bf16[1552,128]{1,0:T(8,128)(2,1)}), bf16[12416,128]{1,0:T(8,128)(2,1)}) %all-gather.2.cloned.1.call-update) | async-done | bytes 3178512 | tf_op jit(solution)/shard_map/all_gather | solution.py:41
  60.6 3.1 %slice.39 = bf16[8,1024,128]{2,1,0:T(8,128)(2,1)} slice(bf16[8,1552,128]{2,1,0:T(8,128)(2,1)} %bitcast.82), slice={[0:8], [0:1024], [0:128]} | slice | bytes 4194304 | tf_op jit(solution)/shard_map/slice | solution.py:44
  64.5 3.1 %fusion.3 = bf16[8,8,128,128]{3,1,2,0:T(8,128)(2,1)S(1)} fusion(bf16[8,8,128,128]{3,2,1,0:T(8,128)(2,1)} %bitcast.10, s32[8,8]{1,0:T(8,128)S(1)} %get-tuple-element.17), kind=kOutput, calls=%fused_computation.8 | convolution fusion | flops 16777728 | bytes 4194560 | tf_op jit(solution)/shard_map/tsc,tcjf->tsjf/dot_general | solution.py:66
  68.3 4.2 %fusion.9 = bf16[2,128,128]{2,0,1:T(2,128)(2,1)S(1)} fusion(f32[8,8,128,128]{3,2,1,0:T(8,128)S(1)} %fusion.2, s32[8,8]{0,1:T(8,128)S(1)} %copy.12), kind=kOutput, calls=%fused_computation.16 | convolution fusion | flops 25198720 | bytes 4260096 | tf_op jit(solution)/shard_map/tsr,tsif->rif/dot_general | solution.py:72
  73.5 4.3 %all-to-all-start.1 = ((bf16[8,256,128]{1,2,0:T(8,128)(2,1)}), bf16[8,256,128]{1,2,0:T(8,128)(2,1)}, u32[]{:S(2)}, u32[]{:S(2)}) async-start(bf16[8,256,128]{1,2,0:T(8,128)(2,1)} %broadcast_in_dim.7), calls=%async_computation.1 | async-start | bytes 1048576 | tf_op jit(solution)/shard_map/all_to_all | solution.py:16
  77.8 1.4 slice.40
  80.0 1.9 %convert_bitcast_fusion = bf16[8,2,8,128,128]{4,2,1,3,0:T(8,128)(2,1)S(1)} fusion(bf16[8,8,128,128]{3,2,1,0:T(8,128)(2,1)S(1)} %bitcast.77, s32[8,8]{1,0:T(8,128)S(1)} %bitcast.90), kind=kOutput, calls=%fused_computation.6 | convolution fusion | flops 35652608 | bytes 6291712 | tf_op jit(solution)/shard_map/tsp,tsij->tpij/dot_general | solution.py:53
  81.8 3.2 %copy.47 = bf16[8,2,8,128,128]{4,2,0,3,1:T(8,128)(2,1)} copy(bf16[8,2,8,128,128]{4,2,1,3,0:T(8,128)(2,1)S(1)} %convert_bitcast_fusion) | data formatting | bytes 8388608 | tf_op jit(solution)/shard_map/reshape | solution.py:56
  85.0 7.3 %reshape.122 = bf16[8192,256]{0,1:T(8,128)(2,1)} reshape(bf16[8,8,128,2,128]{2,1,0,4,3:T(8,128)(2,1)} %bitcast.78) | data formatting | bytes 8388608 | tf_op jit(solution)/shard_map/reshape | solution.py:77
  92.3 1.3 slice_convert_fusion.1
  93.6 1.2 all-to-all-done.1
  94.8 1.9 %fusion.41 = f32[256,1024]{1,0:T(8,128)S(1)} fusion(bf16[256,1024]{0,1:T(8,128)(2,1)} %bitcast.19, bf16[1024,1024]{1,0:T(8,128)(2,1)S(1)} %copy-done), kind=kOutput, calls=%fused_computation.63 | convolution fusion | flops 536870912 | bytes 3670016 | tf_op jit(solution)/shard_map/dot_general | solution.py:86
  97.0 2.1 %fusion.12 = (bf16[256,1024]{1,0:T(8,128)(2,1)S(1)}, f32[256,1024]{1,0:T(8,128)}) fusion(f32[32,8,8,128]{3,2,1,0:T(8,128)S(1)} %bitcast.85, f32[256,1024]{1,0:T(8,128)S(1)} %fusion.41, bf16[1024,1024]{1,0:T(8,128)(2,1)S(1)} %copy-done.6, bf16[32,8,8,128]{3,2,1,0:T(8,128)(2,1)S(1)} %bitcast.88), kind=kOutput, calls=%fused_computation.19 | convolution fusion | flops 539492352 | bytes 6291456 | tf_op jit(solution)/shard_map/dot_general | solution.py:86
  99.6 1.2 fusion.13
  100.8 7.5 %all-to-all-start.2 = ((f32[32,8,1024]{2,1,0:T(8,128)}), f32[32,8,1024]{2,1,0:T(8,128)}, u32[]{:S(2)}, u32[]{:S(2)}) async-start(f32[32,8,1024]{2,1,0:T(8,128)} %fusion.13), calls=%async_computation.2 | async-start | bytes 2097152 | tf_op jit(solution)/shard_map/all_to_all | solution.py:22
  108.2 5.3 %convolution_convert_fusion = bf16[8192,128]{1,0:T(8,128)(2,1)} fusion(bf16[8192,256]{0,1:T(8,128)(2,1)} %reshape.122, bf16[256,1024]{1,0:T(8,128)(2,1)S(1)} %get-tuple-element.18, bf16[1024,1024]{1,0:T(8,128)(2,1)S(1)} %copy-done, s32[]{:T(128)S(6)} %select_n.27), kind=kOutput, calls=%fused_computation | convolution fusion | flops 605061120 | bytes 7077892 | tf_op jit(solution)/shard_map/dot_general | solution.py:115
  113.6 3.4 %concatenate.10 = bf16[32,320,128]{2,1,0:T(8,128)(2,1)} pad(bf16[32,256,128]{2,1,0:T(8,128)(2,1)} %bitcast.79, bf16[]{:T(256)} %constant.36.clone.1), padding=0_0x0_64x0_0 | pad | bytes 4718594 | tf_op jit(solution)/shard_map/concatenate | solution.py:118
  117.0 1.2 fusion.21
  118.3 6.9 %all-to-all-done.2 = f32[32,8,1024]{2,1,0:T(8,128)} async-done(((f32[32,8,1024]{2,1,0:T(8,128)}), f32[32,8,1024]{2,1,0:T(8,128)}, u32[]{:S(2)}, u32[]{:S(2)}) %all-to-all-start.2) | async-done | bytes 1048608 | tf_op jit(solution)/shard_map/all_to_all | solution.py:22
  125.2 1.3 reduce_sum.18
  126.5 0.9 broadcast_dynamic-update-slice_fusion
  127.4 4.6 %all-to-all-start.3 = ((bf16[32,320,128]{2,1,0:T(8,128)(2,1)}), bf16[32,320,128]{2,1,0:T(8,128)(2,1)}, u32[]{:S(2)}, u32[]{:S(2)}) async-start(bf16[32,320,128]{2,1,0:T(8,128)(2,1)} %broadcast_dynamic-update-slice_fusion), calls=%async_computation.3 | async-start | bytes 5242880 | tf_op jit(solution)/shard_map/all_to_all | solution.py:123
  132.0 1.6 multiply_convert_fusion
  133.6 32.4 %all-to-all-done.3 = bf16[32,320,128]{2,1,0:T(8,128)(2,1)} async-done(((bf16[32,320,128]{2,1,0:T(8,128)(2,1)}), bf16[32,320,128]{2,1,0:T(8,128)(2,1)}, u32[]{:S(2)}, u32[]{:S(2)}) %all-to-all-start.3) | async-done | bytes 2621472 | tf_op jit(solution)/shard_map/all_to_all | solution.py:123
  166.0 1.1 slice_convert_fusion
  167.3 0.9 reshape.127
  168.1 0.9 reshape.126
  169.0 1.9 %convert_reduce_fusion = f32[256,128]{1,0:T(8,128)S(1)} fusion(bf16[32,320,128]{2,1,0:T(8,128)(2,1)} %all-to-all-done.3), kind=kLoop, calls=%fused_computation.5 | loop fusion | flops 2064384 | bytes 2228224 | tf_op jit(solution)/shard_map/reduce_sum | solution.py:124
  (33 shorter events, 5.5 us)
Async XLA Ops:
  7.2 87.6 %copy-start = (bf16[1024,1024]{1,0:T(8,128)(2,1)S(1)}, bf16[1024,1024]{1,0:T(8,128)(2,1)}, u32[]{:S(2)}) copy-start(bf16[1024,1024]{1,0:T(8,128)(2,1)} %param.9) | copy-start | bytes 6291460
  7.2 53.4 %all-gather.2.cloned.1.call-start = ((), (), s32[]{:S(2)}) async-start(), calls=%async_computation.4 | async-start | bytes 3575808 | tf_op jit(solution)/shard_map/all_gather | solution.py:41
  14.3 50.2 %all-to-all-start = ((bf16[32,256,128]{2,1,0:T(8,128)(2,1)}), bf16[32,256,128]{2,1,0:T(8,128)(2,1)}, u32[]{:S(2)}, u32[]{:S(2)}) async-start(bf16[32,256,128]{2,1,0:T(8,128)(2,1)} %broadcast_in_dim.6), calls=%async_computation | async-start | bytes 4194304 | tf_op jit(solution)/shard_map/all_to_all | solution.py:16
  64.5 3.1 %copy-start.1 = (bf16[8,1024,128]{2,1,0:T(8,128)(2,1)S(1)}, bf16[8,1024,128]{2,1,0:T(8,128)(2,1)}, u32[]{:S(2)}) copy-start(bf16[8,1024,128]{2,1,0:T(8,128)(2,1)} %slice.39) | copy-start | bytes 6291460
  73.5 21.3 %all-to-all-start.1 = ((bf16[8,256,128]{1,2,0:T(8,128)(2,1)}), bf16[8,256,128]{1,2,0:T(8,128)(2,1)}, u32[]{:S(2)}, u32[]{:S(2)}) async-start(bf16[8,256,128]{1,2,0:T(8,128)(2,1)} %broadcast_in_dim.7), calls=%async_computation.1 | async-start | bytes 1048576 | tf_op jit(solution)/shard_map/all_to_all | solution.py:16
  77.8 2.2 %copy-start.2 = (bf16[8,1024,128]{2,1,0:T(8,128)(2,1)S(1)}, bf16[8,1024,128]{2,1,0:T(8,128)(2,1)}, u32[]{:S(2)}) copy-start(bf16[8,1024,128]{2,1,0:T(8,128)(2,1)} %slice.39) | copy-start | bytes 6291460
  94.8 1.9 %copy-start.3 = (f32[1,256,8,128]{3,2,1,0:T(8,128)S(1)}, f32[1,256,8,128]{3,2,1,0:T(8,128)}, u32[]{:S(2)}) copy-start(f32[1,256,8,128]{3,2,1,0:T(8,128)} %get-tuple-element.14) | copy-start | bytes 3145732
  94.8 1.9 %copy-start.5 = (bf16[1,256,8,128]{3,2,1,0:T(8,128)(2,1)S(1)}, bf16[1,256,8,128]{3,2,1,0:T(8,128)(2,1)}, u32[]{:S(2)}) copy-start(bf16[1,256,8,128]{3,2,1,0:T(8,128)(2,1)} %get-tuple-element.15) | copy-start | bytes 1572868
  94.8 2.2 %copy-start.6 = (bf16[1024,1024]{1,0:T(8,128)(2,1)S(1)}, bf16[1024,1024]{1,0:T(8,128)(2,1)}, u32[]{:S(2)}) copy-start(bf16[1024,1024]{1,0:T(8,128)(2,1)} %param.10) | copy-start | bytes 6291460
  97.0 2.3 %copy-start.4 = (bf16[256,128]{1,0:T(8,128)(2,1)S(1)}, bf16[256,128]{1,0:T(8,128)(2,1)}, u32[]{:S(2)}) copy-start(bf16[256,128]{1,0:T(8,128)(2,1)} %param.7) | copy-start | bytes 196612
  100.8 24.4 %all-to-all-start.2 = ((f32[32,8,1024]{2,1,0:T(8,128)}), f32[32,8,1024]{2,1,0:T(8,128)}, u32[]{:S(2)}, u32[]{:S(2)}) async-start(f32[32,8,1024]{2,1,0:T(8,128)} %fusion.13), calls=%async_computation.2 | async-start | bytes 2097152 | tf_op jit(solution)/shard_map/all_to_all | solution.py:22
  127.4 38.6 %all-to-all-start.3 = ((bf16[32,320,128]{2,1,0:T(8,128)(2,1)}), bf16[32,320,128]{2,1,0:T(8,128)(2,1)}, u32[]{:S(2)}, u32[]{:S(2)}) async-start(bf16[32,320,128]{2,1,0:T(8,128)(2,1)} %broadcast_dynamic-update-slice_fusion), calls=%async_computation.3 | async-start | bytes 5242880 | tf_op jit(solution)/shard_map/all_to_all | solution.py:123
Sparse Core Ops, SparseCore 0:
  11.7 48.8 all-gather.1

commit v11 on v10

--- a/solution.py
+++ b/solution.py
@@ -99,7 +99,7 @@
     )
     grad_scale = 1.0 / math.sqrt(nodes)
     both = jnp.concatenate([weight_part, root_part], axis=0) * grad_scale
-    both_sum = reduce_rows(both, "row", row_count)
+    both_sum = reduce_rows(both.astype(jnp.bfloat16), "row", row_count)
     sum_lanes = both_sum.size // block_edge
     sum_pair = both_sum.astype(jnp.bfloat16).reshape(sum_lanes, block_edge)
 

time: 179 us -> 174 us (0.972)
  waiting for transfers between devices: 78.2 us -> 72.8 us
    all_to_all x1, waiting for transfers between devices: 6.95 us -> 1.56 us  [reduce_rows(): got = lax.all_to_all(pieces, axis_name, 0, 0, tiled=True)]
  transfers between devices with their start and end apart: 5 -> 5, of which waited for: 4 -> 4; matrix products, arithmetic and copies ran while one was open for 19% -> 20% of each run, Pallas kernels for 0% -> 0%
where the time goes in v11:
time: 174 us; the launch traced here: 173 us
  waiting for transfers between devices  72.8 us (42%)
  starting transfers between devices  26.3 us (15%)
  local copies, waits for them, and re-layouts  26.2 us (15%)
  matrix products  21 us (12%)
  between operations  15 us (9%)
  other arithmetic  11.7 us (7%)
    all_gather x1, waiting for transfers between devices, per_device(): lax.all_gather(packed, 'col', axis=0, tiled=True)  37.6 us
    all_to_all x1, waiting for transfers between devices, per_device(): incoming = lax.all_to_all(outgoing, 'row', 0, 0, tiled=True)  32.4 us
    all_to_all x2, starting transfers between devices, gather_rows(): got = lax.all_to_all(spread, axis_name, 0, 0, tiled=True)  13 us
    all_to_all x1, starting transfers between devices, reduce_rows(): got = lax.all_to_all(pieces, axis_name, 0, 0, tiled=True)  7.42 us
    reshape x1, local copies, waits for them, and re-layouts, per_device(): dense_t = jnp.transpose(dense, (0, 2, 4, 1, 3)).reshape(nodes, node_rows)  7.32 us
    all_to_all x1, starting transfers between devices, per_device(): incoming = lax.all_to_all(outgoing, 'row', 0, 0, tiled=True)  5.88 us
    dot_general x1, matrix products, per_device(): jnp.dot(dense_t, aggregated_grad, preferred_element_type=jnp.float32)  5.32 us
    dot_general x1, matrix products, per_device(): jnp.einsum('tsr,tsif->rif', row_hot, products, precision=lax.Precision.HI...  4.21 us
  transfers between devices with their start and end apart: 5, of which 4 were waited for; matrix products, arithmetic and copies ran while one was open for 20% of the time, Pallas kernels for 0%

profile of v11, /device:TPU:1, one launch (start us, length us, event | category | flops | bytes accessed | tf_op | source)
XLA Modules:
  0.0 173.0 jit_solution(13387737339675581025)
XLA Ops:
  8.8 1.1 bitcast_multiply_fusion.1
  9.9 1.6 fusion.21
  11.6 2.7 %broadcast_in_dim.8 = bf16[32,256,128]{2,1,0:T(8,128)(2,1)} broadcast(bf16[256,128]{1,0:T(8,128)(2,1)} %param.7), dimensions={1,2} | broadcast | bytes 2162688 | tf_op jit(solution)/shard_map/broadcast_in_dim | solution.py:15
  14.3 8.6 %all-to-all-start = ((bf16[32,256,128]{2,1,0:T(8,128)(2,1)}), bf16[32,256,128]{2,1,0:T(8,128)(2,1)}, u32[]{:S(2)}, u32[]{:S(2)}) async-start(bf16[32,256,128]{2,1,0:T(8,128)(2,1)} %broadcast_in_dim.8), calls=%async_computation | async-start | bytes 4194304 | tf_op jit(solution)/shard_map/all_to_all | solution.py:16
  22.9 37.6 %all-gather.2.cloned.1.call-done = bf16[12416,128]{1,0:T(8,128)(2,1)} async-done(((bf16[1552,128]{1,0:T(8,128)(2,1)}), bf16[12416,128]{1,0:T(8,128)(2,1)}) %all-gather.2.cloned.1.call-update) | async-done | bytes 3178512 | tf_op jit(solution)/shard_map/all_gather | solution.py:41
  60.6 3.1 %slice.39 = bf16[8,1024,128]{2,1,0:T(8,128)(2,1)} slice(bf16[8,1552,128]{2,1,0:T(8,128)(2,1)} %bitcast.82), slice={[0:8], [0:1024], [0:128]} | slice | bytes 4194304 | tf_op jit(solution)/shard_map/slice | solution.py:44
  64.5 3.1 %fusion.3 = bf16[8,8,128,128]{3,1,2,0:T(8,128)(2,1)S(1)} fusion(bf16[8,8,128,128]{3,2,1,0:T(8,128)(2,1)} %bitcast.10, s32[8,8]{1,0:T(8,128)S(1)} %get-tuple-element.17), kind=kOutput, calls=%fused_computation.8 | convolution fusion | flops 16777728 | bytes 4194560 | tf_op jit(solution)/shard_map/tsc,tcjf->tsjf/dot_general | solution.py:66
  68.3 4.2 %fusion.9 = bf16[2,128,128]{2,0,1:T(2,128)(2,1)S(1)} fusion(f32[8,8,128,128]{3,2,1,0:T(8,128)S(1)} %fusion.2, s32[8,8]{0,1:T(8,128)S(1)} %copy.12), kind=kOutput, calls=%fused_computation.16 | convolution fusion | flops 25198720 | bytes 4260096 | tf_op jit(solution)/shard_map/tsr,tsif->rif/dot_general | solution.py:72
  72.6 0.8 broadcast_in_dim.9
  73.5 4.3 %all-to-all-start.1 = ((bf16[8,256,128]{1,2,0:T(8,128)(2,1)}), bf16[8,256,128]{1,2,0:T(8,128)(2,1)}, u32[]{:S(2)}, u32[]{:S(2)}) async-start(bf16[8,256,128]{1,2,0:T(8,128)(2,1)} %broadcast_in_dim.9), calls=%async_computation.1 | async-start | bytes 1048576 | tf_op jit(solution)/shard_map/all_to_all | solution.py:16
  77.8 1.4 slice.40
  80.0 1.9 %convert_bitcast_fusion = bf16[8,2,8,128,128]{4,2,1,3,0:T(8,128)(2,1)S(1)} fusion(bf16[8,8,128,128]{3,2,1,0:T(8,128)(2,1)S(1)} %bitcast.77, s32[8,8]{1,0:T(8,128)S(1)} %bitcast.90), kind=kOutput, calls=%fused_computation.6 | convolution fusion | flops 35652608 | bytes 6291712 | tf_op jit(solution)/shard_map/tsp,tsij->tpij/dot_general | solution.py:53
  81.8 3.2 %copy.47 = bf16[8,2,8,128,128]{4,2,0,3,1:T(8,128)(2,1)} copy(bf16[8,2,8,128,128]{4,2,1,3,0:T(8,128)(2,1)S(1)} %convert_bitcast_fusion) | data formatting | bytes 8388608 | tf_op jit(solution)/shard_map/reshape | solution.py:56
  85.0 7.3 %reshape.118 = bf16[8192,256]{0,1:T(8,128)(2,1)} reshape(bf16[8,8,128,2,128]{2,1,0,4,3:T(8,128)(2,1)} %bitcast.78) | data formatting | bytes 8388608 | tf_op jit(solution)/shard_map/reshape | solution.py:77
  92.3 1.3 slice_convert_fusion.1
  93.6 1.2 all-to-all-done.1
  94.8 1.9 %fusion.42 = f32[256,1024]{1,0:T(8,128)S(1)} fusion(bf16[256,1024]{0,1:T(8,128)(2,1)} %bitcast.19, bf16[1024,1024]{1,0:T(8,128)(2,1)S(1)} %copy-done), kind=kOutput, calls=%fused_computation.64 | convolution fusion | flops 536870912 | bytes 3670016 | tf_op jit(solution)/shard_map/dot_general | solution.py:86
  97.0 2.1 %fusion.12 = (bf16[256,1024]{1,0:T(8,128)(2,1)S(1)}, f32[256,1024]{1,0:T(8,128)}) fusion(f32[32,8,8,128]{3,2,1,0:T(8,128)S(1)} %bitcast.85, f32[256,1024]{1,0:T(8,128)S(1)} %fusion.42, bf16[1024,1024]{1,0:T(8,128)(2,1)S(1)} %copy-done.6, bf16[32,8,8,128]{3,2,1,0:T(8,128)(2,1)S(1)} %bitcast.88), kind=kOutput, calls=%fused_computation.19 | convolution fusion | flops 539492352 | bytes 6291456 | tf_op jit(solution)/shard_map/dot_general | solution.py:86
  99.7 0.9 fusion.16
  100.5 7.4 %all-to-all-start.2 = ((bf16[32,8,1024]{2,1,0:T(8,128)(2,1)}), bf16[32,8,1024]{2,1,0:T(8,128)(2,1)S(1)}, u32[]{:S(2)}, u32[]{:S(2)}) async-start(bf16[32,8,1024]{2,1,0:T(8,128)(2,1)} %fusion.16), calls=%async_computation.2 | async-start | bytes 1048576 | tf_op jit(solution)/shard_map/all_to_all | solution.py:22
  108.0 5.3 %convolution_convert_fusion = bf16[8192,128]{1,0:T(8,128)(2,1)} fusion(bf16[8192,256]{0,1:T(8,128)(2,1)} %reshape.118, bf16[256,1024]{1,0:T(8,128)(2,1)S(1)} %get-tuple-element.18, bf16[1024,1024]{1,0:T(8,128)(2,1)S(1)} %copy-done, s32[]{:T(128)S(6)} %select_n.27), kind=kOutput, calls=%fused_computation | convolution fusion | flops 605061120 | bytes 7077892 | tf_op jit(solution)/shard_map/dot_general | solution.py:115
  113.3 3.5 %concatenate.10 = bf16[32,320,128]{2,1,0:T(8,128)(2,1)} pad(bf16[32,256,128]{2,1,0:T(8,128)(2,1)} %bitcast.79, bf16[]{:T(256)} %constant.37.clone.1), padding=0_0x0_64x0_0 | pad | bytes 4718594 | tf_op jit(solution)/shard_map/concatenate | solution.py:118
  116.7 1.2 fusion.22
  118.0 1.6 all-to-all-done.2
  119.7 1.0 broadcast_dynamic-update-slice_fusion
  120.7 5.9 %all-to-all-start.3 = ((bf16[32,320,128]{2,1,0:T(8,128)(2,1)}), bf16[32,320,128]{2,1,0:T(8,128)(2,1)}, u32[]{:S(2)}, u32[]{:S(2)}) async-start(bf16[32,320,128]{2,1,0:T(8,128)(2,1)} %broadcast_dynamic-update-slice_fusion), calls=%async_computation.3 | async-start | bytes 5242880 | tf_op jit(solution)/shard_map/all_to_all | solution.py:123
  126.6 1.6 multiply_convert_fusion
  128.2 32.4 %all-to-all-done.3 = bf16[32,320,128]{2,1,0:T(8,128)(2,1)} async-done(((bf16[32,320,128]{2,1,0:T(8,128)(2,1)}), bf16[32,320,128]{2,1,0:T(8,128)(2,1)}, u32[]{:S(2)}, u32[]{:S(2)}) %all-to-all-start.3) | async-done | bytes 2621472 | tf_op jit(solution)/shard_map/all_to_all | solution.py:123
  160.6 1.1 slice_convert_fusion
  161.8 0.9 reshape.123
  162.7 0.9 reshape.122
  163.6 1.9 %convert_reduce_fusion = f32[256,128]{1,0:T(8,128)S(1)} fusion(bf16[32,320,128]{2,1,0:T(8,128)(2,1)} %all-to-all-done.3), kind=kLoop, calls=%fused_computation.5 | loop fusion | flops 2064384 | bytes 2228224 | tf_op jit(solution)/shard_map/reduce_sum | solution.py:124
  (33 shorter events, 4.8 us)
Async XLA Ops:
  7.2 87.6 %copy-start = (bf16[1024,1024]{1,0:T(8,128)(2,1)S(1)}, bf16[1024,1024]{1,0:T(8,128)(2,1)}, u32[]{:S(2)}) copy-start(bf16[1024,1024]{1,0:T(8,128)(2,1)} %param.9) | copy-start | bytes 6291460
  7.2 53.4 %all-gather.2.cloned.1.call-start = ((), (), s32[]{:S(2)}) async-start(), calls=%async_computation.4 | async-start | bytes 3575808 | tf_op jit(solution)/shard_map/all_gather | solution.py:41
  14.3 50.2 %all-to-all-start = ((bf16[32,256,128]{2,1,0:T(8,128)(2,1)}), bf16[32,256,128]{2,1,0:T(8,128)(2,1)}, u32[]{:S(2)}, u32[]{:S(2)}) async-start(bf16[32,256,128]{2,1,0:T(8,128)(2,1)} %broadcast_in_dim.8), calls=%async_computation | async-start | bytes 4194304 | tf_op jit(solution)/shard_map/all_to_all | solution.py:16
  64.5 3.1 %copy-start.1 = (bf16[8,1024,128]{2,1,0:T(8,128)(2,1)S(1)}, bf16[8,1024,128]{2,1,0:T(8,128)(2,1)}, u32[]{:S(2)}) copy-start(bf16[8,1024,128]{2,1,0:T(8,128)(2,1)} %slice.39) | copy-start | bytes 6291460
  73.5 21.3 %all-to-all-start.1 = ((bf16[8,256,128]{1,2,0:T(8,128)(2,1)}), bf16[8,256,128]{1,2,0:T(8,128)(2,1)}, u32[]{:S(2)}, u32[]{:S(2)}) async-start(bf16[8,256,128]{1,2,0:T(8,128)(2,1)} %broadcast_in_dim.9), calls=%async_computation.1 | async-start | bytes 1048576 | tf_op jit(solution)/shard_map/all_to_all | solution.py:16
  77.8 2.2 %copy-start.2 = (bf16[8,1024,128]{2,1,0:T(8,128)(2,1)S(1)}, bf16[8,1024,128]{2,1,0:T(8,128)(2,1)}, u32[]{:S(2)}) copy-start(bf16[8,1024,128]{2,1,0:T(8,128)(2,1)} %slice.39) | copy-start | bytes 6291460
  94.8 1.9 %copy-start.3 = (f32[1,256,8,128]{3,2,1,0:T(8,128)S(1)}, f32[1,256,8,128]{3,2,1,0:T(8,128)}, u32[]{:S(2)}) copy-start(f32[1,256,8,128]{3,2,1,0:T(8,128)} %get-tuple-element.14) | copy-start | bytes 3145732
  94.8 1.9 %copy-start.5 = (bf16[1,256,8,128]{3,2,1,0:T(8,128)(2,1)S(1)}, bf16[1,256,8,128]{3,2,1,0:T(8,128)(2,1)}, u32[]{:S(2)}) copy-start(bf16[1,256,8,128]{3,2,1,0:T(8,128)(2,1)} %get-tuple-element.15) | copy-start | bytes 1572868
  94.8 2.2 %copy-start.6 = (bf16[1024,1024]{1,0:T(8,128)(2,1)S(1)}, bf16[1024,1024]{1,0:T(8,128)(2,1)}, u32[]{:S(2)}) copy-start(bf16[1024,1024]{1,0:T(8,128)(2,1)} %param.10) | copy-start | bytes 6291460
  97.0 2.4 %copy-start.4 = (bf16[256,128]{1,0:T(8,128)(2,1)S(1)}, bf16[256,128]{1,0:T(8,128)(2,1)}, u32[]{:S(2)}) copy-start(bf16[256,128]{1,0:T(8,128)(2,1)} %param.7) | copy-start | bytes 196612
  100.5 19.0 %all-to-all-start.2 = ((bf16[32,8,1024]{2,1,0:T(8,128)(2,1)}), bf16[32,8,1024]{2,1,0:T(8,128)(2,1)S(1)}, u32[]{:S(2)}, u32[]{:S(2)}) async-start(bf16[32,8,1024]{2,1,0:T(8,128)(2,1)} %fusion.16), calls=%async_computation.2 | async-start | bytes 1048576 | tf_op jit(solution)/shard_map/all_to_all | solution.py:22
  120.7 39.9 %all-to-all-start.3 = ((bf16[32,320,128]{2,1,0:T(8,128)(2,1)}), bf16[32,320,128]{2,1,0:T(8,128)(2,1)}, u32[]{:S(2)}, u32[]{:S(2)}) async-start(bf16[32,320,128]{2,1,0:T(8,128)(2,1)} %broadcast_dynamic-update-slice_fusion), calls=%async_computation.3 | async-start | bytes 5242880 | tf_op jit(solution)/shard_map/all_to_all | solution.py:123
Sparse Core Ops, SparseCore 0:
  11.7 48.8 all-gather.1

commit v12 on v11

--- a/solution.py
+++ b/solution.py
@@ -57,19 +57,14 @@
 
     x_all = gather_rows(features, "row", row_count)
     x_tiles = x_all.reshape(col_count, cb, block_edge, feat_dev)
-    col_hot = (
-        (tile_pos % cb)[:, :, None] == jnp.arange(cb, dtype=jnp.int32)[None, None, :]
-    ).astype(values.dtype)
     row_hot = (
         (tile_pos // cb)[:, :, None] == jnp.arange(row_blocks, dtype=jnp.int32)[None, None, :]
     ).astype(jnp.float32)
-    chosen = jnp.einsum(
-        "tsc,tcjf->tsjf", col_hot, x_tiles, preferred_element_type=jnp.float32
-    ).astype(values.dtype)
+    chosen = jnp.take_along_axis(x_tiles, (tile_pos % cb)[:, :, None, None], axis=1)
     products = jnp.einsum(
         "tsij,tsjf->tsif", tile_vals, chosen, preferred_element_type=jnp.float32
     )
-    agg_f32 = jnp.einsum("tsr,tsif->rif", row_hot, products, precision=lax.Precision.HIGHEST)
+    agg_f32 = jnp.sum(products[:, :, None] * row_hot[:, :, :, None, None], axis=(0, 1))
     aggregated = agg_f32.reshape(node_rows, feat_dev).astype(jnp.bfloat16)
 
     agg_parts = gather_rows(aggregated, "col", col_count).reshape(col_count, node_rows, feat_dev)

time: 174 us -> 174 us (level)
  matrix products: 21 us -> 15.9 us
  local copies, waits for them, and re-layouts: 26.2 us -> 30 us
    dot_general x2 -> x0, matrix products: 7.3 us -> none  [the longest x1 4.21 us: per_device(): jnp.einsum('tsr,tsif->rif', row_hot, products, precision=lax.Precision.HI...]
    gather x0 -> x2, local copies, waits for them, and re-layouts: none -> 3.9 us  [per_device(): jnp.take_along_axis(x_tiles, (tile_pos % cb)[:, :, None, None], axis=1)]
    dot_general x1, matrix products: 0.7 us -> 3 us  [per_device(): jnp.einsum('tsij,tsjf->tsif', tile_vals, chosen, preferred_element_type=j...]
where the time goes in v12:
time: 174 us; the launch traced here: 173 us
  waiting for transfers between devices  73.7 us (42%)
  local copies, waits for them, and re-layouts  30 us (17%)
  starting transfers between devices  26.1 us (15%)
  matrix products  15.9 us (9%)
  between operations  14.9 us (9%)
  other arithmetic  12.7 us (7%)
    all_gather x1, waiting for transfers between devices, per_device(): lax.all_gather(packed, 'col', axis=0, tiled=True)  37.6 us
    all_to_all x1, waiting for transfers between devices, per_device(): incoming = lax.all_to_all(outgoing, 'row', 0, 0, tiled=True)  32.4 us
    all_to_all x2, starting transfers between devices, gather_rows(): got = lax.all_to_all(spread, axis_name, 0, 0, tiled=True)  12.8 us
    all_to_all x1, starting transfers between devices, reduce_rows(): got = lax.all_to_all(pieces, axis_name, 0, 0, tiled=True)  7.46 us
    reshape x1, local copies, waits for them, and re-layouts, per_device(): dense_t = jnp.transpose(dense, (0, 2, 4, 1, 3)).reshape(nodes, node_rows)  7.3 us
    all_to_all x1, starting transfers between devices, per_device(): incoming = lax.all_to_all(outgoing, 'row', 0, 0, tiled=True)  5.87 us
    dot_general x1, matrix products, per_device(): jnp.dot(dense_t, aggregated_grad, preferred_element_type=jnp.float32)  5.31 us
    gather x2, local copies, waits for them, and re-layouts, per_device(): jnp.take_along_axis(x_tiles, (tile_pos % cb)[:, :, None, None], axis=1)  3.9 us
  transfers between devices with their start and end apart: 5, of which 4 were waited for; matrix products, arithmetic and copies ran while one was open for 20% of the time, Pallas kernels for 0%

profile of v12, /device:TPU:1, one launch (start us, length us, event | category | flops | bytes accessed | tf_op | source)
XLA Modules:
  0.0 173.3 jit_solution(12382273419876091709)
XLA Ops:
  8.8 1.1 bitcast_multiply_fusion.1
  9.9 1.6 fusion.14
  11.6 2.7 %broadcast_in_dim.17 = bf16[32,256,128]{2,1,0:T(8,128)(2,1)} broadcast(bf16[256,128]{1,0:T(8,128)(2,1)} %param.7), dimensions={1,2} | broadcast | bytes 2162688 | tf_op jit(solution)/shard_map/broadcast_in_dim | solution.py:15
  14.3 8.6 %all-to-all-start = ((bf16[32,256,128]{2,1,0:T(8,128)(2,1)}), bf16[32,256,128]{2,1,0:T(8,128)(2,1)}, u32[]{:S(2)}, u32[]{:S(2)}) async-start(bf16[32,256,128]{2,1,0:T(8,128)(2,1)} %broadcast_in_dim.17), calls=%async_computation | async-start | bytes 4194304 | tf_op jit(solution)/shard_map/all_to_all | solution.py:16
  22.9 37.6 %all-gather.2.cloned.1.call-done = bf16[12416,128]{1,0:T(8,128)(2,1)} async-done(((bf16[1552,128]{1,0:T(8,128)(2,1)}), bf16[12416,128]{1,0:T(8,128)(2,1)}) %all-gather.2.cloned.1.call-update) | async-done | bytes 3178512 | tf_op jit(solution)/shard_map/all_gather | solution.py:41
  60.6 3.1 %slice.40 = bf16[8,1024,128]{2,1,0:T(8,128)(2,1)} slice(bf16[8,1552,128]{2,1,0:T(8,128)(2,1)} %bitcast.74), slice={[0:8], [0:1024], [0:128]} | slice | bytes 4194304 | tf_op jit(solution)/shard_map/slice | solution.py:44
  64.6 3.8 %gather_fusion = bf16[64,128,128]{2,1,0:T(8,128)(2,1)} fusion(bf16[8,8,128,128]{3,2,1,0:T(8,128)(2,1)} %bitcast.7, s32[64]{0:T(128)S(1)} %reshape.188), kind=kCustom, calls=%fused_computation | custom fusion | bytes 4194816 | tf_op jit(solution)/shard_map/jit(take_along_axis)/gather | solution.py:63
  68.4 3.0 %fusion.1 = f32[8,8,128,128]{3,2,1,0:T(8,128)S(1)} fusion(bf16[8,8,128,128]{3,2,1,0:T(8,128)(2,1)} %bitcast.67, bf16[8,8,128,128]{3,2,1,0:T(8,128)(2,1)} %bitcast.71, pred[8,8]{1,0:T(8,128)(4,1)S(1)} %compare_and_fusion), kind=kOutput, calls=%fused_computation.7 | convolution fusion | flops 269484032 | bytes 8388672 | tf_op jit(solution)/shard_map/tsij,tsjf->tsif/dot_general | solution.py:64
  72.3 0.8 broadcast_in_dim.19
  73.1 4.1 %all-to-all-start.1 = ((bf16[8,256,128]{1,2,0:T(8,128)(2,1)}), bf16[8,256,128]{1,2,0:T(8,128)(2,1)}, u32[]{:S(2)}, u32[]{:S(2)}) async-start(bf16[8,256,128]{1,2,0:T(8,128)(2,1)} %broadcast_in_dim.19), calls=%async_computation.1 | async-start | bytes 1048576 | tf_op jit(solution)/shard_map/all_to_all | solution.py:16
  77.3 1.4 slice.42
  79.4 1.9 %convert_bitcast_fusion = bf16[8,2,8,128,128]{4,2,1,3,0:T(8,128)(2,1)S(1)} fusion(bf16[8,8,128,128]{3,2,1,0:T(8,128)(2,1)S(1)} %bitcast.68, s32[8,8]{1,0:T(8,128)S(1)} %bitcast.84), kind=kOutput, calls=%fused_computation.5 | convolution fusion | flops 35652608 | bytes 6291712 | tf_op jit(solution)/shard_map/tsp,tsij->tpij/dot_general | solution.py:53
  81.3 3.2 %copy.34 = bf16[8,2,8,128,128]{4,2,0,3,1:T(8,128)(2,1)} copy(bf16[8,2,8,128,128]{4,2,1,3,0:T(8,128)(2,1)S(1)} %convert_bitcast_fusion) | data formatting | bytes 8388608 | tf_op jit(solution)/shard_map/reshape | solution.py:56
  84.5 7.3 %reshape.179 = bf16[8192,256]{0,1:T(8,128)(2,1)} reshape(bf16[8,8,128,2,128]{2,1,0,4,3:T(8,128)(2,1)} %bitcast.69) | data formatting | bytes 8388608 | tf_op jit(solution)/shard_map/reshape | solution.py:72
  91.8 1.2 slice_convert_fusion.1
  93.0 2.1 %all-to-all-done.1 = bf16[8,256,128]{1,2,0:T(8,128)(2,1)} async-done(((bf16[8,256,128]{1,2,0:T(8,128)(2,1)}), bf16[8,256,128]{1,2,0:T(8,128)(2,1)}, u32[]{:S(2)}, u32[]{:S(2)}) %all-to-all-start.1) | async-done | bytes 524320 | tf_op jit(solution)/shard_map/all_to_all | solution.py:16
  95.1 1.9 %fusion.34 = f32[256,1024]{1,0:T(8,128)S(1)} fusion(bf16[256,1024]{0,1:T(8,128)(2,1)} %bitcast.16, bf16[1024,1024]{1,0:T(8,128)(2,1)S(1)} %copy-done), kind=kOutput, calls=%fused_computation.68 | convolution fusion | flops 536870912 | bytes 3670016 | tf_op jit(solution)/shard_map/dot_general | solution.py:81
  97.3 2.1 %fusion.4 = (bf16[256,1024]{1,0:T(8,128)(2,1)S(1)}, f32[256,1024]{1,0:T(8,128)}) fusion(f32[32,8,8,128]{3,2,1,0:T(8,128)S(1)} %bitcast.77, f32[256,1024]{1,0:T(8,128)S(1)} %fusion.34, bf16[1024,1024]{1,0:T(8,128)(2,1)S(1)} %copy-done.5, bf16[32,8,8,128]{3,2,1,0:T(8,128)(2,1)S(1)} %bitcast.80), kind=kOutput, calls=%fused_computation.16 | convolution fusion | flops 539492352 | bytes 6291456 | tf_op jit(solution)/shard_map/dot_general | solution.py:81
  99.9 0.9 fusion.9
  100.8 7.5 %all-to-all-start.2 = ((bf16[32,8,1024]{2,1,0:T(8,128)(2,1)}), bf16[32,8,1024]{2,1,0:T(8,128)(2,1)S(1)}, u32[]{:S(2)}, u32[]{:S(2)}) async-start(bf16[32,8,1024]{2,1,0:T(8,128)(2,1)} %fusion.9), calls=%async_computation.2 | async-start | bytes 1048576 | tf_op jit(solution)/shard_map/all_to_all | solution.py:22
  108.3 5.3 %convolution_convert_fusion = bf16[8192,128]{1,0:T(8,128)(2,1)} fusion(bf16[8192,256]{0,1:T(8,128)(2,1)} %reshape.179, bf16[256,1024]{1,0:T(8,128)(2,1)S(1)} %get-tuple-element.16, bf16[1024,1024]{1,0:T(8,128)(2,1)S(1)} %copy-done, s32[]{:T(128)S(6)} %select_n.68), kind=kOutput, calls=%fused_computation.1 | convolution fusion | flops 605061120 | bytes 7077892 | tf_op jit(solution)/shard_map/dot_general | solution.py:110
  113.6 3.4 %concatenate.10 = bf16[32,320,128]{2,1,0:T(8,128)(2,1)} pad(bf16[32,256,128]{2,1,0:T(8,128)(2,1)} %bitcast.70, bf16[]{:T(256)} %constant.51.clone.1), padding=0_0x0_64x0_0 | pad | bytes 4718594 | tf_op jit(solution)/shard_map/concatenate | solution.py:113
  117.1 1.2 fusion.15
  118.3 1.6 all-to-all-done.2
  120.0 1.0 broadcast_dynamic-update-slice_fusion
  121.0 5.9 %all-to-all-start.3 = ((bf16[32,320,128]{2,1,0:T(8,128)(2,1)}), bf16[32,320,128]{2,1,0:T(8,128)(2,1)}, u32[]{:S(2)}, u32[]{:S(2)}) async-start(bf16[32,320,128]{2,1,0:T(8,128)(2,1)} %broadcast_dynamic-update-slice_fusion), calls=%async_computation.3 | async-start | bytes 5242880 | tf_op jit(solution)/shard_map/all_to_all | solution.py:118
  126.9 1.6 multiply_convert_fusion
  128.5 32.4 %all-to-all-done.3 = bf16[32,320,128]{2,1,0:T(8,128)(2,1)} async-done(((bf16[32,320,128]{2,1,0:T(8,128)(2,1)}), bf16[32,320,128]{2,1,0:T(8,128)(2,1)}, u32[]{:S(2)}, u32[]{:S(2)}) %all-to-all-start.3) | async-done | bytes 2621472 | tf_op jit(solution)/shard_map/all_to_all | solution.py:118
  160.9 1.1 slice_convert_fusion
  162.1 0.9 reshape.183
  163.0 0.9 reshape.184
  163.9 1.9 %convert_reduce_fusion = f32[256,128]{1,0:T(8,128)S(1)} fusion(bf16[32,320,128]{2,1,0:T(8,128)(2,1)} %all-to-all-done.3), kind=kLoop, calls=%fused_computation.4 | loop fusion | flops 2064384 | bytes 2228224 | tf_op jit(solution)/shard_map/reduce_sum | solution.py:119
  (33 shorter events, 5.0 us)
Async XLA Ops:
  7.2 87.9 %copy-start = (bf16[1024,1024]{1,0:T(8,128)(2,1)S(1)}, bf16[1024,1024]{1,0:T(8,128)(2,1)}, u32[]{:S(2)}) copy-start(bf16[1024,1024]{1,0:T(8,128)(2,1)} %param.9) | copy-start | bytes 6291460
  7.2 53.4 %all-gather.2.cloned.1.call-start = ((), (), s32[]{:S(2)}) async-start(), calls=%async_computation.4 | async-start | bytes 3575808 | tf_op jit(solution)/shard_map/all_gather | solution.py:41
  14.3 50.3 %all-to-all-start = ((bf16[32,256,128]{2,1,0:T(8,128)(2,1)}), bf16[32,256,128]{2,1,0:T(8,128)(2,1)}, u32[]{:S(2)}, u32[]{:S(2)}) async-start(bf16[32,256,128]{2,1,0:T(8,128)(2,1)} %broadcast_in_dim.17), calls=%async_computation | async-start | bytes 4194304 | tf_op jit(solution)/shard_map/all_to_all | solution.py:16
  73.1 22.0 %all-to-all-start.1 = ((bf16[8,256,128]{1,2,0:T(8,128)(2,1)}), bf16[8,256,128]{1,2,0:T(8,128)(2,1)}, u32[]{:S(2)}, u32[]{:S(2)}) async-start(bf16[8,256,128]{1,2,0:T(8,128)(2,1)} %broadcast_in_dim.19), calls=%async_computation.1 | async-start | bytes 1048576 | tf_op jit(solution)/shard_map/all_to_all | solution.py:16
  77.3 2.2 %copy-start.1 = (bf16[8,1024,128]{2,1,0:T(8,128)(2,1)S(1)}, bf16[8,1024,128]{2,1,0:T(8,128)(2,1)}, u32[]{:S(2)}) copy-start(bf16[8,1024,128]{2,1,0:T(8,128)(2,1)} %slice.40) | copy-start | bytes 6291460
  95.1 1.9 %copy-start.2 = (f32[1,256,8,128]{3,2,1,0:T(8,128)S(1)}, f32[1,256,8,128]{3,2,1,0:T(8,128)}, u32[]{:S(2)}) copy-start(f32[1,256,8,128]{3,2,1,0:T(8,128)} %get-tuple-element.14) | copy-start | bytes 3145732
  95.1 1.9 %copy-start.4 = (bf16[1,256,8,128]{3,2,1,0:T(8,128)(2,1)S(1)}, bf16[1,256,8,128]{3,2,1,0:T(8,128)(2,1)}, u32[]{:S(2)}) copy-start(bf16[1,256,8,128]{3,2,1,0:T(8,128)(2,1)} %get-tuple-element.15) | copy-start | bytes 1572868
  95.1 2.2 %copy-start.5 = (bf16[1024,1024]{1,0:T(8,128)(2,1)S(1)}, bf16[1024,1024]{1,0:T(8,128)(2,1)}, u32[]{:S(2)}) copy-start(bf16[1024,1024]{1,0:T(8,128)(2,1)} %param.10) | copy-start | bytes 6291460
  97.3 2.1 %copy-start.3 = (bf16[256,128]{1,0:T(8,128)(2,1)S(1)}, bf16[256,128]{1,0:T(8,128)(2,1)}, u32[]{:S(2)}) copy-start(bf16[256,128]{1,0:T(8,128)(2,1)} %param.7) | copy-start | bytes 196612
  100.8 19.1 %all-to-all-start.2 = ((bf16[32,8,1024]{2,1,0:T(8,128)(2,1)}), bf16[32,8,1024]{2,1,0:T(8,128)(2,1)S(1)}, u32[]{:S(2)}, u32[]{:S(2)}) async-start(bf16[32,8,1024]{2,1,0:T(8,128)(2,1)} %fusion.9), calls=%async_computation.2 | async-start | bytes 1048576 | tf_op jit(solution)/shard_map/all_to_all | solution.py:22
  121.0 39.9 %all-to-all-start.3 = ((bf16[32,320,128]{2,1,0:T(8,128)(2,1)}), bf16[32,320,128]{2,1,0:T(8,128)(2,1)}, u32[]{:S(2)}, u32[]{:S(2)}) async-start(bf16[32,320,128]{2,1,0:T(8,128)(2,1)} %broadcast_dynamic-update-slice_fusion), calls=%async_computation.3 | async-start | bytes 5242880 | tf_op jit(solution)/shard_map/all_to_all | solution.py:118
Sparse Core Ops, SparseCore 0:
  11.7 48.8 all-gather.1

commit v13 on v11

--- a/solution.py
+++ b/solution.py
@@ -100,8 +100,15 @@
     grad_scale = 1.0 / math.sqrt(nodes)
     both = jnp.concatenate([weight_part, root_part], axis=0) * grad_scale
     both_sum = reduce_rows(both.astype(jnp.bfloat16), "row", row_count)
+    sum_rows, sum_cols = both_sum.shape
+    lane_tiles = sum_cols // block_edge
     sum_lanes = both_sum.size // block_edge
-    sum_pair = both_sum.astype(jnp.bfloat16).reshape(sum_lanes, block_edge)
+    sum_pair = (
+        both_sum.astype(jnp.bfloat16)
+        .reshape(sum_rows, lane_tiles, block_edge)
+        .transpose(1, 0, 2)
+        .reshape(sum_lanes, block_edge)
+    )
 
     w_rows = lax.dynamic_slice_in_dim(weight, col_index * feat_dev, feat_dev, 0)
     r_rows = lax.dynamic_slice_in_dim(root_weight, col_index * feat_dev, feat_dev, 0)
@@ -122,7 +129,12 @@
     )
     incoming = lax.all_to_all(outgoing, "row", 0, 0, tiled=True)
     summed_cols = incoming[:, :node_rows].astype(jnp.float32).sum(0)
-    got_sums = incoming[:, node_rows:].astype(jnp.float32)
+    got_sums = (
+        incoming[:, node_rows:]
+        .reshape(row_count, lane_tiles, sum_rows, block_edge)
+        .transpose(0, 2, 1, 3)
+        .astype(jnp.float32)
+    )
     half = row_count // 2
     weight_sum = got_sums[:half].reshape(feat_dev, -1)
     root_sum = got_sums[half:].reshape(feat_dev, -1)

time: 174 us -> 173 us (level)
  no operation moved by 1% of the time
where the time goes in v13:
time: 173 us; the launch traced here: 172 us
  waiting for transfers between devices  72.8 us (42%)
  starting transfers between devices  26.3 us (15%)
  local copies, waits for them, and re-layouts  25.4 us (15%)
  matrix products  21 us (12%)
  between operations  15 us (9%)
  other arithmetic  11.7 us (7%)
    all_gather x1, waiting for transfers between devices, per_device(): lax.all_gather(packed, 'col', axis=0, tiled=True)  37.6 us
    all_to_all x1, waiting for transfers between devices, per_device(): incoming = lax.all_to_all(outgoing, 'row', 0, 0, tiled=True)  32.4 us
    all_to_all x2, starting transfers between devices, gather_rows(): got = lax.all_to_all(spread, axis_name, 0, 0, tiled=True)  13 us
    all_to_all x1, starting transfers between devices, reduce_rows(): got = lax.all_to_all(pieces, axis_name, 0, 0, tiled=True)  7.41 us
    reshape x1, local copies, waits for them, and re-layouts, per_device(): dense_t = jnp.transpose(dense, (0, 2, 4, 1, 3)).reshape(nodes, node_rows)  7.32 us
    all_to_all x1, starting transfers between devices, per_device(): incoming = lax.all_to_all(outgoing, 'row', 0, 0, tiled=True)  5.88 us
    dot_general x1, matrix products, per_device(): jnp.dot(dense_t, aggregated_grad, preferred_element_type=jnp.float32)  5.31 us
    dot_general x1, matrix products, per_device(): jnp.einsum('tsr,tsif->rif', row_hot, products, precision=lax.Precision.HI...  4.21 us
  transfers between devices with their start and end apart: 5, of which 4 were waited for; matrix products, arithmetic and copies ran while one was open for 20% of the time, Pallas kernels for 0%

profile of v13, /device:TPU:1, one launch (start us, length us, event | category | flops | bytes accessed | tf_op | source)
XLA Modules:
  0.0 172.2 jit_solution(908833760072933062)
XLA Ops:
  8.8 1.1 bitcast_multiply_fusion.1
  9.9 1.6 fusion.21
  11.6 2.7 %broadcast_in_dim.8 = bf16[32,256,128]{2,1,0:T(8,128)(2,1)} broadcast(bf16[256,128]{1,0:T(8,128)(2,1)} %param.7), dimensions={1,2} | broadcast | bytes 2162688 | tf_op jit(solution)/shard_map/broadcast_in_dim | solution.py:15
  14.3 8.6 %all-to-all-start = ((bf16[32,256,128]{2,1,0:T(8,128)(2,1)}), bf16[32,256,128]{2,1,0:T(8,128)(2,1)}, u32[]{:S(2)}, u32[]{:S(2)}) async-start(bf16[32,256,128]{2,1,0:T(8,128)(2,1)} %broadcast_in_dim.8), calls=%async_computation | async-start | bytes 4194304 | tf_op jit(solution)/shard_map/all_to_all | solution.py:16
  22.9 37.6 %all-gather.2.cloned.1.call-done = bf16[12416,128]{1,0:T(8,128)(2,1)} async-done(((bf16[1552,128]{1,0:T(8,128)(2,1)}), bf16[12416,128]{1,0:T(8,128)(2,1)}) %all-gather.2.cloned.1.call-update) | async-done | bytes 3178512 | tf_op jit(solution)/shard_map/all_gather | solution.py:41
  60.6 3.1 %slice.39 = bf16[8,1024,128]{2,1,0:T(8,128)(2,1)} slice(bf16[8,1552,128]{2,1,0:T(8,128)(2,1)} %bitcast.98), slice={[0:8], [0:1024], [0:128]} | slice | bytes 4194304 | tf_op jit(solution)/shard_map/slice | solution.py:44
  63.7 0.7 slice_convert_fusion.1
  64.5 3.1 %fusion.3 = bf16[8,8,128,128]{3,1,2,0:T(8,128)(2,1)S(1)} fusion(bf16[8,8,128,128]{3,2,1,0:T(8,128)(2,1)} %bitcast.10, s32[8,8]{1,0:T(8,128)S(1)} %get-tuple-element.17), kind=kOutput, calls=%fused_computation.8 | convolution fusion | flops 16777728 | bytes 4194560 | tf_op jit(solution)/shard_map/tsc,tcjf->tsjf/dot_general | solution.py:66
  68.3 4.2 %fusion.9 = bf16[2,128,128]{2,0,1:T(2,128)(2,1)S(1)} fusion(f32[8,8,128,128]{3,2,1,0:T(8,128)S(1)} %fusion.2, s32[8,8]{0,1:T(8,128)S(1)} %copy.12), kind=kOutput, calls=%fused_computation.16 | convolution fusion | flops 25198720 | bytes 4260096 | tf_op jit(solution)/shard_map/tsr,tsif->rif/dot_general | solution.py:72
  72.6 0.8 broadcast_in_dim.9
  73.5 4.3 %all-to-all-start.1 = ((bf16[8,256,128]{1,2,0:T(8,128)(2,1)}), bf16[8,256,128]{1,2,0:T(8,128)(2,1)}, u32[]{:S(2)}, u32[]{:S(2)}) async-start(bf16[8,256,128]{1,2,0:T(8,128)(2,1)} %broadcast_in_dim.9), calls=%async_computation.1 | async-start | bytes 1048576 | tf_op jit(solution)/shard_map/all_to_all | solution.py:16
  77.8 1.4 slice.40
  80.0 1.9 %convert_bitcast_fusion = bf16[8,2,8,128,128]{4,2,1,3,0:T(8,128)(2,1)S(1)} fusion(bf16[8,8,128,128]{3,2,1,0:T(8,128)(2,1)S(1)} %bitcast.93, s32[8,8]{1,0:T(8,128)S(1)} %bitcast.107), kind=kOutput, calls=%fused_computation.6 | convolution fusion | flops 35652608 | bytes 6291712 | tf_op jit(solution)/shard_map/tsp,tsij->tpij/dot_general | solution.py:53
  81.8 3.2 %copy.47 = bf16[8,2,8,128,128]{4,2,0,3,1:T(8,128)(2,1)} copy(bf16[8,2,8,128,128]{4,2,1,3,0:T(8,128)(2,1)S(1)} %convert_bitcast_fusion) | data formatting | bytes 8388608 | tf_op jit(solution)/shard_map/reshape | solution.py:56
  85.0 7.3 %reshape.124 = bf16[8192,256]{0,1:T(8,128)(2,1)} reshape(bf16[8,8,128,2,128]{2,1,0,4,3:T(8,128)(2,1)} %bitcast.94) | data formatting | bytes 8388608 | tf_op jit(solution)/shard_map/reshape | solution.py:77
  92.3 1.3 slice_convert_fusion
  93.6 1.2 all-to-all-done.1
  94.8 1.9 %fusion.41 = f32[256,1024]{1,0:T(8,128)S(1)} fusion(bf16[256,1024]{0,1:T(8,128)(2,1)} %bitcast.19, bf16[1024,1024]{1,0:T(8,128)(2,1)S(1)} %copy-done), kind=kOutput, calls=%fused_computation.66 | convolution fusion | flops 536870912 | bytes 3670016 | tf_op jit(solution)/shard_map/dot_general | solution.py:86
  97.0 2.1 %fusion.12 = (bf16[256,1024]{1,0:T(8,128)(2,1)S(1)}, f32[256,1024]{1,0:T(8,128)}) fusion(f32[32,8,8,128]{3,2,1,0:T(8,128)S(1)} %bitcast.101, f32[256,1024]{1,0:T(8,128)S(1)} %fusion.41, bf16[1024,1024]{1,0:T(8,128)(2,1)S(1)} %copy-done.6, bf16[32,8,8,128]{3,2,1,0:T(8,128)(2,1)S(1)} %bitcast.104), kind=kOutput, calls=%fused_computation.19 | convolution fusion | flops 539492352 | bytes 6291456 | tf_op jit(solution)/shard_map/dot_general | solution.py:86
  99.7 0.9 fusion.16
  100.5 7.4 %all-to-all-start.2 = ((bf16[32,8,1024]{2,1,0:T(8,128)(2,1)}), bf16[32,8,1024]{2,1,0:T(8,128)(2,1)S(1)}, u32[]{:S(2)}, u32[]{:S(2)}) async-start(bf16[32,8,1024]{2,1,0:T(8,128)(2,1)} %fusion.16), calls=%async_computation.2 | async-start | bytes 1048576 | tf_op jit(solution)/shard_map/all_to_all | solution.py:22
  108.0 5.3 %convolution_convert_fusion = bf16[8192,128]{1,0:T(8,128)(2,1)} fusion(bf16[8192,256]{0,1:T(8,128)(2,1)} %reshape.124, bf16[256,1024]{1,0:T(8,128)(2,1)S(1)} %get-tuple-element.18, bf16[1024,1024]{1,0:T(8,128)(2,1)S(1)} %copy-done, s32[]{:T(128)S(6)} %select_n.27), kind=kOutput, calls=%fused_computation | convolution fusion | flops 605061120 | bytes 7077892 | tf_op jit(solution)/shard_map/dot_general | solution.py:122
  113.3 3.5 %concatenate.10 = bf16[32,320,128]{2,1,0:T(8,128)(2,1)} pad(bf16[32,256,128]{2,1,0:T(8,128)(2,1)} %bitcast.95, bf16[]{:T(256)} %constant.37.clone.1), padding=0_0x0_64x0_0 | pad | bytes 4718594 | tf_op jit(solution)/shard_map/concatenate | solution.py:125
  116.7 1.2 fusion.22
  118.0 1.6 all-to-all-done.2
  119.7 1.0 broadcast_dynamic-update-slice_fusion
  120.7 5.9 %all-to-all-start.3 = ((bf16[32,320,128]{2,1,0:T(8,128)(2,1)}), bf16[32,320,128]{2,1,0:T(8,128)(2,1)}, u32[]{:S(2)}, u32[]{:S(2)}) async-start(bf16[32,320,128]{2,1,0:T(8,128)(2,1)} %broadcast_dynamic-update-slice_fusion), calls=%async_computation.3 | async-start | bytes 5242880 | tf_op jit(solution)/shard_map/all_to_all | solution.py:130
  126.6 1.6 multiply_convert_fusion
  128.2 32.4 %all-to-all-done.3 = bf16[32,320,128]{2,1,0:T(8,128)(2,1)} async-done(((bf16[32,320,128]{2,1,0:T(8,128)(2,1)}), bf16[32,320,128]{2,1,0:T(8,128)(2,1)}, u32[]{:S(2)}, u32[]{:S(2)}) %all-to-all-start.3) | async-done | bytes 2621472 | tf_op jit(solution)/shard_map/all_to_all | solution.py:130
  160.5 1.1 convert_bitcast_fusion.1
  161.7 1.1 slice_bitcast_fusion
  162.8 1.9 %convert_reduce_fusion = f32[256,128]{1,0:T(8,128)S(1)} fusion(bf16[32,320,128]{2,1,0:T(8,128)(2,1)} %all-to-all-done.3), kind=kLoop, calls=%fused_computation.5 | loop fusion | flops 2064384 | bytes 2228224 | tf_op jit(solution)/shard_map/reduce_sum | solution.py:131
  (30 shorter events, 4.0 us)
Async XLA Ops:
  7.2 87.6 %copy-start = (bf16[1024,1024]{1,0:T(8,128)(2,1)S(1)}, bf16[1024,1024]{1,0:T(8,128)(2,1)}, u32[]{:S(2)}) copy-start(bf16[1024,1024]{1,0:T(8,128)(2,1)} %param.9) | copy-start | bytes 6291460
  7.2 53.4 %all-gather.2.cloned.1.call-start = ((), (), s32[]{:S(2)}) async-start(), calls=%async_computation.4 | async-start | bytes 3575808 | tf_op jit(solution)/shard_map/all_gather | solution.py:41
  14.3 50.2 %all-to-all-start = ((bf16[32,256,128]{2,1,0:T(8,128)(2,1)}), bf16[32,256,128]{2,1,0:T(8,128)(2,1)}, u32[]{:S(2)}, u32[]{:S(2)}) async-start(bf16[32,256,128]{2,1,0:T(8,128)(2,1)} %broadcast_in_dim.8), calls=%async_computation | async-start | bytes 4194304 | tf_op jit(solution)/shard_map/all_to_all | solution.py:16
  64.5 3.1 %copy-start.1 = (bf16[8,1024,128]{2,1,0:T(8,128)(2,1)S(1)}, bf16[8,1024,128]{2,1,0:T(8,128)(2,1)}, u32[]{:S(2)}) copy-start(bf16[8,1024,128]{2,1,0:T(8,128)(2,1)} %slice.39) | copy-start | bytes 6291460
  73.5 21.3 %all-to-all-start.1 = ((bf16[8,256,128]{1,2,0:T(8,128)(2,1)}), bf16[8,256,128]{1,2,0:T(8,128)(2,1)}, u32[]{:S(2)}, u32[]{:S(2)}) async-start(bf16[8,256,128]{1,2,0:T(8,128)(2,1)} %broadcast_in_dim.9), calls=%async_computation.1 | async-start | bytes 1048576 | tf_op jit(solution)/shard_map/all_to_all | solution.py:16
  77.8 2.2 %copy-start.2 = (bf16[8,1024,128]{2,1,0:T(8,128)(2,1)S(1)}, bf16[8,1024,128]{2,1,0:T(8,128)(2,1)}, u32[]{:S(2)}) copy-start(bf16[8,1024,128]{2,1,0:T(8,128)(2,1)} %slice.39) | copy-start | bytes 6291460
  94.8 1.9 %copy-start.3 = (f32[1,256,8,128]{3,2,1,0:T(8,128)S(1)}, f32[1,256,8,128]{3,2,1,0:T(8,128)}, u32[]{:S(2)}) copy-start(f32[1,256,8,128]{3,2,1,0:T(8,128)} %get-tuple-element.14) | copy-start | bytes 3145732
  94.8 1.9 %copy-start.5 = (bf16[1,256,8,128]{3,2,1,0:T(8,128)(2,1)S(1)}, bf16[1,256,8,128]{3,2,1,0:T(8,128)(2,1)}, u32[]{:S(2)}) copy-start(bf16[1,256,8,128]{3,2,1,0:T(8,128)(2,1)} %get-tuple-element.15) | copy-start | bytes 1572868
  94.8 2.2 %copy-start.6 = (bf16[1024,1024]{1,0:T(8,128)(2,1)S(1)}, bf16[1024,1024]{1,0:T(8,128)(2,1)}, u32[]{:S(2)}) copy-start(bf16[1024,1024]{1,0:T(8,128)(2,1)} %param.10) | copy-start | bytes 6291460
  97.0 2.4 %copy-start.4 = (bf16[256,128]{1,0:T(8,128)(2,1)S(1)}, bf16[256,128]{1,0:T(8,128)(2,1)}, u32[]{:S(2)}) copy-start(bf16[256,128]{1,0:T(8,128)(2,1)} %param.7) | copy-start | bytes 196612
  100.5 19.0 %all-to-all-start.2 = ((bf16[32,8,1024]{2,1,0:T(8,128)(2,1)}), bf16[32,8,1024]{2,1,0:T(8,128)(2,1)S(1)}, u32[]{:S(2)}, u32[]{:S(2)}) async-start(bf16[32,8,1024]{2,1,0:T(8,128)(2,1)} %fusion.16), calls=%async_computation.2 | async-start | bytes 1048576 | tf_op jit(solution)/shard_map/all_to_all | solution.py:22
  120.7 39.9 %all-to-all-start.3 = ((bf16[32,320,128]{2,1,0:T(8,128)(2,1)}), bf16[32,320,128]{2,1,0:T(8,128)(2,1)}, u32[]{:S(2)}, u32[]{:S(2)}) async-start(bf16[32,320,128]{2,1,0:T(8,128)(2,1)} %broadcast_dynamic-update-slice_fusion), calls=%async_computation.3 | async-start | bytes 5242880 | tf_op jit(solution)/shard_map/all_to_all | solution.py:130
Sparse Core Ops, SparseCore 0:
  11.7 48.8 all-gather.1

commit v14 on v13

--- a/solution.py
+++ b/solution.py
@@ -69,7 +69,7 @@
     products = jnp.einsum(
         "tsij,tsjf->tsif", tile_vals, chosen, preferred_element_type=jnp.float32
     )
-    agg_f32 = jnp.einsum("tsr,tsif->rif", row_hot, products, precision=lax.Precision.HIGHEST)
+    agg_f32 = jnp.sum(products[:, :, None] * row_hot[:, :, :, None, None], axis=(0, 1))
     aggregated = agg_f32.reshape(node_rows, feat_dev).astype(jnp.bfloat16)
 
     agg_parts = gather_rows(aggregated, "col", col_count).reshape(col_count, node_rows, feat_dev)

time: 173 us -> 170 us (0.983)
  matrix products: 21 us -> 16.7 us
    dot_general x1 -> x0, matrix products: 4.21 us -> none  [per_device(): jnp.einsum('tsr,tsif->rif', row_hot, products, precision=lax.Precision.HI...]
where the time goes in v14:
time: 170 us; the launch traced here: 169 us
  waiting for transfers between devices  73.7 us (43%)
  starting transfers between devices  26.1 us (15%)
  local copies, waits for them, and re-layouts  25.2 us (15%)
  matrix products  16.7 us (10%)
  between operations  14.9 us (9%)
  other arithmetic  12.7 us (7%)
    all_gather x1, waiting for transfers between devices, per_device(): lax.all_gather(packed, 'col', axis=0, tiled=True)  37.6 us
    all_to_all x1, waiting for transfers between devices, per_device(): incoming = lax.all_to_all(outgoing, 'row', 0, 0, tiled=True)  32.4 us
    all_to_all x2, starting transfers between devices, gather_rows(): got = lax.all_to_all(spread, axis_name, 0, 0, tiled=True)  12.8 us
    all_to_all x1, starting transfers between devices, reduce_rows(): got = lax.all_to_all(pieces, axis_name, 0, 0, tiled=True)  7.45 us
    reshape x1, local copies, waits for them, and re-layouts, per_device(): dense_t = jnp.transpose(dense, (0, 2, 4, 1, 3)).reshape(nodes, node_rows)  7.3 us
    all_to_all x1, starting transfers between devices, per_device(): incoming = lax.all_to_all(outgoing, 'row', 0, 0, tiled=True)  5.88 us
    dot_general x1, matrix products, per_device(): jnp.dot(dense_t, aggregated_grad, preferred_element_type=jnp.float32)  5.32 us
    broadcast_in_dim x2, local copies, waits for them, and re-layouts, gather_rows(): spread = jnp.broadcast_to(block[None], (parts,) + block.shape)  3.54 us
  transfers between devices with their start and end apart: 5, of which 4 were waited for; matrix products, arithmetic and copies ran while one was open for 20% of the time, Pallas kernels for 0%

profile of v14, /device:TPU:1, one launch (start us, length us, event | category | flops | bytes accessed | tf_op | source)
XLA Modules:
  0.0 169.3 jit_solution(5242020450863528833)
XLA Ops:
  7.2 0.8 convert_bitcast_fusion.2
  8.8 1.1 bitcast_multiply_fusion.1
  9.9 1.6 fusion.17
  11.6 2.7 %broadcast_in_dim.8 = bf16[32,256,128]{2,1,0:T(8,128)(2,1)} broadcast(bf16[256,128]{1,0:T(8,128)(2,1)} %param.7), dimensions={1,2} | broadcast | bytes 2162688 | tf_op jit(solution)/shard_map/broadcast_in_dim | solution.py:15
  14.3 8.6 %all-to-all-start = ((bf16[32,256,128]{2,1,0:T(8,128)(2,1)}), bf16[32,256,128]{2,1,0:T(8,128)(2,1)}, u32[]{:S(2)}, u32[]{:S(2)}) async-start(bf16[32,256,128]{2,1,0:T(8,128)(2,1)} %broadcast_in_dim.8), calls=%async_computation | async-start | bytes 4194304 | tf_op jit(solution)/shard_map/all_to_all | solution.py:16
  22.9 37.6 %all-gather.2.cloned.1.call-done = bf16[12416,128]{1,0:T(8,128)(2,1)} async-done(((bf16[1552,128]{1,0:T(8,128)(2,1)}), bf16[12416,128]{1,0:T(8,128)(2,1)}) %all-gather.2.cloned.1.call-update) | async-done | bytes 3178512 | tf_op jit(solution)/shard_map/all_gather | solution.py:41
  60.6 3.1 %slice.38 = bf16[8,1024,128]{2,1,0:T(8,128)(2,1)} slice(bf16[8,1552,128]{2,1,0:T(8,128)(2,1)} %bitcast.90), slice={[0:8], [0:1024], [0:128]} | slice | bytes 4194304 | tf_op jit(solution)/shard_map/slice | solution.py:44
  63.7 0.7 slice_convert_fusion.1
  64.5 3.1 %fusion.5 = bf16[8,8,128,128]{3,1,2,0:T(8,128)(2,1)S(1)} fusion(bf16[8,8,128,128]{3,2,1,0:T(8,128)(2,1)} %bitcast.9, s32[8,8]{1,0:T(8,128)S(1)} %get-tuple-element.16), kind=kOutput, calls=%fused_computation.10 | convolution fusion | flops 17826304 | bytes 4194560 | tf_op jit(solution)/shard_map/tsc,tcjf->tsjf/dot_general | solution.py:66
  69.1 0.8 broadcast_in_dim.9
  70.0 4.1 %all-to-all-start.1 = ((bf16[8,256,128]{1,2,0:T(8,128)(2,1)}), bf16[8,256,128]{1,2,0:T(8,128)(2,1)}, u32[]{:S(2)}, u32[]{:S(2)}) async-start(bf16[8,256,128]{1,2,0:T(8,128)(2,1)} %broadcast_in_dim.9), calls=%async_computation.1 | async-start | bytes 1048576 | tf_op jit(solution)/shard_map/all_to_all | solution.py:16
  74.1 1.4 slice.40
  76.3 1.9 %convert_bitcast_fusion = bf16[8,2,8,128,128]{4,2,1,3,0:T(8,128)(2,1)S(1)} fusion(bf16[8,8,128,128]{3,2,1,0:T(8,128)(2,1)S(1)} %bitcast.85, s32[8,8]{1,0:T(8,128)S(1)} %bitcast.99), kind=kOutput, calls=%fused_computation.4 | convolution fusion | flops 35652608 | bytes 6291712 | tf_op jit(solution)/shard_map/tsp,tsij->tpij/dot_general | solution.py:53
  78.2 3.2 %copy.48 = bf16[8,2,8,128,128]{4,2,0,3,1:T(8,128)(2,1)} copy(bf16[8,2,8,128,128]{4,2,1,3,0:T(8,128)(2,1)S(1)} %convert_bitcast_fusion) | data formatting | bytes 8388608 | tf_op jit(solution)/shard_map/reshape | solution.py:56
  81.4 7.3 %reshape.129 = bf16[8192,256]{0,1:T(8,128)(2,1)} reshape(bf16[8,8,128,2,128]{2,1,0,4,3:T(8,128)(2,1)} %bitcast.86) | data formatting | bytes 8388608 | tf_op jit(solution)/shard_map/reshape | solution.py:77
  88.7 1.2 slice_convert_fusion
  89.9 2.1 %all-to-all-done.1 = bf16[8,256,128]{1,2,0:T(8,128)(2,1)} async-done(((bf16[8,256,128]{1,2,0:T(8,128)(2,1)}), bf16[8,256,128]{1,2,0:T(8,128)(2,1)}, u32[]{:S(2)}, u32[]{:S(2)}) %all-to-all-start.1) | async-done | bytes 524320 | tf_op jit(solution)/shard_map/all_to_all | solution.py:16
  92.0 1.9 %fusion.34 = f32[256,1024]{1,0:T(8,128)S(1)} fusion(bf16[256,1024]{0,1:T(8,128)(2,1)} %bitcast.16, bf16[1024,1024]{1,0:T(8,128)(2,1)S(1)} %copy-done), kind=kOutput, calls=%fused_computation.62 | convolution fusion | flops 536870912 | bytes 3670016 | tf_op jit(solution)/shard_map/dot_general | solution.py:86
  94.2 2.1 %fusion.8 = (bf16[256,1024]{1,0:T(8,128)(2,1)S(1)}, f32[256,1024]{1,0:T(8,128)}) fusion(f32[32,8,8,128]{3,2,1,0:T(8,128)S(1)} %bitcast.93, f32[256,1024]{1,0:T(8,128)S(1)} %fusion.34, bf16[1024,1024]{1,0:T(8,128)(2,1)S(1)} %copy-done.6, bf16[32,8,8,128]{3,2,1,0:T(8,128)(2,1)S(1)} %bitcast.96), kind=kOutput, calls=%fused_computation.17 | convolution fusion | flops 539492352 | bytes 6291456 | tf_op jit(solution)/shard_map/dot_general | solution.py:86
  96.8 0.9 fusion.12
  97.7 7.5 %all-to-all-start.2 = ((bf16[32,8,1024]{2,1,0:T(8,128)(2,1)}), bf16[32,8,1024]{2,1,0:T(8,128)(2,1)S(1)}, u32[]{:S(2)}, u32[]{:S(2)}) async-start(bf16[32,8,1024]{2,1,0:T(8,128)(2,1)} %fusion.12), calls=%async_computation.2 | async-start | bytes 1048576 | tf_op jit(solution)/shard_map/all_to_all | solution.py:22
  105.2 5.3 %convolution_convert_fusion = bf16[8192,128]{1,0:T(8,128)(2,1)} fusion(bf16[8192,256]{0,1:T(8,128)(2,1)} %reshape.129, bf16[256,1024]{1,0:T(8,128)(2,1)S(1)} %get-tuple-element.18, bf16[1024,1024]{1,0:T(8,128)(2,1)S(1)} %copy-done, s32[]{:T(128)S(6)} %select_n.27), kind=kOutput, calls=%fused_computation | convolution fusion | flops 605061120 | bytes 7077892 | tf_op jit(solution)/shard_map/dot_general | solution.py:122
  110.5 3.5 %concatenate.10 = bf16[32,320,128]{2,1,0:T(8,128)(2,1)} pad(bf16[32,256,128]{2,1,0:T(8,128)(2,1)} %bitcast.87, bf16[]{:T(256)} %constant.37.clone.1), padding=0_0x0_64x0_0 | pad | bytes 4718594 | tf_op jit(solution)/shard_map/concatenate | solution.py:125
  113.9 1.2 fusion.18
  115.2 1.6 all-to-all-done.2
  116.9 0.9 broadcast_dynamic-update-slice_fusion
  117.8 5.9 %all-to-all-start.3 = ((bf16[32,320,128]{2,1,0:T(8,128)(2,1)}), bf16[32,320,128]{2,1,0:T(8,128)(2,1)}, u32[]{:S(2)}, u32[]{:S(2)}) async-start(bf16[32,320,128]{2,1,0:T(8,128)(2,1)} %broadcast_dynamic-update-slice_fusion), calls=%async_computation.3 | async-start | bytes 5242880 | tf_op jit(solution)/shard_map/all_to_all | solution.py:130
  123.7 1.6 multiply_convert_fusion
  125.3 32.4 %all-to-all-done.3 = bf16[32,320,128]{2,1,0:T(8,128)(2,1)} async-done(((bf16[32,320,128]{2,1,0:T(8,128)(2,1)}), bf16[32,320,128]{2,1,0:T(8,128)(2,1)}, u32[]{:S(2)}, u32[]{:S(2)}) %all-to-all-start.3) | async-done | bytes 2621472 | tf_op jit(solution)/shard_map/all_to_all | solution.py:130
  157.7 1.1 convert_bitcast_fusion.1
  158.8 1.1 slice_bitcast_fusion
  159.9 1.9 %convert_reduce_fusion = f32[256,128]{1,0:T(8,128)S(1)} fusion(bf16[32,320,128]{2,1,0:T(8,128)(2,1)} %all-to-all-done.3), kind=kLoop, calls=%fused_computation.3 | loop fusion | flops 2064384 | bytes 2228224 | tf_op jit(solution)/shard_map/reduce_sum | solution.py:131
  (29 shorter events, 4.0 us)
Async XLA Ops:
  7.2 84.8 %copy-start = (bf16[1024,1024]{1,0:T(8,128)(2,1)S(1)}, bf16[1024,1024]{1,0:T(8,128)(2,1)}, u32[]{:S(2)}) copy-start(bf16[1024,1024]{1,0:T(8,128)(2,1)} %param.9) | copy-start | bytes 6291460
  7.2 53.4 %all-gather.2.cloned.1.call-start = ((), (), s32[]{:S(2)}) async-start(), calls=%async_computation.4 | async-start | bytes 3575808 | tf_op jit(solution)/shard_map/all_gather | solution.py:41
  14.3 50.2 %all-to-all-start = ((bf16[32,256,128]{2,1,0:T(8,128)(2,1)}), bf16[32,256,128]{2,1,0:T(8,128)(2,1)}, u32[]{:S(2)}, u32[]{:S(2)}) async-start(bf16[32,256,128]{2,1,0:T(8,128)(2,1)} %broadcast_in_dim.8), calls=%async_computation | async-start | bytes 4194304 | tf_op jit(solution)/shard_map/all_to_all | solution.py:16
  64.5 3.1 %copy-start.1 = (bf16[8,1024,128]{2,1,0:T(8,128)(2,1)S(1)}, bf16[8,1024,128]{2,1,0:T(8,128)(2,1)}, u32[]{:S(2)}) copy-start(bf16[8,1024,128]{2,1,0:T(8,128)(2,1)} %slice.38) | copy-start | bytes 6291460
  70.0 22.0 %all-to-all-start.1 = ((bf16[8,256,128]{1,2,0:T(8,128)(2,1)}), bf16[8,256,128]{1,2,0:T(8,128)(2,1)}, u32[]{:S(2)}, u32[]{:S(2)}) async-start(bf16[8,256,128]{1,2,0:T(8,128)(2,1)} %broadcast_in_dim.9), calls=%async_computation.1 | async-start | bytes 1048576 | tf_op jit(solution)/shard_map/all_to_all | solution.py:16
  74.1 2.2 %copy-start.2 = (bf16[8,1024,128]{2,1,0:T(8,128)(2,1)S(1)}, bf16[8,1024,128]{2,1,0:T(8,128)(2,1)}, u32[]{:S(2)}) copy-start(bf16[8,1024,128]{2,1,0:T(8,128)(2,1)} %slice.38) | copy-start | bytes 6291460
  92.0 1.9 %copy-start.3 = (f32[1,256,8,128]{3,2,1,0:T(8,128)S(1)}, f32[1,256,8,128]{3,2,1,0:T(8,128)}, u32[]{:S(2)}) copy-start(f32[1,256,8,128]{3,2,1,0:T(8,128)} %get-tuple-element.14) | copy-start | bytes 3145732
  92.0 1.9 %copy-start.5 = (bf16[1,256,8,128]{3,2,1,0:T(8,128)(2,1)S(1)}, bf16[1,256,8,128]{3,2,1,0:T(8,128)(2,1)}, u32[]{:S(2)}) copy-start(bf16[1,256,8,128]{3,2,1,0:T(8,128)(2,1)} %get-tuple-element.15) | copy-start | bytes 1572868
  92.0 2.2 %copy-start.6 = (bf16[1024,1024]{1,0:T(8,128)(2,1)S(1)}, bf16[1024,1024]{1,0:T(8,128)(2,1)}, u32[]{:S(2)}) copy-start(bf16[1024,1024]{1,0:T(8,128)(2,1)} %param.10) | copy-start | bytes 6291460
  94.2 2.1 %copy-start.4 = (bf16[256,128]{1,0:T(8,128)(2,1)S(1)}, bf16[256,128]{1,0:T(8,128)(2,1)}, u32[]{:S(2)}) copy-start(bf16[256,128]{1,0:T(8,128)(2,1)} %param.7) | copy-start | bytes 196612
  97.7 19.1 %all-to-all-start.2 = ((bf16[32,8,1024]{2,1,0:T(8,128)(2,1)}), bf16[32,8,1024]{2,1,0:T(8,128)(2,1)S(1)}, u32[]{:S(2)}, u32[]{:S(2)}) async-start(bf16[32,8,1024]{2,1,0:T(8,128)(2,1)} %fusion.12), calls=%async_computation.2 | async-start | bytes 1048576 | tf_op jit(solution)/shard_map/all_to_all | solution.py:22
  117.8 39.9 %all-to-all-start.3 = ((bf16[32,320,128]{2,1,0:T(8,128)(2,1)}), bf16[32,320,128]{2,1,0:T(8,128)(2,1)}, u32[]{:S(2)}, u32[]{:S(2)}) async-start(bf16[32,320,128]{2,1,0:T(8,128)(2,1)} %broadcast_dynamic-update-slice_fusion), calls=%async_computation.3 | async-start | bytes 5242880 | tf_op jit(solution)/shard_map/all_to_all | solution.py:130
Sparse Core Ops, SparseCore 0:
  11.7 48.8 all-gather.1

commit v15 on v14

--- a/solution.py
+++ b/solution.py
@@ -99,16 +99,16 @@
     )
     grad_scale = 1.0 / math.sqrt(nodes)
     both = jnp.concatenate([weight_part, root_part], axis=0) * grad_scale
-    both_sum = reduce_rows(both.astype(jnp.bfloat16), "row", row_count)
-    sum_rows, sum_cols = both_sum.shape
-    lane_tiles = sum_cols // block_edge
-    sum_lanes = both_sum.size // block_edge
-    sum_pair = (
-        both_sum.astype(jnp.bfloat16)
-        .reshape(sum_rows, lane_tiles, block_edge)
-        .transpose(1, 0, 2)
-        .reshape(sum_lanes, block_edge)
+    sum_rows = both.shape[0] // row_count
+    lane_tiles = both.shape[1] // block_edge
+    sum_lanes = sum_rows * lane_tiles
+    both_tiled = (
+        both.astype(jnp.bfloat16)
+        .reshape(row_count, sum_rows, lane_tiles, block_edge)
+        .transpose(0, 2, 1, 3)
+        .reshape(row_count * sum_lanes, block_edge)
     )
+    sum_pair = reduce_rows(both_tiled, "row", row_count).astype(jnp.bfloat16)
 
     w_rows = lax.dynamic_slice_in_dim(weight, col_index * feat_dev, feat_dev, 0)
     r_rows = lax.dynamic_slice_in_dim(root_weight, col_index * feat_dev, feat_dev, 0)

time: 170 us -> 170 us (level)
  no operation moved by 1% of the time
where the time goes in v15:
time: 170 us; the launch traced here: 169 us
  waiting for transfers between devices  73.7 us (43%)
  starting transfers between devices  26.2 us (15%)
  local copies, waits for them, and re-layouts  25.2 us (15%)
  matrix products  16.7 us (10%)
  between operations  14.9 us (9%)
  other arithmetic  12.7 us (7%)
    all_gather x1, waiting for transfers between devices, per_device(): lax.all_gather(packed, 'col', axis=0, tiled=True)  37.6 us
    all_to_all x1, waiting for transfers between devices, per_device(): incoming = lax.all_to_all(outgoing, 'row', 0, 0, tiled=True)  32.4 us
    all_to_all x2, starting transfers between devices, gather_rows(): got = lax.all_to_all(spread, axis_name, 0, 0, tiled=True)  12.8 us
    all_to_all x1, starting transfers between devices, reduce_rows(): got = lax.all_to_all(pieces, axis_name, 0, 0, tiled=True)  7.45 us
    reshape x1, local copies, waits for them, and re-layouts, per_device(): dense_t = jnp.transpose(dense, (0, 2, 4, 1, 3)).reshape(nodes, node_rows)  7.3 us
    all_to_all x1, starting transfers between devices, per_device(): incoming = lax.all_to_all(outgoing, 'row', 0, 0, tiled=True)  5.88 us
    dot_general x1, matrix products, per_device(): jnp.dot(dense_t, aggregated_grad, preferred_element_type=jnp.float32)  5.32 us
    broadcast_in_dim x2, local copies, waits for them, and re-layouts, gather_rows(): spread = jnp.broadcast_to(block[None], (parts,) + block.shape)  3.54 us
  transfers between devices with their start and end apart: 5, of which 4 were waited for; matrix products, arithmetic and copies ran while one was open for 20% of the time, Pallas kernels for 0%

profile of v15, /device:TPU:1, one launch (start us, length us, event | category | flops | bytes accessed | tf_op | source)
XLA Modules:
  0.0 169.4 jit_solution(3972209200056676001)
XLA Ops:
  7.2 0.8 convert_bitcast_fusion.2
  8.8 1.1 bitcast_multiply_fusion.1
  9.9 1.6 fusion.17
  11.6 2.7 %broadcast_in_dim.6 = bf16[32,256,128]{2,1,0:T(8,128)(2,1)} broadcast(bf16[256,128]{1,0:T(8,128)(2,1)} %param.7), dimensions={1,2} | broadcast | bytes 2162688 | tf_op jit(solution)/shard_map/broadcast_in_dim | solution.py:15
  14.3 8.6 %all-to-all-start = ((bf16[32,256,128]{2,1,0:T(8,128)(2,1)}), bf16[32,256,128]{2,1,0:T(8,128)(2,1)}, u32[]{:S(2)}, u32[]{:S(2)}) async-start(bf16[32,256,128]{2,1,0:T(8,128)(2,1)} %broadcast_in_dim.6), calls=%async_computation | async-start | bytes 4194304 | tf_op jit(solution)/shard_map/all_to_all | solution.py:16
  22.9 37.6 %all-gather.2.cloned.1.call-done = bf16[12416,128]{1,0:T(8,128)(2,1)} async-done(((bf16[1552,128]{1,0:T(8,128)(2,1)}), bf16[12416,128]{1,0:T(8,128)(2,1)}) %all-gather.2.cloned.1.call-update) | async-done | bytes 3178512 | tf_op jit(solution)/shard_map/all_gather | solution.py:41
  60.6 3.1 %slice.38 = bf16[8,1024,128]{2,1,0:T(8,128)(2,1)} slice(bf16[8,1552,128]{2,1,0:T(8,128)(2,1)} %bitcast.89), slice={[0:8], [0:1024], [0:128]} | slice | bytes 4194304 | tf_op jit(solution)/shard_map/slice | solution.py:44
  63.7 0.7 slice_convert_fusion.1
  64.5 3.1 %fusion.5 = bf16[8,8,128,128]{3,1,2,0:T(8,128)(2,1)S(1)} fusion(bf16[8,8,128,128]{3,2,1,0:T(8,128)(2,1)} %bitcast.9, s32[8,8]{1,0:T(8,128)S(1)} %get-tuple-element.16), kind=kOutput, calls=%fused_computation.10 | convolution fusion | flops 17826304 | bytes 4194560 | tf_op jit(solution)/shard_map/tsc,tcjf->tsjf/dot_general | solution.py:66
  69.1 0.8 broadcast_in_dim.7
  70.0 4.1 %all-to-all-start.1 = ((bf16[8,256,128]{1,2,0:T(8,128)(2,1)}), bf16[8,256,128]{1,2,0:T(8,128)(2,1)}, u32[]{:S(2)}, u32[]{:S(2)}) async-start(bf16[8,256,128]{1,2,0:T(8,128)(2,1)} %broadcast_in_dim.7), calls=%async_computation.1 | async-start | bytes 1048576 | tf_op jit(solution)/shard_map/all_to_all | solution.py:16
  74.1 1.4 slice.40
  76.3 1.9 %convert_bitcast_fusion = bf16[8,2,8,128,128]{4,2,1,3,0:T(8,128)(2,1)S(1)} fusion(bf16[8,8,128,128]{3,2,1,0:T(8,128)(2,1)S(1)} %bitcast.84, s32[8,8]{1,0:T(8,128)S(1)} %bitcast.97), kind=kOutput, calls=%fused_computation.4 | convolution fusion | flops 35652608 | bytes 6291712 | tf_op jit(solution)/shard_map/tsp,tsij->tpij/dot_general | solution.py:53
  78.2 3.2 %copy.48 = bf16[8,2,8,128,128]{4,2,0,3,1:T(8,128)(2,1)} copy(bf16[8,2,8,128,128]{4,2,1,3,0:T(8,128)(2,1)S(1)} %convert_bitcast_fusion) | data formatting | bytes 8388608 | tf_op jit(solution)/shard_map/reshape | solution.py:56
  81.4 7.3 %reshape.126 = bf16[8192,256]{0,1:T(8,128)(2,1)} reshape(bf16[8,8,128,2,128]{2,1,0,4,3:T(8,128)(2,1)} %bitcast.85) | data formatting | bytes 8388608 | tf_op jit(solution)/shard_map/reshape | solution.py:77
  88.7 1.2 slice_convert_fusion
  89.9 2.1 %all-to-all-done.1 = bf16[8,256,128]{1,2,0:T(8,128)(2,1)} async-done(((bf16[8,256,128]{1,2,0:T(8,128)(2,1)}), bf16[8,256,128]{1,2,0:T(8,128)(2,1)}, u32[]{:S(2)}, u32[]{:S(2)}) %all-to-all-start.1) | async-done | bytes 524320 | tf_op jit(solution)/shard_map/all_to_all | solution.py:16
  92.0 1.9 %fusion.34 = f32[256,1024]{1,0:T(8,128)S(1)} fusion(bf16[256,1024]{0,1:T(8,128)(2,1)} %bitcast.16, bf16[1024,1024]{1,0:T(8,128)(2,1)S(1)} %copy-done), kind=kOutput, calls=%fused_computation.62 | convolution fusion | flops 536870912 | bytes 3670016 | tf_op jit(solution)/shard_map/dot_general | solution.py:86
  94.2 2.1 %fusion.8 = (bf16[256,1024]{1,0:T(8,128)(2,1)S(1)}, f32[256,1024]{1,0:T(8,128)}) fusion(f32[32,8,8,128]{3,2,1,0:T(8,128)S(1)} %bitcast.92, f32[256,1024]{1,0:T(8,128)S(1)} %fusion.34, bf16[1024,1024]{1,0:T(8,128)(2,1)S(1)} %copy-done.6, bf16[32,8,8,128]{3,2,1,0:T(8,128)(2,1)S(1)} %bitcast.95), kind=kOutput, calls=%fused_computation.17 | convolution fusion | flops 539492352 | bytes 6291456 | tf_op jit(solution)/shard_map/dot_general | solution.py:86
  96.8 0.9 fusion.12
  97.8 7.5 %all-to-all-start.2 = ((bf16[32,64,128]{2,1,0:T(8,128)(2,1)}), bf16[32,64,128]{2,1,0:T(8,128)(2,1)S(1)}, u32[]{:S(2)}, u32[]{:S(2)}) async-start(bf16[32,64,128]{2,1,0:T(8,128)(2,1)} %fusion.12), calls=%async_computation.2 | async-start | bytes 1048576 | tf_op jit(solution)/shard_map/all_to_all | solution.py:22
  105.2 5.3 %convolution_convert_fusion = bf16[8192,128]{1,0:T(8,128)(2,1)} fusion(bf16[8192,256]{0,1:T(8,128)(2,1)} %reshape.126, bf16[256,1024]{1,0:T(8,128)(2,1)S(1)} %get-tuple-element.18, bf16[1024,1024]{1,0:T(8,128)(2,1)S(1)} %copy-done, s32[]{:T(128)S(6)} %select_n.27), kind=kOutput, calls=%fused_computation | convolution fusion | flops 605061120 | bytes 7077892 | tf_op jit(solution)/shard_map/dot_general | solution.py:122
  110.5 3.5 %concatenate.10 = bf16[32,320,128]{2,1,0:T(8,128)(2,1)} pad(bf16[32,256,128]{2,1,0:T(8,128)(2,1)} %bitcast.86, bf16[]{:T(256)} %constant.37.clone.1), padding=0_0x0_64x0_0 | pad | bytes 4718594 | tf_op jit(solution)/shard_map/concatenate | solution.py:125
  114.0 1.2 fusion.18
  115.3 1.6 all-to-all-done.2
  116.9 0.9 broadcast_dynamic-update-slice_fusion
  117.9 5.9 %all-to-all-start.3 = ((bf16[32,320,128]{2,1,0:T(8,128)(2,1)}), bf16[32,320,128]{2,1,0:T(8,128)(2,1)}, u32[]{:S(2)}, u32[]{:S(2)}) async-start(bf16[32,320,128]{2,1,0:T(8,128)(2,1)} %broadcast_dynamic-update-slice_fusion), calls=%async_computation.3 | async-start | bytes 5242880 | tf_op jit(solution)/shard_map/all_to_all | solution.py:130
  123.7 1.6 multiply_convert_fusion
  125.3 32.4 %all-to-all-done.3 = bf16[32,320,128]{2,1,0:T(8,128)(2,1)} async-done(((bf16[32,320,128]{2,1,0:T(8,128)(2,1)}), bf16[32,320,128]{2,1,0:T(8,128)(2,1)}, u32[]{:S(2)}, u32[]{:S(2)}) %all-to-all-start.3) | async-done | bytes 2621472 | tf_op jit(solution)/shard_map/all_to_all | solution.py:130
  157.7 1.1 convert_bitcast_fusion.1
  158.9 1.1 slice_bitcast_fusion
  160.0 1.9 %convert_reduce_fusion = f32[256,128]{1,0:T(8,128)S(1)} fusion(bf16[32,320,128]{2,1,0:T(8,128)(2,1)} %all-to-all-done.3), kind=kLoop, calls=%fused_computation.3 | loop fusion | flops 2064384 | bytes 2228224 | tf_op jit(solution)/shard_map/reduce_sum | solution.py:131
  (29 shorter events, 4.0 us)
Async XLA Ops:
  7.2 84.8 %copy-start = (bf16[1024,1024]{1,0:T(8,128)(2,1)S(1)}, bf16[1024,1024]{1,0:T(8,128)(2,1)}, u32[]{:S(2)}) copy-start(bf16[1024,1024]{1,0:T(8,128)(2,1)} %param.9) | copy-start | bytes 6291460
  7.2 53.4 %all-gather.2.cloned.1.call-start = ((), (), s32[]{:S(2)}) async-start(), calls=%async_computation.4 | async-start | bytes 3575808 | tf_op jit(solution)/shard_map/all_gather | solution.py:41
  14.3 50.2 %all-to-all-start = ((bf16[32,256,128]{2,1,0:T(8,128)(2,1)}), bf16[32,256,128]{2,1,0:T(8,128)(2,1)}, u32[]{:S(2)}, u32[]{:S(2)}) async-start(bf16[32,256,128]{2,1,0:T(8,128)(2,1)} %broadcast_in_dim.6), calls=%async_computation | async-start | bytes 4194304 | tf_op jit(solution)/shard_map/all_to_all | solution.py:16
  64.5 3.1 %copy-start.1 = (bf16[8,1024,128]{2,1,0:T(8,128)(2,1)S(1)}, bf16[8,1024,128]{2,1,0:T(8,128)(2,1)}, u32[]{:S(2)}) copy-start(bf16[8,1024,128]{2,1,0:T(8,128)(2,1)} %slice.38) | copy-start | bytes 6291460
  70.0 22.0 %all-to-all-start.1 = ((bf16[8,256,128]{1,2,0:T(8,128)(2,1)}), bf16[8,256,128]{1,2,0:T(8,128)(2,1)}, u32[]{:S(2)}, u32[]{:S(2)}) async-start(bf16[8,256,128]{1,2,0:T(8,128)(2,1)} %broadcast_in_dim.7), calls=%async_computation.1 | async-start | bytes 1048576 | tf_op jit(solution)/shard_map/all_to_all | solution.py:16
  74.1 2.2 %copy-start.2 = (bf16[8,1024,128]{2,1,0:T(8,128)(2,1)S(1)}, bf16[8,1024,128]{2,1,0:T(8,128)(2,1)}, u32[]{:S(2)}) copy-start(bf16[8,1024,128]{2,1,0:T(8,128)(2,1)} %slice.38) | copy-start | bytes 6291460
  92.0 1.9 %copy-start.3 = (f32[1,256,8,128]{3,2,1,0:T(8,128)S(1)}, f32[1,256,8,128]{3,2,1,0:T(8,128)}, u32[]{:S(2)}) copy-start(f32[1,256,8,128]{3,2,1,0:T(8,128)} %get-tuple-element.14) | copy-start | bytes 3145732
  92.0 1.9 %copy-start.5 = (bf16[1,256,8,128]{3,2,1,0:T(8,128)(2,1)S(1)}, bf16[1,256,8,128]{3,2,1,0:T(8,128)(2,1)}, u32[]{:S(2)}) copy-start(bf16[1,256,8,128]{3,2,1,0:T(8,128)(2,1)} %get-tuple-element.15) | copy-start | bytes 1572868
  92.0 2.2 %copy-start.6 = (bf16[1024,1024]{1,0:T(8,128)(2,1)S(1)}, bf16[1024,1024]{1,0:T(8,128)(2,1)}, u32[]{:S(2)}) copy-start(bf16[1024,1024]{1,0:T(8,128)(2,1)} %param.10) | copy-start | bytes 6291460
  94.2 2.1 %copy-start.4 = (bf16[256,128]{1,0:T(8,128)(2,1)S(1)}, bf16[256,128]{1,0:T(8,128)(2,1)}, u32[]{:S(2)}) copy-start(bf16[256,128]{1,0:T(8,128)(2,1)} %param.7) | copy-start | bytes 196612
  97.8 19.1 %all-to-all-start.2 = ((bf16[32,64,128]{2,1,0:T(8,128)(2,1)}), bf16[32,64,128]{2,1,0:T(8,128)(2,1)S(1)}, u32[]{:S(2)}, u32[]{:S(2)}) async-start(bf16[32,64,128]{2,1,0:T(8,128)(2,1)} %fusion.12), calls=%async_computation.2 | async-start | bytes 1048576 | tf_op jit(solution)/shard_map/all_to_all | solution.py:22
  117.9 39.9 %all-to-all-start.3 = ((bf16[32,320,128]{2,1,0:T(8,128)(2,1)}), bf16[32,320,128]{2,1,0:T(8,128)(2,1)}, u32[]{:S(2)}, u32[]{:S(2)}) async-start(bf16[32,320,128]{2,1,0:T(8,128)(2,1)} %broadcast_dynamic-update-slice_fusion), calls=%async_computation.3 | async-start | bytes 5242880 | tf_op jit(solution)/shard_map/all_to_all | solution.py:130
Sparse Core Ops, SparseCore 0:
  11.7 48.8 all-gather.1

commit v16 on v15

--- a/solution.py
+++ b/solution.py
@@ -33,7 +33,7 @@
 
     live = (jnp.arange(slots, dtype=jnp.int32) < counts[0, 0]).astype(values.dtype)
     own_vals = (values[0, 0] * live[:, None, None]).reshape(slots * block_edge, block_edge)
-    pos_row = jnp.zeros((16, block_edge), values.dtype)
+    pos_row = jnp.zeros((block_edge, block_edge), values.dtype)
     pos_row = lax.dynamic_update_slice(
         pos_row, positions[0, 0].astype(values.dtype).reshape(1, slots), (0, 0)
     )
@@ -41,9 +41,7 @@
     all_packed = lax.all_gather(packed, "col", axis=0, tiled=True).reshape(
         col_count, packed.shape[0], block_edge
     )
-    tile_vals = all_packed[:, : slots * block_edge].reshape(
-        col_count, slots, block_edge, block_edge
-    )
+    tile_vals = all_packed.reshape(col_count, -1, block_edge, block_edge)[:, :slots]
     tile_pos = all_packed[:, slots * block_edge, :slots].astype(jnp.int32)
     cb = row_count * node_rows // col_count // block_edge
     n_pos = row_blocks * cb
@@ -77,7 +75,7 @@
     dense_t = jnp.transpose(dense, (0, 2, 4, 1, 3)).reshape(nodes, node_rows)
     agg_parts, dense_t = lax.optimization_barrier((agg_parts, dense_t))
     agg_full = jnp.moveaxis(agg_parts, 0, 1).reshape(node_rows, col_count * feat_dev)
-    pair_parts = all_packed[:, slots * block_edge + 16 :].reshape(
+    pair_parts = all_packed[:, (slots + 1) * block_edge :].reshape(
         col_count, 2, node_rows, feat_dev
     )
     pair_full = jnp.moveaxis(pair_parts, 0, 2).reshape(2, node_rows, col_count * feat_dev)

time: 170 us -> 170 us (level)
    all_gather x1, waiting for transfers between devices: 37.6 us -> 39.9 us  [per_device(): lax.all_gather(packed, 'col', axis=0, tiled=True)]
  transfers between devices with their start and end apart: 5 -> 5, of which waited for: 4 -> 4; matrix products, arithmetic and copies ran while one was open for 20% -> 19% of each run, Pallas kernels for 0% -> 0%
where the time goes in v16:
time: 170 us; the launch traced here: 169 us
  waiting for transfers between devices  74.3 us (44%)
  starting transfers between devices  26.1 us (15%)
  local copies, waits for them, and re-layouts  23.7 us (14%)
  matrix products  16.7 us (10%)
  between operations  14.9 us (9%)
  other arithmetic  12.7 us (7%)
    all_gather x1, waiting for transfers between devices, per_device(): lax.all_gather(packed, 'col', axis=0, tiled=True)  39.9 us
    all_to_all x1, waiting for transfers between devices, per_device(): incoming = lax.all_to_all(outgoing, 'row', 0, 0, tiled=True)  32.4 us
    all_to_all x2, starting transfers between devices, gather_rows(): got = lax.all_to_all(spread, axis_name, 0, 0, tiled=True)  12.8 us
    all_to_all x1, starting transfers between devices, reduce_rows(): got = lax.all_to_all(pieces, axis_name, 0, 0, tiled=True)  7.37 us
    reshape x1, local copies, waits for them, and re-layouts, per_device(): dense_t = jnp.transpose(dense, (0, 2, 4, 1, 3)).reshape(nodes, node_rows)  7.29 us
    all_to_all x1, starting transfers between devices, per_device(): incoming = lax.all_to_all(outgoing, 'row', 0, 0, tiled=True)  5.89 us
    dot_general x1, matrix products, per_device(): jnp.dot(dense_t, aggregated_grad, preferred_element_type=jnp.float32)  5.33 us
    broadcast_in_dim x2, local copies, waits for them, and re-layouts, gather_rows(): spread = jnp.broadcast_to(block[None], (parts,) + block.shape)  3.48 us
  transfers between devices with their start and end apart: 5, of which 4 were waited for; matrix products, arithmetic and copies ran while one was open for 19% of the time, Pallas kernels for 0%

profile of v16, /device:TPU:1, one launch (start us, length us, event | category | flops | bytes accessed | tf_op | source)
XLA Modules:
  0.0 168.5 jit_solution(12683011915921730170)
XLA Ops:
  7.2 0.8 convert_bitcast_fusion.2
  8.8 1.1 bitcast_multiply_fusion.1
  9.9 1.7 fusion.17
  11.6 2.6 %broadcast_in_dim.6 = bf16[32,256,128]{2,1,0:T(8,128)(2,1)} broadcast(bf16[256,128]{1,0:T(8,128)(2,1)} %param.7), dimensions={1,2} | broadcast | bytes 2162688 | tf_op jit(solution)/shard_map/broadcast_in_dim | solution.py:15
  14.2 8.6 %all-to-all-start = ((bf16[32,256,128]{2,1,0:T(8,128)(2,1)}), bf16[32,256,128]{2,1,0:T(8,128)(2,1)}, u32[]{:S(2)}, u32[]{:S(2)}) async-start(bf16[32,256,128]{2,1,0:T(8,128)(2,1)} %broadcast_in_dim.6), calls=%async_computation | async-start | bytes 4194304 | tf_op jit(solution)/shard_map/all_to_all | solution.py:16
  22.9 39.9 %all-gather.2.cloned.1.call-done = bf16[13312,128]{1,0:T(8,128)(2,1)} async-done(((bf16[1664,128]{1,0:T(8,128)(2,1)}), bf16[13312,128]{1,0:T(8,128)(2,1)}) %all-gather.2.cloned.1.call-update) | async-done | bytes 3407888 | tf_op jit(solution)/shard_map/all_gather | solution.py:41
  62.8 0.7 slice_convert_fusion.1
  63.6 3.1 %fusion.5 = bf16[8,8,128,128]{3,1,2,0:T(8,128)(2,1)S(1)} fusion(bf16[8,8,128,128]{3,2,1,0:T(8,128)(2,1)} %bitcast.9, s32[8,8]{1,0:T(8,128)S(1)} %get-tuple-element.16), kind=kOutput, calls=%fused_computation.10 | convolution fusion | flops 17826304 | bytes 4194560 | tf_op jit(solution)/shard_map/tsc,tcjf->tsjf/dot_general | solution.py:64
  67.4 0.7 multiply_reduce_fusion
  68.2 0.8 broadcast_in_dim.7
  69.1 4.2 %all-to-all-start.1 = ((bf16[8,256,128]{1,2,0:T(8,128)(2,1)}), bf16[8,256,128]{1,2,0:T(8,128)(2,1)}, u32[]{:S(2)}, u32[]{:S(2)}) async-start(bf16[8,256,128]{1,2,0:T(8,128)(2,1)} %broadcast_in_dim.7), calls=%async_computation.1 | async-start | bytes 1048576 | tf_op jit(solution)/shard_map/all_to_all | solution.py:16
  73.2 1.3 slice.40
  74.6 1.8 %slice.39 = bf16[8,8,128,128]{3,2,1,0:T(8,128)(2,1)S(1)} slice(bf16[8,13,128,128]{3,2,1,0:T(8,128)(2,1)} %bitcast.89), slice={[0:8], [0:8], [0:128], [0:128]} | slice | bytes 4194304 | tf_op jit(solution)/shard_map/slice | solution.py:44
  77.1 1.9 %convert_bitcast_fusion = bf16[8,2,8,128,128]{4,2,1,3,0:T(8,128)(2,1)S(1)} fusion(bf16[8,8,128,128]{3,2,1,0:T(8,128)(2,1)S(1)} %slice.39, s32[8,8]{1,0:T(8,128)S(1)} %bitcast.96), kind=kOutput, calls=%fused_computation.4 | convolution fusion | flops 35652608 | bytes 6291712 | tf_op jit(solution)/shard_map/tsp,tsij->tpij/dot_general | solution.py:51
  79.0 3.2 %copy.47 = bf16[8,2,8,128,128]{4,2,0,3,1:T(8,128)(2,1)} copy(bf16[8,2,8,128,128]{4,2,1,3,0:T(8,128)(2,1)S(1)} %convert_bitcast_fusion) | data formatting | bytes 8388608 | tf_op jit(solution)/shard_map/reshape | solution.py:54
  82.1 7.3 %reshape.122 = bf16[8192,256]{0,1:T(8,128)(2,1)} reshape(bf16[8,8,128,2,128]{2,1,0,4,3:T(8,128)(2,1)} %bitcast.83) | data formatting | bytes 8388608 | tf_op jit(solution)/shard_map/reshape | solution.py:75
  89.4 1.2 slice_convert_fusion
  91.2 1.9 %fusion.34 = f32[256,1024]{1,0:T(8,128)S(1)} fusion(bf16[256,1024]{0,1:T(8,128)(2,1)} %bitcast.16, bf16[1024,1024]{1,0:T(8,128)(2,1)S(1)} %copy-done), kind=kOutput, calls=%fused_computation.62 | convolution fusion | flops 536870912 | bytes 3670016 | tf_op jit(solution)/shard_map/dot_general | solution.py:84
  93.4 2.1 %fusion.8 = (bf16[256,1024]{1,0:T(8,128)(2,1)S(1)}, f32[256,1024]{1,0:T(8,128)}) fusion(f32[32,8,8,128]{3,2,1,0:T(8,128)S(1)} %bitcast.91, f32[256,1024]{1,0:T(8,128)S(1)} %fusion.34, bf16[1024,1024]{1,0:T(8,128)(2,1)S(1)} %copy-done.5, bf16[32,8,8,128]{3,2,1,0:T(8,128)(2,1)S(1)} %bitcast.94), kind=kOutput, calls=%fused_computation.17 | convolution fusion | flops 539492352 | bytes 6291456 | tf_op jit(solution)/shard_map/dot_general | solution.py:84
  96.0 0.9 fusion.12
  97.0 7.4 %all-to-all-start.2 = ((bf16[32,64,128]{2,1,0:T(8,128)(2,1)}), bf16[32,64,128]{2,1,0:T(8,128)(2,1)S(1)}, u32[]{:S(2)}, u32[]{:S(2)}) async-start(bf16[32,64,128]{2,1,0:T(8,128)(2,1)} %fusion.12), calls=%async_computation.2 | async-start | bytes 1048576 | tf_op jit(solution)/shard_map/all_to_all | solution.py:22
  104.3 5.3 %convolution_convert_fusion = bf16[8192,128]{1,0:T(8,128)(2,1)} fusion(bf16[8192,256]{0,1:T(8,128)(2,1)} %reshape.122, bf16[256,1024]{1,0:T(8,128)(2,1)S(1)} %get-tuple-element.18, bf16[1024,1024]{1,0:T(8,128)(2,1)S(1)} %copy-done, s32[]{:T(128)S(6)} %select_n.27), kind=kOutput, calls=%fused_computation | convolution fusion | flops 605061120 | bytes 7077892 | tf_op jit(solution)/shard_map/dot_general | solution.py:120
  109.7 3.5 %concatenate.10 = bf16[32,320,128]{2,1,0:T(8,128)(2,1)} pad(bf16[32,256,128]{2,1,0:T(8,128)(2,1)} %bitcast.84, bf16[]{:T(256)} %constant.37.clone.1), padding=0_0x0_64x0_0 | pad | bytes 4718594 | tf_op jit(solution)/shard_map/concatenate | solution.py:123
  113.1 1.2 fusion.18
  114.4 1.6 all-to-all-done.2
  116.0 1.0 broadcast_dynamic-update-slice_fusion
  117.0 5.9 %all-to-all-start.3 = ((bf16[32,320,128]{2,1,0:T(8,128)(2,1)}), bf16[32,320,128]{2,1,0:T(8,128)(2,1)}, u32[]{:S(2)}, u32[]{:S(2)}) async-start(bf16[32,320,128]{2,1,0:T(8,128)(2,1)} %broadcast_dynamic-update-slice_fusion), calls=%async_computation.3 | async-start | bytes 5242880 | tf_op jit(solution)/shard_map/all_to_all | solution.py:128
  122.9 1.6 multiply_convert_fusion
  124.5 32.4 %all-to-all-done.3 = bf16[32,320,128]{2,1,0:T(8,128)(2,1)} async-done(((bf16[32,320,128]{2,1,0:T(8,128)(2,1)}), bf16[32,320,128]{2,1,0:T(8,128)(2,1)}, u32[]{:S(2)}, u32[]{:S(2)}) %all-to-all-start.3) | async-done | bytes 2621472 | tf_op jit(solution)/shard_map/all_to_all | solution.py:128
  156.9 1.1 convert_bitcast_fusion.1
  158.0 1.1 slice_bitcast_fusion
  159.1 1.9 %convert_reduce_fusion = f32[256,128]{1,0:T(8,128)S(1)} fusion(bf16[32,320,128]{2,1,0:T(8,128)(2,1)} %all-to-all-done.3), kind=kLoop, calls=%fused_computation.3 | loop fusion | flops 2064384 | bytes 2228224 | tf_op jit(solution)/shard_map/reduce_sum | solution.py:129
  (27 shorter events, 3.8 us)
Async XLA Ops:
  7.2 84.0 %copy-start = (bf16[1024,1024]{1,0:T(8,128)(2,1)S(1)}, bf16[1024,1024]{1,0:T(8,128)(2,1)}, u32[]{:S(2)}) copy-start(bf16[1024,1024]{1,0:T(8,128)(2,1)} %param.9) | copy-start | bytes 6291460
  7.2 55.6 %all-gather.2.cloned.1.call-start = ((), (), s32[]{:S(2)}) async-start(), calls=%async_computation.4 | async-start | bytes 3833856 | tf_op jit(solution)/shard_map/all_gather | solution.py:41
  14.2 49.3 %all-to-all-start = ((bf16[32,256,128]{2,1,0:T(8,128)(2,1)}), bf16[32,256,128]{2,1,0:T(8,128)(2,1)}, u32[]{:S(2)}, u32[]{:S(2)}) async-start(bf16[32,256,128]{2,1,0:T(8,128)(2,1)} %broadcast_in_dim.6), calls=%async_computation | async-start | bytes 4194304 | tf_op jit(solution)/shard_map/all_to_all | solution.py:16
  63.6 3.1 %copy-start.1 = (bf16[13312,128]{1,0:T(8,128)(2,1)S(1)}, bf16[13312,128]{1,0:T(8,128)(2,1)}, u32[]{:S(2)}) copy-start(bf16[13312,128]{1,0:T(8,128)(2,1)} %all-gather.2.cloned.1.call-done) | copy-start | bytes 10223620
  69.1 22.1 %all-to-all-start.1 = ((bf16[8,256,128]{1,2,0:T(8,128)(2,1)}), bf16[8,256,128]{1,2,0:T(8,128)(2,1)}, u32[]{:S(2)}, u32[]{:S(2)}) async-start(bf16[8,256,128]{1,2,0:T(8,128)(2,1)} %broadcast_in_dim.7), calls=%async_computation.1 | async-start | bytes 1048576 | tf_op jit(solution)/shard_map/all_to_all | solution.py:16
  91.2 1.9 %copy-start.2 = (f32[1,256,8,128]{3,2,1,0:T(8,128)S(1)}, f32[1,256,8,128]{3,2,1,0:T(8,128)}, u32[]{:S(2)}) copy-start(f32[1,256,8,128]{3,2,1,0:T(8,128)} %get-tuple-element.14) | copy-start | bytes 3145732
  91.2 1.9 %copy-start.4 = (bf16[1,256,8,128]{3,2,1,0:T(8,128)(2,1)S(1)}, bf16[1,256,8,128]{3,2,1,0:T(8,128)(2,1)}, u32[]{:S(2)}) copy-start(bf16[1,256,8,128]{3,2,1,0:T(8,128)(2,1)} %get-tuple-element.15) | copy-start | bytes 1572868
  91.2 2.2 %copy-start.5 = (bf16[1024,1024]{1,0:T(8,128)(2,1)S(1)}, bf16[1024,1024]{1,0:T(8,128)(2,1)}, u32[]{:S(2)}) copy-start(bf16[1024,1024]{1,0:T(8,128)(2,1)} %param.10) | copy-start | bytes 6291460
  93.4 2.1 %copy-start.3 = (bf16[256,128]{1,0:T(8,128)(2,1)S(1)}, bf16[256,128]{1,0:T(8,128)(2,1)}, u32[]{:S(2)}) copy-start(bf16[256,128]{1,0:T(8,128)(2,1)} %param.7) | copy-start | bytes 196612
  97.0 19.0 %all-to-all-start.2 = ((bf16[32,64,128]{2,1,0:T(8,128)(2,1)}), bf16[32,64,128]{2,1,0:T(8,128)(2,1)S(1)}, u32[]{:S(2)}, u32[]{:S(2)}) async-start(bf16[32,64,128]{2,1,0:T(8,128)(2,1)} %fusion.12), calls=%async_computation.2 | async-start | bytes 1048576 | tf_op jit(solution)/shard_map/all_to_all | solution.py:22
  117.0 39.9 %all-to-all-start.3 = ((bf16[32,320,128]{2,1,0:T(8,128)(2,1)}), bf16[32,320,128]{2,1,0:T(8,128)(2,1)}, u32[]{:S(2)}, u32[]{:S(2)}) async-start(bf16[32,320,128]{2,1,0:T(8,128)(2,1)} %broadcast_dynamic-update-slice_fusion), calls=%async_computation.3 | async-start | bytes 5242880 | tf_op jit(solution)/shard_map/all_to_all | solution.py:128
Sparse Core Ops, SparseCore 0:
  11.7 50.9 all-gather.1
